TPU v7x, 128 devices: a whole 4x4x4 slice. The times are simulated.
128 devices in a mesh: tok: 32 (over x, y, core), tp: 4 (over z).
Axes of the slice: x: 4, y: 4, z: 4, core: 2. Of those that a mesh axis runs over, the one named last changes fastest.
Arguments:
- context: bfloat16 [16384, 1536], P('tok', 'tp'), may hold values from -6 to 6
- attn_weight: bfloat16 [1536, 1536], P('tp'), may hold values from -0.15625 to 0.15625
- residual: bfloat16 [16384, 1536], P(('tok', 'tp')), may hold values from -6 to 6
- gain_first: float32 [1536], replicated, may hold values from 0.5 to 1.5
- router: bfloat16 [1536, 40], replicated, may hold values from -46 to 46
- routes: int32 [16384, 8], P(('tok', 'tp')), may hold values from 0 to 39, as said below
- lengths: int32 [32], replicated, may hold values from 1 to 512, 14336 in all
- slot_expert: int32 [64], replicated, may hold values from 0 to 39, as said below
- w_in: bfloat16 [64, 1536, 1024], P('tok'), may hold values from -1 to 1
- w_out: bfloat16 [64, 512, 1536], P('tok'), may hold values from -1 to 1
- gain_next: float32 [1536], replicated, may hold values from 0.5 to 1.5
Outputs:
- stream_out: bfloat16 [16384, 1536], P(('tok', 'tp'))
- next_normed: bfloat16 [16384, 1536], P(('tok', 'tp'))
Inputs may be any that keep to these rules, and one draw needn't show every extreme that they name: `routes`: each row names 8 different experts. In the rows of one device no expert is named by more than 30 rows, and some expert is named by exactly 30 rows. `slot_expert`: every expert is held by at least one slot; slot s lies on token shard s // 2. `lengths`: some token shard is full.
All inputs are finite; a program needn't handle non-finite values.
Results may differ from a plain program's by a relative error of at most 0.015.
Values may be sent and summed in bfloat16 or wider, within the bound.
No kernel may reach another device: no remote copies, remote signals or barrier semaphores. Data moves between devices by JAX's collectives and lax.ppermute only.
A program may use at most 128 MiB of HBM per device.

v0:
```python
import jax
import jax.numpy as jnp
from jax import lax
from jax.sharding import PartitionSpec as P

E = 40
TOPK = 8
MOST = 30


def rms_norm(source, gain_vec):
    values = source.astype(jnp.float32)
    inverse_rms = lax.rsqrt(jnp.mean(values * values, axis=-1, keepdims=True) + 1e-06)
    return (values * inverse_rms * gain_vec).astype(jnp.bfloat16)


def serve_slots(slot_expert, tok_position):
    slot_total = slot_expert.shape[0]
    present = (slot_expert[None, :] == jnp.arange(E, dtype=jnp.int32)[:, None]).astype(jnp.int32)
    replica_count = jnp.sum(present, axis=1)
    replica_rank = jnp.cumsum(present, axis=1) - 1
    wanted = tok_position % replica_count
    chosen_slot = (present == 1) & (replica_rank == wanted[:, None])
    slot_ids = jnp.arange(slot_total, dtype=jnp.int32)[None, :]
    return jnp.sum(jnp.where(chosen_slot, slot_ids, 0), axis=1)


def shards(
    context,
    attn_weight,
    residual,
    gain_first,
    router,
    routes,
    lengths,
    slot_expert,
    w_in,
    w_out,
    gain_next,
):
    row_count = residual.shape[0]
    width = residual.shape[1]
    hidden_units = w_out.shape[1]
    tok_rank = lax.axis_index("tok")
    tp_rank = lax.axis_index("tp")
    tok_total = lax.axis_size("tok")
    attn_out = lax.psum_scatter(
        jnp.dot(context, attn_weight, preferred_element_type=jnp.float32).astype(jnp.bfloat16),
        "tp",
        scatter_dimension=0,
        tiled=True,
    ).astype(jnp.float32)
    stream = (residual.astype(jnp.float32) + attn_out).astype(jnp.bfloat16)
    normed = rms_norm(stream, gain_first)
    logits = jnp.dot(normed, router, preferred_element_type=jnp.float32)
    chooser = routes[:, :, None] == jnp.arange(E, dtype=jnp.int32)[None, None, :]
    scores = jnp.sum(jnp.where(chooser, logits[:, None, :], jnp.float32(0.0)), axis=-1)
    gate_probs = jax.nn.softmax(scores, axis=-1)
    length_cap = jnp.sum(
        jnp.where(jnp.arange(lengths.shape[0], dtype=jnp.int32) == tok_rank, lengths, 0)
    )
    live_rows = tp_rank * row_count + jnp.arange(row_count, dtype=jnp.int32) < length_cap
    serving = serve_slots(slot_expert, tok_rank)
    slot_of = jnp.sum(jnp.where(chooser, serving[None, None, :], 0), axis=-1)
    flat_choose = (
        (chooser & live_rows[:, None, None]).reshape(row_count * TOPK, E).astype(jnp.int32)
    )
    running_rank = jnp.cumsum(flat_choose, axis=0) - 1
    position = jnp.sum(running_rank * flat_choose, axis=1)
    bucket_depth = MOST
    slot_total = slot_expert.shape[0]
    capacity = slot_total * bucket_depth
    live_flat = jnp.repeat(live_rows, TOPK)
    target = jnp.where(live_flat, slot_of.reshape(-1) * bucket_depth + position, capacity)
    repeated = jnp.repeat(normed, TOPK, axis=0)
    outgoing = jnp.zeros((capacity, width), jnp.bfloat16).at[target].set(repeated, mode="drop")
    outgoing = outgoing.reshape(tok_total, w_in.shape[0], bucket_depth, width)
    arrived = lax.all_to_all(outgoing, "tok", split_axis=0, concat_axis=0, tiled=True)
    hidden = jnp.einsum("nsmd,sdf->nsmf", arrived, w_in, preferred_element_type=jnp.float32)
    activated = (jax.nn.silu(hidden[..., :hidden_units]) * hidden[..., hidden_units:]).astype(
        jnp.bfloat16
    )
    computed = jnp.einsum(
        "nsmf,sfd->nsmd", activated, w_out, preferred_element_type=jnp.float32
    ).astype(jnp.bfloat16)
    returned = lax.all_to_all(computed, "tok", split_axis=0, concat_axis=0, tiled=True)
    fetched = returned.reshape(capacity, width)[jnp.minimum(target, capacity - 1)]
    weight_flat = jnp.where(live_rows[:, None], gate_probs, jnp.float32(0.0)).reshape(-1)
    expert_sum = jnp.sum(
        (fetched.astype(jnp.float32) * weight_flat[:, None]).reshape(row_count, TOPK, width), axis=1
    )
    stream_out = (stream.astype(jnp.float32) + expert_sum).astype(jnp.bfloat16)
    next_normed = rms_norm(stream_out, gain_next)
    return (stream_out, next_normed)


def solution(mesh):
    return jax.shard_map(
        shards,
        mesh=mesh,
        in_specs=(
            P("tok", "tp"),
            P("tp", None),
            P(("tok", "tp"), None),
            P(),
            P(),
            P(("tok", "tp"), None),
            P(),
            P(),
            P("tok", None, None),
            P("tok", None, None),
            P(),
        ),
        out_specs=(P(("tok", "tp"), None), P(("tok", "tp"), None)),
        check_vma=False,
    )
```

profile of v0, /device:TPU:8, one launch (start us, length us, event | category | flops | bytes accessed | tf_op | source)
XLA Modules:
  0.0 316.4 jit_solution(8848198256989141203)
XLA Ops:
  7.2 3.7 %convolution_convert_fusion = bf16[512,1536]{1,0:T(8,128)(2,1)} fusion(bf16[512,384]{1,0:T(8,128)(2,1)} %param.11, bf16[384,1536]{1,0:T(8,128)(2,1)} %param.12), kind=kOutput, calls=%fused_computation.14 | convolution fusion | flops 604766208 | bytes 3145728 | tf_op jit(solution)/shard_map/dot_general | solution.py:48
  11.0 1.3 fusion.33
  14.9 1.4 copy.43
  16.3 1.5 eq.86
  17.9 1.5 eq.82
  20.8 1.3 fusion.29
  22.1 1.6 reduce_window_sum.24
  24.5 0.9 select_reduce_fusion.2
  25.5 0.8 select_reduce_fusion.1
  27.0 0.9 mul.83
  27.9 1.4 fusion.28
  29.3 21.8 %reduce-window.6 = s32[40,8,128]{2,1,0:T(8,128)} reduce-window(s32[40,8,128]{2,1,0:T(8,128)} %fusion.28, s32[]{:T(128)} %constant.24.clone.1), window={size=1x1x128 pad=0_0x0_0x127_0}, to_apply=%region_6.7 | reduce-window | flops 5201920 | bytes 327684 | tf_op jit(solution)/shard_map/reduce-window
  51.1 1.7 slice.18
  52.7 1.0 copy.46
  54.5 1.0 add_add_fusion
  57.0 1.2 fusion.20
  58.2 1.3 fusion.22
  59.5 9.0 %scatter_custom_fusion = bf16[1920,1536]{1,0:T(8,128)(2,1)} fusion(s32[1024]{0:T(1024)S(1)} %bitcast.48, bf16[]{:T(256)} %constant.17.clone.1, bf16[128,1536]{1,0:T(8,128)(2,1)S(1)} %fusion.22), kind=kCustom, calls=%fused_computation.11 | custom fusion | bytes 6291458 | tf_op jit(solution)/shard_map/scatter | solution.py:76
  68.5 8.2 %reshape.186 = bf16[32,2,30,1536]{3,2,1,0:T(8,128)(2,1)} reshape(bf16[1920,1536]{1,0:T(8,128)(2,1)} %scatter_custom_fusion) | data formatting | bytes 11796480 | tf_op jit(solution)/shard_map/reshape | solution.py:77
  76.8 11.2 %copy.48 = bf16[32,2,30,1536]{3,1,2,0:T(2,128)(2,1)S(1)} copy(bf16[32,2,30,1536]{3,2,1,0:T(8,128)(2,1)} %reshape.186) | data formatting | bytes 11796480 | tf_op jit(solution)/shard_map/reshape | solution.py:77
  88.0 74.9 %all_to_all.10 = bf16[32,2,30,1536]{3,1,2,0:T(2,128)(2,1)S(1)} all-to-all(bf16[32,2,30,1536]{3,1,2,0:T(2,128)(2,1)S(1)} %copy.48), channel_id=1, replica_groups=mesh['tok'=32,'tp'=4] {'tok'}, dimensions={0} | all-to-all | bytes 11796480 | tf_op jit(solution)/shard_map/all_to_all | solution.py:78
  162.9 8.3 %fusion.8 = f32[32,2,30,1024]{3,0,2,1:T(8,128)S(1)} fusion(bf16[2,1536,1024]{2,1,0:T(8,128)(2,1)} %param.19, bf16[32,2,30,1536]{3,1,2,0:T(2,128)(2,1)S(1)} %all_to_all.10), kind=kOutput, calls=%fused_computation.13 | convolution fusion | flops 6039797760 | bytes 20054016 | tf_op jit(solution)/shard_map/nsmd,sdf->nsmf/dot_general | solution.py:79
  171.2 3.5 %convert_bitcast_fusion = bf16[32,2,30,1536]{3,0,2,1:T(8,128)(2,1)S(1)} fusion(bf16[2,512,1536]{2,1,0:T(8,128)(2,1)S(1)} %copy-done, f32[32,2,30,1024]{3,0,2,1:T(8,128)S(1)} %fusion.8), kind=kOutput, calls=%fused_computation.7 | convolution fusion | flops 3028746240 | bytes 16908288 | tf_op jit(solution)/shard_map/nsmf,sfd->nsmd/dot_general | solution.py:83
  174.8 15.2 %copy.50 = bf16[32,2,30,1536]{3,1,2,0:T(2,128)(2,1)} copy(bf16[32,2,30,1536]{3,0,2,1:T(8,128)(2,1)S(1)} %convert_bitcast_fusion) | data formatting | bytes 11796480 | tf_op jit(solution)/shard_map/convert_element_type | solution.py:85
  189.9 6.0 %all-to-all-start.1 = ((bf16[32,2,30,1536]{3,1,2,0:T(2,128)(2,1)}), bf16[32,2,30,1536]{3,1,2,0:T(2,128)(2,1)}, u32[]{:S(2)}, u32[]{:S(2)}) async-start(bf16[32,2,30,1536]{3,1,2,0:T(2,128)(2,1)} %copy.50), calls=%async_computation.2 | async-start | bytes 11796480 | tf_op jit(solution)/shard_map/all_to_all | solution.py:86
  197.1 79.6 %all-to-all-done.1 = bf16[32,2,30,1536]{3,1,2,0:T(2,128)(2,1)} async-done(((bf16[32,2,30,1536]{3,1,2,0:T(2,128)(2,1)}), bf16[32,2,30,1536]{3,1,2,0:T(2,128)(2,1)}, u32[]{:S(2)}, u32[]{:S(2)}) %all-to-all-start.1) | async-done | bytes 5898272 | tf_op jit(solution)/shard_map/all_to_all | solution.py:86
  276.7 6.8 %copy.51 = bf16[32,2,30,1536]{3,2,1,0:T(8,128)(2,1)} copy(bf16[32,2,30,1536]{3,1,2,0:T(2,128)(2,1)} %all-to-all-done.1) | data formatting | bytes 11796480 | tf_op jit(solution)/shard_map/all_to_all | solution.py:86
  283.5 8.2 %reshape.187 = bf16[1920,1536]{1,0:T(8,128)(2,1)} reshape(bf16[32,2,30,1536]{3,2,1,0:T(8,128)(2,1)} %copy.51) | data formatting | bytes 11796480 | tf_op jit(solution)/shard_map/reshape | solution.py:87
  291.7 10.9 %gather_fusion = bf16[1024,1536]{1,0:T(8,128)(2,1)} fusion(bf16[1920,1536]{1,0:T(8,128)(2,1)} %reshape.187, s32[1024]{0:T(1024)S(1)} %broadcast_clamp_fusion), kind=kCustom, calls=%fused_computation | custom fusion | bytes 6295552 | tf_op jit(solution)/shard_map/gather | solution.py:87
  302.6 4.7 %fusion = f32[128,1536]{1,0:T(8,128)S(1)} fusion(bf16[1024,1536]{1,0:T(8,128)(2,1)} %gather_fusion, f32[128,8]{1,0:T(8,128)} %copy.52), kind=kLoop, calls=%fused_computation.3 | loop fusion | flops 4521984 | bytes 3936256 | tf_op jit(solution)/shard_map/reduce_sum | solution.py:89
  307.3 1.3 fusion.17
  308.6 0.9 fusion.19
  (48 shorter events, 9.0 us)
Async XLA Ops:
  7.2 164.1 %copy-start = (bf16[2,512,1536]{2,1,0:T(8,128)(2,1)S(1)}, bf16[2,512,1536]{2,1,0:T(8,128)(2,1)}, u32[]{:S(2)}) copy-start(bf16[2,512,1536]{2,1,0:T(8,128)(2,1)} %param.20) | copy-start | bytes 9437188
  7.2 49.8 %copy-start.2 = (bf16[128,1536]{1,0:T(8,128)(2,1)S(1)}, bf16[128,1536]{1,0:T(8,128)(2,1)}, u32[]{:S(2)}) copy-start(bf16[128,1536]{1,0:T(8,128)(2,1)} %param.13) | copy-start | bytes 1179652
  7.2 49.8 %reduce-scatter.2.cloned.1.call-start = ((), (), s32[]{:S(2)}) async-start(), calls=%async_computation.3 | async-start | bytes 1966080 | tf_op jit(solution)/shard_map/reduce_scatter | solution.py:47
  12.9 0.5 copy-start.8
  189.9 6.1 %copy-start.5 = (bf16[1536,40]{0,1:T(8,128)(2,1)S(1)}, bf16[1536,40]{0,1:T(8,128)(2,1)}, u32[]{:S(2)}) copy-start(bf16[1536,40]{0,1:T(8,128)(2,1)} %param.15) | copy-start | bytes 368644
  189.9 6.3 %copy-start.6 = (s32[128,8]{0,1:T(8,128)S(1)}, s32[128,8]{0,1:T(8,128)}, u32[]{:S(2)}) copy-start(s32[128,8]{0,1:T(8,128)} %param.16) | copy-start | bytes 12292
  189.9 6.4 %copy-start.9 = (pred[128]{0:T(512)(128)(4,1)S(1)}, pred[128]{0:T(512)(128)(4,1)}, u32[]{:S(2)}) copy-start(pred[128]{0:T(512)(128)(4,1)} %copy-done.8) | copy-start | bytes 388
  189.9 86.8 %all-to-all-start.1 = ((bf16[32,2,30,1536]{3,1,2,0:T(2,128)(2,1)}), bf16[32,2,30,1536]{3,1,2,0:T(2,128)(2,1)}, u32[]{:S(2)}, u32[]{:S(2)}) async-start(bf16[32,2,30,1536]{3,1,2,0:T(2,128)(2,1)} %copy.50), calls=%async_computation.2 | async-start | bytes 11796480 | tf_op jit(solution)/shard_map/all_to_all | solution.py:86
  291.7 15.6 %copy-start.3 = (bf16[128,1536]{1,0:T(8,128)(2,1)S(1)}, bf16[128,1536]{1,0:T(8,128)(2,1)}, u32[]{:S(2)}) copy-start(bf16[128,1536]{1,0:T(8,128)(2,1)} %param.13) | copy-start | bytes 1179652
  291.7 17.8 %copy-start.1 = (bf16[2,512,1536]{2,1,0:T(8,128)(2,1)S(1)}, bf16[2,512,1536]{2,1,0:T(8,128)(2,1)}, u32[]{:S(2)}) copy-start(bf16[2,512,1536]{2,1,0:T(8,128)(2,1)} %param.20) | copy-start | bytes 9437188
  302.6 6.0 %copy-start.7 = (f32[1536]{0:T(1024)S(1)}, f32[1536]{0:T(1024)}, u32[]{:S(2)}) copy-start(f32[1536]{0:T(1024)} %param.21) | copy-start | bytes 18436
  308.6 0.9 copy-start.4
Sparse Core Ops, SparseCore 0:
  11.1 28.1 reduce-scatter.1
where the time goes:
time: 319 us; the launch traced here: 316 us
  local copies, waits for them, and re-layouts  82.6 us (26%)
  waiting for transfers between devices  79.7 us (25%)
  blocking collectives  74.9 us (23%)
  other arithmetic  43.1 us (14%)
  matrix products  15.8 us (5%)
  between operations  14.3 us (4%)
  starting transfers between devices  6.09 us (2%)
    all_to_all x1, waiting for transfers between devices, shards(): lax.all_to_all(computed, 'tok', split_axis=0, concat_axis=0, tiled=True)  79.6 us
    all_to_all x1, blocking collectives, shards(): lax.all_to_all(outgoing, 'tok', split_axis=0, concat_axis=0, tiled=True)  74.9 us
    another operation x2, other arithmetic  21.8 us
    reshape x2, local copies, waits for them, and re-layouts, shards(): outgoing = outgoing.reshape(tok_total, w_in.shape[0], bucket_depth, width)  19.4 us
    convert_element_type x1, local copies, waits for them, and re-layouts, shards(): computed = jnp.einsum('nsmf,sfd->nsmd', activated, w_out, preferred_eleme...  15.2 us
    gather x1, local copies, waits for them, and re-layouts, shards(): returned.reshape(capacity, width)[jnp.minimum(target, capacity - 1)]  10.9 us
    scatter x1, local copies, waits for them, and re-layouts, shards(): jnp.zeros((capacity, width), jnp.bfloat16).at[target]  9.02 us
    dot_general x1, matrix products, shards(): jnp.einsum('nsmd,sdf->nsmf', arrived, w_in, preferred_element_type=jnp.fl...  8.34 us
  transfers between devices with their start and end apart: 2, of which 1 were waited for; matrix products, arithmetic and copies ran while one was open for 15% of the time, Pallas kernels for 0%

commit v1 on v0

--- a/solution.py
+++ b/solution.py
@@ -6,6 +6,7 @@
 E = 40
 TOPK = 8
 MOST = 30
+DEPTH = 32
 
 
 def rms_norm(source, gain_vec):
@@ -41,9 +42,12 @@
     row_count = residual.shape[0]
     width = residual.shape[1]
     hidden_units = w_out.shape[1]
+    local_slots = w_in.shape[0]
     tok_rank = lax.axis_index("tok")
     tp_rank = lax.axis_index("tp")
     tok_total = lax.axis_size("tok")
+    slot_total = slot_expert.shape[0]
+    capacity = slot_total * DEPTH
     attn_out = lax.psum_scatter(
         jnp.dot(context, attn_weight, preferred_element_type=jnp.float32).astype(jnp.bfloat16),
         "tp",
@@ -62,20 +66,20 @@
     live_rows = tp_rank * row_count + jnp.arange(row_count, dtype=jnp.int32) < length_cap
     serving = serve_slots(slot_expert, tok_rank)
     slot_of = jnp.sum(jnp.where(chooser, serving[None, None, :], 0), axis=-1)
-    flat_choose = (
-        (chooser & live_rows[:, None, None]).reshape(row_count * TOPK, E).astype(jnp.int32)
-    )
-    running_rank = jnp.cumsum(flat_choose, axis=0) - 1
-    position = jnp.sum(running_rank * flat_choose, axis=1)
-    bucket_depth = MOST
-    slot_total = slot_expert.shape[0]
-    capacity = slot_total * bucket_depth
-    live_flat = jnp.repeat(live_rows, TOPK)
-    target = jnp.where(live_flat, slot_of.reshape(-1) * bucket_depth + position, capacity)
-    repeated = jnp.repeat(normed, TOPK, axis=0)
-    outgoing = jnp.zeros((capacity, width), jnp.bfloat16).at[target].set(repeated, mode="drop")
-    outgoing = outgoing.reshape(tok_total, w_in.shape[0], bucket_depth, width)
+    named = (jnp.any(chooser, axis=1) & live_rows[:, None]).astype(jnp.bfloat16)
+    row_ids = jnp.arange(row_count, dtype=jnp.int32)
+    before = (row_ids[None, :] < row_ids[:, None]).astype(jnp.bfloat16)
+    earlier = jnp.dot(before, named, preferred_element_type=jnp.float32).astype(jnp.int32)
+    position = jnp.sum(jnp.where(chooser, earlier[:, None, :], 0), axis=-1)
+    target = jnp.where(live_rows[:, None], slot_of * DEPTH + position, capacity)
+    picks = target[:, :, None] == jnp.arange(capacity, dtype=jnp.int32)[None, None, :]
+    dispatch = jnp.any(picks, axis=1).astype(jnp.bfloat16)
+    outgoing = lax.dot_general(
+        dispatch, normed, (((0,), (0,)), ((), ())), preferred_element_type=jnp.float32
+    ).astype(jnp.bfloat16)
+    outgoing = outgoing.reshape(tok_total, local_slots * DEPTH, width)
     arrived = lax.all_to_all(outgoing, "tok", split_axis=0, concat_axis=0, tiled=True)
+    arrived = arrived.reshape(tok_total, local_slots, DEPTH, width)
     hidden = jnp.einsum("nsmd,sdf->nsmf", arrived, w_in, preferred_element_type=jnp.float32)
     activated = (jax.nn.silu(hidden[..., :hidden_units]) * hidden[..., hidden_units:]).astype(
         jnp.bfloat16
@@ -83,11 +87,15 @@
     computed = jnp.einsum(
         "nsmf,sfd->nsmd", activated, w_out, preferred_element_type=jnp.float32
     ).astype(jnp.bfloat16)
+    computed = computed.reshape(tok_total, local_slots * DEPTH, width)
     returned = lax.all_to_all(computed, "tok", split_axis=0, concat_axis=0, tiled=True)
-    fetched = returned.reshape(capacity, width)[jnp.minimum(target, capacity - 1)]
-    weight_flat = jnp.where(live_rows[:, None], gate_probs, jnp.float32(0.0)).reshape(-1)
-    expert_sum = jnp.sum(
-        (fetched.astype(jnp.float32) * weight_flat[:, None]).reshape(row_count, TOPK, width), axis=1
+    returned = returned.reshape(capacity, width)
+    gate_live = jnp.where(live_rows[:, None], gate_probs, jnp.float32(0.0))
+    combine = jnp.sum(jnp.where(picks, gate_live[:, :, None], jnp.float32(0.0)), axis=1)
+    combine_hi = combine.astype(jnp.bfloat16)
+    combine_lo = (combine - combine_hi.astype(jnp.float32)).astype(jnp.bfloat16)
+    expert_sum = jnp.dot(combine_hi, returned, preferred_element_type=jnp.float32) + jnp.dot(
+        combine_lo, returned, preferred_element_type=jnp.float32
     )
     stream_out = (stream.astype(jnp.float32) + expert_sum).astype(jnp.bfloat16)
     next_normed = rms_norm(stream_out, gain_next)

time: 319 us -> 252 us (0.79)
  local copies, waits for them, and re-layouts: 82.6 us -> 3.99 us
  other arithmetic: 43.1 us -> 18.4 us
  waiting for transfers between devices: 79.7 us -> 97.8 us
  matrix products: 15.8 us -> 32.2 us
  blocking collectives: 74.9 us -> 79 us
    reshape x4 -> x0, local copies, waits for them, and re-layouts: 28.4 us -> none  [the longest x2 19.4 us: shards(): outgoing = outgoing.reshape(tok_total, w_in.shape[0], bucket_depth, width)]
    another operation x2 -> x0, other arithmetic: 21.8 us -> none
    reduce_scatter x1, waiting for transfers between devices: 0.02 us -> 17.3 us  [shards(): lax.psum_scatter(jnp.dot(context, attn_weight, preferred_element_type=jnp...]
    convert_element_type x1, local copies, waits for them, and re-layouts: 15.2 us -> 3.09 us  [shards(): computed = jnp.einsum('nsmf,sfd->nsmd', activated, w_out, preferred_eleme...]
    dot_general x0 -> x4, matrix products: none -> 11.2 us  [the longest x1 4.17 us: shards(): jnp.dot(combine_hi, returned, preferred_element_type=jnp.float32)]
    gather x1 -> x0, local copies, waits for them, and re-layouts: 10.9 us -> none  [shards(): returned.reshape(capacity, width)[jnp.minimum(target, capacity - 1)]]
    scatter x1 -> x0, local copies, waits for them, and re-layouts: 9.02 us -> none  [shards(): jnp.zeros((capacity, width), jnp.bfloat16).at[target]]
    all_to_all x1 -> x0, local copies, waits for them, and re-layouts: 6.77 us -> none  [shards(): lax.all_to_all(computed, 'tok', split_axis=0, concat_axis=0, tiled=True)]
  transfers between devices with their start and end apart: 2 -> 2, of which waited for: 1 -> 2; matrix products, arithmetic and copies ran while one was open for 15% -> 7% of each run, Pallas kernels for 0% -> 0%
where the time goes in v1:
time: 252 us
  waiting for transfers between devices  97.8 us (39%)
  blocking collectives  79 us (31%)
  matrix products  32.2 us (13%)
  other arithmetic  18.4 us (7%)
  between operations  14.2 us (6%)
  starting transfers between devices  6.16 us (2%)
  local copies, waits for them, and re-layouts  3.99 us (2%)
    all_to_all x1, waiting for transfers between devices, shards(): lax.all_to_all(computed, 'tok', split_axis=0, concat_axis=0, tiled=True)  80.4 us
    all_to_all x1, blocking collectives, shards(): lax.all_to_all(outgoing, 'tok', split_axis=0, concat_axis=0, tiled=True)  79 us
    reduce_scatter x1, waiting for transfers between devices, shards(): lax.psum_scatter(jnp.dot(context, attn_weight, preferred_element_type=jnp...  17.3 us
    dot_general x1, matrix products, shards(): jnp.einsum('nsmd,sdf->nsmf', arrived, w_in, preferred_element_type=jnp.fl...  8.82 us
    dot_general x1, matrix products, shards(): jnp.einsum('nsmf,sfd->nsmd', activated, w_out, preferred_element_type=jnp...  7.27 us
    all_to_all x1, starting transfers between devices, shards(): lax.all_to_all(computed, 'tok', split_axis=0, concat_axis=0, tiled=True)  6.12 us
  transfers between devices with their start and end apart: 2, of which 2 were waited for; matrix products, arithmetic and copies ran while one was open for 7% of the time, Pallas kernels for 0%

profile of v1, /device:TPU:8, one launch (start us, length us, event | category | flops | bytes accessed | tf_op | source)
XLA Modules:
  0.0 251.8 jit_solution(1874638575443308843)
XLA Ops:
  7.2 0.0 reduce-scatter.2.cloned.1.call-start
  7.2 3.7 %convolution_convert_fusion.1 = bf16[512,1536]{1,0:T(8,128)(2,1)} fusion(bf16[512,384]{1,0:T(8,128)(2,1)} %param.11, bf16[384,1536]{1,0:T(8,128)(2,1)} %param.12), kind=kOutput, calls=%fused_computation.12 | convolution fusion | flops 604766208 | bytes 3145728 | tf_op jit(solution)/shard_map/dot_general | solution.py:52
  10.9 0.0 reduce-scatter.2.cloned.1.call-update
  10.9 0.7 fusion.28
  11.6 0.2 reduce_window_sum.11
  11.8 1.3 fusion.34
  13.1 0.7 add_compare_fusion.1
  13.8 0.8 fusion.31
  14.6 0.7 fusion.24
  15.3 0.1 and_select_fusion
  15.4 0.8 select_reduce_fusion.4
  16.2 0.1 convolution_convert_fusion.2
  16.4 0.8 select_reduce_fusion.3
  17.2 0.1 copy.21
  17.3 4.7 %fusion = pred[128,2048]{1,0:T(8,128)(4,1)} fusion(s32[128,8]{1,0:T(8,128)S(1)} %copy.21), kind=kLoop, calls=%fused_computation.2 | loop fusion | flops 3932160 | bytes 266240 | tf_op jit(solution)/shard_map/reduce_or | solution.py:76
  22.0 17.3 %reduce-scatter.2.cloned.1.call-done = bf16[128,1536]{1,0:T(8,128)(2,1)} async-done(((bf16[512,1536]{1,0:T(8,128)(2,1)}), bf16[128,1536]{1,0:T(8,128)(2,1)}) %reduce-scatter.2.cloned.1.call-update) | async-done | bytes 393232 | tf_op jit(solution)/shard_map/reduce_scatter | solution.py:51
  39.3 1.3 fusion.18
  40.7 3.0 %convolution_convert_fusion = bf16[2048,1536]{1,0:T(8,128)(2,1)S(1)} fusion(pred[128,2048]{1,0:T(8,128)(4,1)} %fusion, bf16[128,1536]{1,0:T(8,128)(2,1)S(1)} %get-tuple-element.5, f32[1536]{0:T(1024)S(1)} %copy-done.5, f32[128]{0:T(128)S(1)} %add_rsqrt_fusion.1), kind=kOutput, calls=%fused_computation.3 | convolution fusion | flops 809238528 | bytes 6953472 | tf_op jit(solution)/shard_map/dot_general | solution.py:77
  43.7 79.0 %all_to_all.10 = bf16[32,64,1536]{2,1,0:T(8,128)(2,1)S(1)} all-to-all(bf16[32,64,1536]{2,1,0:T(8,128)(2,1)S(1)} %bitcast.26), channel_id=1, replica_groups=mesh['tok'=32,'tp'=4] {'tok'}, dimensions={0} | all-to-all | bytes 12582912 | tf_op jit(solution)/shard_map/all_to_all | solution.py:81
  122.7 8.8 %fusion.5 = f32[32,2,32,1024]{3,2,0,1:T(8,128)} fusion(bf16[2,1536,1024]{2,1,0:T(8,128)(2,1)S(1)} %bitcast.30, bf16[32,2,32,1536]{3,2,1,0:T(8,128)(2,1)S(1)} %bitcast.28), kind=kOutput, calls=%fused_computation.10 | convolution fusion | flops 6442450944 | bytes 20971520 | tf_op jit(solution)/shard_map/nsmd,sdf->nsmf/dot_general | solution.py:83
  131.5 7.3 %convert_bitcast_fusion = bf16[32,2,32,1536]{3,2,0,1:T(8,128)(2,1)S(1)} fusion(bf16[2,512,1536]{2,1,0:T(8,128)(2,1)S(1)} %copy-done, f32[32,2,32,1024]{3,2,0,1:T(8,128)} %fusion.5), kind=kOutput, calls=%fused_computation.7 | convolution fusion | flops 3230662656 | bytes 17825792 | tf_op jit(solution)/shard_map/nsmf,sfd->nsmd/dot_general | solution.py:87
  138.8 3.1 %copy.24 = bf16[32,2,32,1536]{3,2,1,0:T(8,128)(2,1)} copy(bf16[32,2,32,1536]{3,2,0,1:T(8,128)(2,1)S(1)} %convert_bitcast_fusion) | data formatting | bytes 12582912 | tf_op jit(solution)/shard_map/convert_element_type | solution.py:89
  141.9 6.1 %all-to-all-start.1 = ((bf16[32,64,1536]{2,1,0:T(8,128)(2,1)}), bf16[32,64,1536]{2,1,0:T(8,128)(2,1)}, u32[]{:S(2)}, u32[]{:S(2)}) async-start(bf16[32,64,1536]{2,1,0:T(8,128)(2,1)} %bitcast.27), calls=%async_computation.2 | async-start | bytes 12582912 | tf_op jit(solution)/shard_map/all_to_all | solution.py:91
  148.0 1.2 fusion.26
  149.2 0.0 copy-done.4
  149.3 0.6 divide_select_fusion
  150.0 0.7 copy.22
  150.7 4.7 %select_reduce_fusion = f32[128,2048]{1,0:T(8,128)} fusion(f32[128,8]{1,0:T(8,128)} %copy.22, s32[128,8]{1,0:T(8,128)} %copy-done.3), kind=kLoop, calls=%fused_computation | loop fusion | flops 6029312 | bytes 1056768 | tf_op jit(solution)/shard_map/reduce_sum | solution.py:94
  155.4 80.4 %all-to-all-done.1 = bf16[32,64,1536]{2,1,0:T(8,128)(2,1)} async-done(((bf16[32,64,1536]{2,1,0:T(8,128)(2,1)}), bf16[32,64,1536]{2,1,0:T(8,128)(2,1)}, u32[]{:S(2)}, u32[]{:S(2)}) %all-to-all-start.1) | async-done | bytes 6291488 | tf_op jit(solution)/shard_map/all_to_all | solution.py:91
  235.8 4.2 %fusion.22 = f32[128,1536]{1,0:T(8,128)S(1)} fusion(bf16[2048,1536]{1,0:T(8,128)(2,1)} %bitcast.9, f32[128,2048]{1,0:T(8,128)} %select_reduce_fusion), kind=kOutput, calls=%fused_computation.31 | convolution fusion | flops 805568512 | bytes 8126464 | tf_op jit(solution)/shard_map/dot_general | solution.py:97
  240.1 3.9 %fusion.15 = (f32[128]{0:T(128)S(1)}, bf16[128,1536]{1,0:T(8,128)(2,1)S(1)}) fusion(f32[128,1536]{1,0:T(8,128)S(1)} %fusion.22, bf16[2048,1536]{1,0:T(8,128)(2,1)} %bitcast.9, f32[128,2048]{1,0:T(8,128)S(1)} %copy-done.1, bf16[128,1536]{1,0:T(8,128)(2,1)S(1)} %get-tuple-element.5), kind=kOutput, calls=%fused_computation.23 | convolution fusion | flops 807731072 | bytes 8913408 | tf_op jit(solution)/shard_map/dot_general | solution.py:97
  244.0 0.9 fusion.17
  (26 shorter events, 0.1 us)
Async XLA Ops:
  7.2 124.4 %copy-start = (bf16[2,512,1536]{2,1,0:T(8,128)(2,1)S(1)}, bf16[2,512,1536]{2,1,0:T(8,128)(2,1)}, u32[]{:S(2)}) copy-start(bf16[2,512,1536]{2,1,0:T(8,128)(2,1)} %param.20) | copy-start | bytes 9437188
  7.2 33.5 %copy-start.5 = (f32[1536]{0:T(1024)S(1)}, f32[1536]{0:T(1024)}, u32[]{:S(2)}) copy-start(f32[1536]{0:T(1024)} %param.14) | copy-start | bytes 18436
  7.2 32.1 %reduce-scatter.2.cloned.1.call-start = ((), (), s32[]{:S(2)}) async-start(), calls=%async_computation.3 | async-start | bytes 1966080 | tf_op jit(solution)/shard_map/reduce_scatter | solution.py:51
  13.8 3.4 %copy-start.7 = (pred[128]{0:T(512)(128)(4,1)}, pred[128]{0:T(512)(128)(4,1)S(1)}, u32[]{:S(2)}) copy-start(pred[128]{0:T(512)(128)(4,1)S(1)} %add_compare_fusion.1) | copy-start | bytes 388
  17.3 4.7 %copy-start.3 = (s32[128,8]{1,0:T(8,128)}, s32[128,8]{1,0:T(8,128)S(1)}, u32[]{:S(2)}) copy-start(s32[128,8]{1,0:T(8,128)S(1)} %copy.21) | copy-start | bytes 12292
  40.6 82.1 %slice-start = ((s8[6291456]{0:T(1024)(128)(4,1)}), s8[4194304]{0:T(1024)(128)(4,1)S(1)}, s32[]{:S(2)}) async-start(s8[6291456]{0:T(1024)(128)(4,1)} %bitcast.29), calls=%async_computation.4 | async-start | bytes 8388608
  43.7 79.1 %slice-start.1 = ((s8[6291456]{0:T(1024)(128)(4,1)}), s8[2097152]{0:T(1024)(128)(4,1)S(1)}, s32[]{:S(2)}) async-start(s8[6291456]{0:T(1024)(128)(4,1)} %bitcast.29), calls=%async_computation.5 | async-start | bytes 4194304
  141.9 7.4 %copy-start.4 = (s32[128,8]{0,1:T(8,128)S(1)}, s32[128,8]{0,1:T(8,128)}, u32[]{:S(2)}) copy-start(s32[128,8]{0,1:T(8,128)} %param.16) | copy-start | bytes 12292
  141.9 93.9 %all-to-all-start.1 = ((bf16[32,64,1536]{2,1,0:T(8,128)(2,1)}), bf16[32,64,1536]{2,1,0:T(8,128)(2,1)}, u32[]{:S(2)}, u32[]{:S(2)}) async-start(bf16[32,64,1536]{2,1,0:T(8,128)(2,1)} %bitcast.27), calls=%async_computation.2 | async-start | bytes 12582912 | tf_op jit(solution)/shard_map/all_to_all | solution.py:91
  235.8 4.2 %copy-start.1 = (f32[128,2048]{1,0:T(8,128)S(1)}, f32[128,2048]{1,0:T(8,128)}, u32[]{:S(2)}) copy-start(f32[128,2048]{1,0:T(8,128)} %select_reduce_fusion) | copy-start | bytes 3145732
  240.0 4.0 %copy-start.6 = (f32[1536]{0:T(1024)S(1)}, f32[1536]{0:T(1024)}, u32[]{:S(2)}) copy-start(f32[1536]{0:T(1024)} %param.21) | copy-start | bytes 18436
  244.0 0.9 copy-start.2
Sparse Core Ops, SparseCore 0:
  11.1 28.1 reduce-scatter.1

commit v2 on v1

--- a/solution.py
+++ b/solution.py
@@ -48,12 +48,14 @@
     tok_total = lax.axis_size("tok")
     slot_total = slot_expert.shape[0]
     capacity = slot_total * DEPTH
-    attn_out = lax.psum_scatter(
-        jnp.dot(context, attn_weight, preferred_element_type=jnp.float32).astype(jnp.bfloat16),
-        "tp",
-        scatter_dimension=0,
-        tiled=True,
-    ).astype(jnp.float32)
+    tp_total = lax.axis_size("tp")
+    partial = jnp.dot(context, attn_weight, preferred_element_type=jnp.float32).astype(jnp.bfloat16)
+    blocks = partial.reshape(tp_total, row_count, width)
+    attn_out = blocks[tp_rank].astype(jnp.float32)
+    for shift in range(1, tp_total):
+        sent = blocks[(tp_rank + shift) % tp_total]
+        pairs = [(j, (j + shift) % tp_total) for j in range(tp_total)]
+        attn_out = attn_out + lax.ppermute(sent, "tp", pairs).astype(jnp.float32)
     stream = (residual.astype(jnp.float32) + attn_out).astype(jnp.bfloat16)
     normed = rms_norm(stream, gain_first)
     logits = jnp.dot(normed, router, preferred_element_type=jnp.float32)

time: 252 us -> 237 us (0.940)
  between operations: 14.2 us -> 0.86 us
  waiting for transfers between devices: 97.8 us -> 89.5 us
  starting transfers between devices: 6.16 us -> 11.4 us
    reduce_scatter x1 -> x0, waiting for transfers between devices: 17.3 us -> none  [shards(): lax.psum_scatter(jnp.dot(context, attn_weight, preferred_element_type=jnp...]
    ppermute x0 -> x3, waiting for transfers between devices: none -> 9.06 us  [shards(): attn_out = attn_out + lax.ppermute(sent, 'tp', pairs).astype(jnp.float32)]
    ppermute x0 -> x3, starting transfers between devices: none -> 5.29 us  [shards(): attn_out = attn_out + lax.ppermute(sent, 'tp', pairs).astype(jnp.float32)]
  transfers between devices with their start and end apart: 2 -> 4, of which waited for: 2 -> 3; matrix products, arithmetic and copies ran while one was open for 7% -> 7% of each run, Pallas kernels for 0% -> 0%
where the time goes in v2:
time: 237 us; the launch traced here: 236 us
  waiting for transfers between devices  89.5 us (38%)
  blocking collectives  79.2 us (33%)
  matrix products  31.1 us (13%)
  other arithmetic  18.1 us (8%)
  starting transfers between devices  11.4 us (5%)
  local copies, waits for them, and re-layouts  6.27 us (3%)
    all_to_all x1, waiting for transfers between devices, shards(): lax.all_to_all(computed, 'tok', split_axis=0, concat_axis=0, tiled=True)  80.4 us
    all_to_all x1, blocking collectives, shards(): lax.all_to_all(outgoing, 'tok', split_axis=0, concat_axis=0, tiled=True)  79.2 us
    ppermute x3, waiting for transfers between devices, shards(): attn_out = attn_out + lax.ppermute(sent, 'tp', pairs).astype(jnp.float32)  9.06 us
    dot_general x1, matrix products, shards(): jnp.einsum('nsmd,sdf->nsmf', arrived, w_in, preferred_element_type=jnp.fl...  8.82 us
    dot_general x1, matrix products, shards(): jnp.einsum('nsmf,sfd->nsmd', activated, w_out, preferred_element_type=jnp...  7.27 us
    all_to_all x1, starting transfers between devices, shards(): lax.all_to_all(computed, 'tok', split_axis=0, concat_axis=0, tiled=True)  6.12 us
    ppermute x3, starting transfers between devices, shards(): attn_out = attn_out + lax.ppermute(sent, 'tp', pairs).astype(jnp.float32)  5.29 us
  transfers between devices with their start and end apart: 4, of which 3 were waited for; matrix products, arithmetic and copies ran while one was open for 7% of the time, Pallas kernels for 0%

profile of v2, /device:TPU:8, one launch (start us, length us, event | category | flops | bytes accessed | tf_op | source)
XLA Modules:
  0.0 236.4 jit_solution(17123621651510899417)
XLA Ops:
  0.7 3.7 %convolution_convert_fusion.1 = bf16[512,1536]{1,0:T(8,128)(2,1)} fusion(bf16[512,384]{1,0:T(8,128)(2,1)} %param.11, bf16[384,1536]{1,0:T(8,128)(2,1)} %param.12), kind=kOutput, calls=%fused_computation.12 | convolution fusion | flops 604766208 | bytes 3145728 | tf_op jit(solution)/shard_map/dot_general | solution.py:52
  4.4 2.3 dynamic-slice_bitcast_fusion.2
  6.6 4.0 %collective-permute-start.2 = (bf16[128,1536]{1,0:T(8,128)(2,1)}, bf16[128,1536]{1,0:T(8,128)(2,1)}, u32[]{:S(2)}, u32[]{:S(2)}) collective-permute-start(bf16[128,1536]{1,0:T(8,128)(2,1)} %get-tuple-element.7), channel_id=1, source_target_pairs={{0,3},{1,0},{2,1},{3,2},{4,7},{5,4},{6,5},{7,6},{8,11},{9,8},{10,9... | collective-permute-start | bytes 1179656 | tf_op jit(solution)/shard_map/ppermute | solution.py:58
  10.7 1.3 collective-permute-start
  11.9 0.7 fusion.32
  12.6 0.8 fusion.35
  13.4 0.2 reduce_window_sum.11
  13.6 0.7 fusion.28
  14.3 0.1 and_select_fusion
  14.4 1.3 fusion.38
  15.7 0.8 select_reduce_fusion.4
  16.5 0.6 add_compare_fusion.1
  17.1 0.1 convolution_convert_fusion.2
  17.2 0.8 select_reduce_fusion.3
  18.2 4.0 %fusion = pred[128,2048]{1,0:T(8,128)(4,1)S(1)} fusion(s32[128,8]{1,0:T(8,128)S(1)} %copy.21), kind=kLoop, calls=%fused_computation.2 | loop fusion | flops 3932160 | bytes 266240 | tf_op jit(solution)/shard_map/reduce_or | solution.py:78
  22.1 5.6 %collective-permute-done.2 = bf16[128,1536]{1,0:T(8,128)(2,1)} collective-permute-done((bf16[128,1536]{1,0:T(8,128)(2,1)}, bf16[128,1536]{1,0:T(8,128)(2,1)}, u32[]{:S(2)}, u32[]{:S(2)}) %collective-permute-start.2) | collective-permute-done | bytes 393248 | tf_op jit(solution)/shard_map/ppermute | solution.py:58
  27.8 3.4 %collective-permute-done = bf16[128,1536]{1,0:T(8,128)(2,1)} collective-permute-done((bf16[128,1536]{1,0:T(8,128)(2,1)}, bf16[128,1536]{1,0:T(8,128)(2,1)}, u32[]{:S(2)}, u32[]{:S(2)}) %collective-permute-start) | collective-permute-done | bytes 393248 | tf_op jit(solution)/shard_map/ppermute | solution.py:58
  31.2 1.8 fusion.18
  33.1 1.9 convolution_convert_fusion
  35.0 79.2 %all_to_all.10 = bf16[32,64,1536]{2,1,0:T(8,128)(2,1)S(1)} all-to-all(bf16[32,64,1536]{2,1,0:T(8,128)(2,1)S(1)} %bitcast.37), channel_id=1, replica_groups=mesh['tok'=32,'tp'=4] {'tok'}, dimensions={0} | all-to-all | bytes 12582912 | tf_op jit(solution)/shard_map/all_to_all | solution.py:83
  114.2 8.8 %fusion.5 = f32[32,2,32,1024]{3,2,0,1:T(8,128)} fusion(bf16[2,1536,1024]{2,1,0:T(8,128)(2,1)S(1)} %bitcast.43, bf16[32,2,32,1536]{3,2,1,0:T(8,128)(2,1)S(1)} %bitcast.39), kind=kOutput, calls=%fused_computation.10 | convolution fusion | flops 6442450944 | bytes 20971520 | tf_op jit(solution)/shard_map/nsmd,sdf->nsmf/dot_general | solution.py:85
  123.0 7.3 %convert_bitcast_fusion = bf16[32,2,32,1536]{3,2,0,1:T(8,128)(2,1)S(1)} fusion(bf16[2,512,1536]{2,1,0:T(8,128)(2,1)S(1)} %copy-done, f32[32,2,32,1024]{3,2,0,1:T(8,128)} %fusion.5), kind=kOutput, calls=%fused_computation.7 | convolution fusion | flops 3230662656 | bytes 17825792 | tf_op jit(solution)/shard_map/nsmf,sfd->nsmd/dot_general | solution.py:89
  130.3 3.1 %copy.24 = bf16[32,2,32,1536]{3,2,1,0:T(8,128)(2,1)} copy(bf16[32,2,32,1536]{3,2,0,1:T(8,128)(2,1)S(1)} %convert_bitcast_fusion) | data formatting | bytes 12582912 | tf_op jit(solution)/shard_map/convert_element_type | solution.py:91
  133.4 6.1 %all-to-all-start.1 = ((bf16[32,64,1536]{2,1,0:T(8,128)(2,1)}), bf16[32,64,1536]{2,1,0:T(8,128)(2,1)}, u32[]{:S(2)}, u32[]{:S(2)}) async-start(bf16[32,64,1536]{2,1,0:T(8,128)(2,1)} %bitcast.38), calls=%async_computation.1 | async-start | bytes 12582912 | tf_op jit(solution)/shard_map/all_to_all | solution.py:93
  139.5 1.2 fusion.30
  140.8 0.6 divide_select_fusion
  141.4 0.7 copy.22
  142.2 4.7 %select_reduce_fusion = f32[128,2048]{1,0:T(8,128)} fusion(f32[128,8]{1,0:T(8,128)} %copy.22, s32[128,8]{1,0:T(8,128)} %copy-done.3), kind=kLoop, calls=%fused_computation | loop fusion | flops 6029312 | bytes 1056768 | tf_op jit(solution)/shard_map/reduce_sum | solution.py:96
  146.9 80.4 %all-to-all-done.1 = bf16[32,64,1536]{2,1,0:T(8,128)(2,1)} async-done(((bf16[32,64,1536]{2,1,0:T(8,128)(2,1)}), bf16[32,64,1536]{2,1,0:T(8,128)(2,1)}, u32[]{:S(2)}, u32[]{:S(2)}) %all-to-all-start.1) | async-done | bytes 6291488 | tf_op jit(solution)/shard_map/all_to_all | solution.py:93
  227.3 4.2 %fusion.26 = f32[128,1536]{1,0:T(8,128)S(1)} fusion(bf16[2048,1536]{1,0:T(8,128)(2,1)} %bitcast.14, f32[128,2048]{1,0:T(8,128)} %select_reduce_fusion), kind=kOutput, calls=%fused_computation.38 | convolution fusion | flops 805568512 | bytes 8126464 | tf_op jit(solution)/shard_map/dot_general | solution.py:99
  231.5 3.9 %fusion.15 = (f32[128]{0:T(128)S(1)}, bf16[128,1536]{1,0:T(8,128)(2,1)S(1)}) fusion(f32[128,1536]{1,0:T(8,128)S(1)} %fusion.26, bf16[2048,1536]{1,0:T(8,128)(2,1)} %bitcast.14, f32[128,2048]{1,0:T(8,128)S(1)} %copy-done.1, bf16[128,1536]{1,0:T(8,128)(2,1)S(1)} %get-tuple-element.5), kind=kOutput, calls=%fused_computation.23 | convolution fusion | flops 807731072 | bytes 8913408 | tf_op jit(solution)/shard_map/dot_general | solution.py:99
  235.5 0.9 fusion.17
  (30 shorter events, 0.3 us)
Async XLA Ops:
  0.6 122.4 %copy-start = (bf16[2,512,1536]{2,1,0:T(8,128)(2,1)S(1)}, bf16[2,512,1536]{2,1,0:T(8,128)(2,1)}, u32[]{:S(2)}) copy-start(bf16[2,512,1536]{2,1,0:T(8,128)(2,1)} %param.20) | copy-start | bytes 9437188
  0.6 32.4 %copy-start.5 = (f32[1536]{0:T(1024)S(1)}, f32[1536]{0:T(1024)}, u32[]{:S(2)}) copy-start(f32[1536]{0:T(1024)} %param.14) | copy-start | bytes 18436
  6.6 21.1 %collective-permute-start.2 = (bf16[128,1536]{1,0:T(8,128)(2,1)}, bf16[128,1536]{1,0:T(8,128)(2,1)}, u32[]{:S(2)}, u32[]{:S(2)}) collective-permute-start(bf16[128,1536]{1,0:T(8,128)(2,1)} %get-tuple-element.7), channel_id=1, source_target_pairs={{0,3},{1,0},{2,1},{3,2},{4,7},{5,4},{6,5},{7,6},{8,11},{9,8},{10,9... | collective-permute-start | bytes 1179656 | tf_op jit(solution)/shard_map/ppermute | solution.py:58
  10.7 17.1 %collective-permute-start.1 = (bf16[128,1536]{1,0:T(8,128)(2,1)}, bf16[128,1536]{1,0:T(8,128)(2,1)}, u32[]{:S(2)}, u32[]{:S(2)}) collective-permute-start(bf16[128,1536]{1,0:T(8,128)(2,1)} %get-tuple-element.8), channel_id=1, source_target_pairs={{0,2},{1,3},{2,0},{3,1},{4,6},{5,7},{6,4},{7,5},{8,10},{9,11},{10,... | collective-permute-start | bytes 1179656 | tf_op jit(solution)/shard_map/ppermute | solution.py:58
  10.7 20.5 %collective-permute-start = (bf16[128,1536]{1,0:T(8,128)(2,1)}, bf16[128,1536]{1,0:T(8,128)(2,1)}, u32[]{:S(2)}, u32[]{:S(2)}) collective-permute-start(bf16[128,1536]{1,0:T(8,128)(2,1)} %get-tuple-element.6), channel_id=1, source_target_pairs={{0,1},{1,2},{2,3},{3,0},{4,5},{5,6},{6,7},{7,4},{8,9},{9,10},{10,1... | collective-permute-start | bytes 1179656 | tf_op jit(solution)/shard_map/ppermute | solution.py:58
  17.1 1.0 copy-start.7
  18.2 9.6 %copy-start.3 = (s32[128,8]{1,0:T(8,128)}, s32[128,8]{1,0:T(8,128)S(1)}, u32[]{:S(2)}) copy-start(s32[128,8]{1,0:T(8,128)S(1)} %copy.21) | copy-start | bytes 12292
  33.1 81.1 %slice-start = ((s8[6291456]{0:T(1024)(128)(4,1)}), s8[4194304]{0:T(1024)(128)(4,1)S(1)}, s32[]{:S(2)}) async-start(s8[6291456]{0:T(1024)(128)(4,1)} %bitcast.42), calls=%async_computation.2 | async-start | bytes 8388608
  35.0 79.2 %slice-start.1 = ((s8[6291456]{0:T(1024)(128)(4,1)}), s8[2097152]{0:T(1024)(128)(4,1)S(1)}, s32[]{:S(2)}) async-start(s8[6291456]{0:T(1024)(128)(4,1)} %bitcast.42), calls=%async_computation.3 | async-start | bytes 4194304
  133.4 7.3 %copy-start.4 = (s32[128,8]{0,1:T(8,128)S(1)}, s32[128,8]{0,1:T(8,128)}, u32[]{:S(2)}) copy-start(s32[128,8]{0,1:T(8,128)} %param.16) | copy-start | bytes 12292
  133.4 93.9 %all-to-all-start.1 = ((bf16[32,64,1536]{2,1,0:T(8,128)(2,1)}), bf16[32,64,1536]{2,1,0:T(8,128)(2,1)}, u32[]{:S(2)}, u32[]{:S(2)}) async-start(bf16[32,64,1536]{2,1,0:T(8,128)(2,1)} %bitcast.38), calls=%async_computation.1 | async-start | bytes 12582912 | tf_op jit(solution)/shard_map/all_to_all | solution.py:93
  227.3 4.2 %copy-start.1 = (f32[128,2048]{1,0:T(8,128)S(1)}, f32[128,2048]{1,0:T(8,128)}, u32[]{:S(2)}) copy-start(f32[128,2048]{1,0:T(8,128)} %select_reduce_fusion) | copy-start | bytes 3145732
  231.5 4.0 %copy-start.6 = (f32[1536]{0:T(1024)S(1)}, f32[1536]{0:T(1024)}, u32[]{:S(2)}) copy-start(f32[1536]{0:T(1024)} %param.21) | copy-start | bytes 18436
  235.4 0.9 copy-start.2

commit v3 on v2

--- a/solution.py
+++ b/solution.py
@@ -74,31 +74,36 @@
     earlier = jnp.dot(before, named, preferred_element_type=jnp.float32).astype(jnp.int32)
     position = jnp.sum(jnp.where(chooser, earlier[:, None, :], 0), axis=-1)
     target = jnp.where(live_rows[:, None], slot_of * DEPTH + position, capacity)
-    picks = target[:, :, None] == jnp.arange(capacity, dtype=jnp.int32)[None, None, :]
-    dispatch = jnp.any(picks, axis=1).astype(jnp.bfloat16)
-    outgoing = lax.dot_general(
-        dispatch, normed, (((0,), (0,)), ((), ())), preferred_element_type=jnp.float32
-    ).astype(jnp.bfloat16)
-    outgoing = outgoing.reshape(tok_total, local_slots * DEPTH, width)
-    arrived = lax.all_to_all(outgoing, "tok", split_axis=0, concat_axis=0, tiled=True)
-    arrived = arrived.reshape(tok_total, local_slots, DEPTH, width)
-    hidden = jnp.einsum("nsmd,sdf->nsmf", arrived, w_in, preferred_element_type=jnp.float32)
-    activated = (jax.nn.silu(hidden[..., :hidden_units]) * hidden[..., hidden_units:]).astype(
-        jnp.bfloat16
-    )
-    computed = jnp.einsum(
-        "nsmf,sfd->nsmd", activated, w_out, preferred_element_type=jnp.float32
-    ).astype(jnp.bfloat16)
-    computed = computed.reshape(tok_total, local_slots * DEPTH, width)
-    returned = lax.all_to_all(computed, "tok", split_axis=0, concat_axis=0, tiled=True)
-    returned = returned.reshape(capacity, width)
     gate_live = jnp.where(live_rows[:, None], gate_probs, jnp.float32(0.0))
-    combine = jnp.sum(jnp.where(picks, gate_live[:, :, None], jnp.float32(0.0)), axis=1)
-    combine_hi = combine.astype(jnp.bfloat16)
-    combine_lo = (combine - combine_hi.astype(jnp.float32)).astype(jnp.bfloat16)
-    expert_sum = jnp.dot(combine_hi, returned, preferred_element_type=jnp.float32) + jnp.dot(
-        combine_lo, returned, preferred_element_type=jnp.float32
-    )
+    column = jnp.arange(tok_total * DEPTH, dtype=jnp.int32)
+    expert_sum = jnp.zeros((row_count, width), jnp.float32)
+    for local in range(local_slots):
+        slot_cols = (column // DEPTH) * (local_slots * DEPTH) + local * DEPTH + column % DEPTH
+        picks = target[:, :, None] == slot_cols[None, None, :]
+        dispatch = jnp.any(picks, axis=1).astype(jnp.bfloat16)
+        outgoing = lax.dot_general(
+            dispatch, normed, (((0,), (0,)), ((), ())), preferred_element_type=jnp.float32
+        ).astype(jnp.bfloat16)
+        outgoing = outgoing.reshape(tok_total, DEPTH, width)
+        arrived = lax.all_to_all(outgoing, "tok", split_axis=0, concat_axis=0, tiled=True)
+        arrived = arrived.reshape(tok_total * DEPTH, width)
+        hidden = jnp.dot(arrived, w_in[local], preferred_element_type=jnp.float32)
+        activated = (
+            jax.nn.silu(hidden[:, :hidden_units]) * hidden[:, hidden_units:]
+        ).astype(jnp.bfloat16)
+        computed = jnp.dot(activated, w_out[local], preferred_element_type=jnp.float32).astype(
+            jnp.bfloat16
+        )
+        computed = computed.reshape(tok_total, DEPTH, width)
+        returned = lax.all_to_all(computed, "tok", split_axis=0, concat_axis=0, tiled=True)
+        returned = returned.reshape(tok_total * DEPTH, width)
+        combine = jnp.sum(jnp.where(picks, gate_live[:, :, None], jnp.float32(0.0)), axis=1)
+        combine_hi = combine.astype(jnp.bfloat16)
+        combine_lo = (combine - combine_hi.astype(jnp.float32)).astype(jnp.bfloat16)
+        expert_sum = expert_sum + (
+            jnp.dot(combine_hi, returned, preferred_element_type=jnp.float32)
+            + jnp.dot(combine_lo, returned, preferred_element_type=jnp.float32)
+        )
     stream_out = (stream.astype(jnp.float32) + expert_sum).astype(jnp.bfloat16)
     next_normed = rms_norm(stream_out, gain_next)
     return (stream_out, next_normed)

time: 237 us -> 224 us (0.945)
  blocking collectives: 79.2 us -> 0 us
  waiting for transfers between devices: 89.5 us -> 138 us
  starting transfers between devices: 11.4 us -> 30.3 us
  matrix products: 31.1 us -> 38.8 us
  other arithmetic: 18.1 us -> 11.4 us
  local copies, waits for them, and re-layouts: 6.27 us -> 2.45 us
    all_to_all x1 -> x0, blocking collectives: 79.2 us -> none  [shards(): lax.all_to_all(outgoing, 'tok', split_axis=0, concat_axis=0, tiled=True)]
    all_to_all x0 -> x2, waiting for transfers between devices: none -> 65.6 us  [shards(): lax.all_to_all(outgoing, 'tok', split_axis=0, concat_axis=0, tiled=True)]
    all_to_all x1 -> x2, waiting for transfers between devices: 80.4 us -> 59.6 us  [shards(): lax.all_to_all(computed, 'tok', split_axis=0, concat_axis=0, tiled=True)]
    all_to_all x0 -> x2, starting transfers between devices: none -> 13.4 us  [shards(): lax.all_to_all(outgoing, 'tok', split_axis=0, concat_axis=0, tiled=True)]
    all_to_all x1 -> x2, starting transfers between devices: 6.12 us -> 11.6 us  [shards(): lax.all_to_all(computed, 'tok', split_axis=0, concat_axis=0, tiled=True)]
    dot_general x2 -> x4, matrix products: 16.1 us -> 19.8 us  [the longest x2 12.8 us: shards(): hidden = jnp.dot(arrived, w_in[local], preferred_element_type=jnp.float32)]
    ppermute x3, waiting for transfers between devices: 9.06 us -> 12.7 us  [shards(): attn_out = attn_out + lax.ppermute(sent, 'tp', pairs).astype(jnp.float32)]
    dot_general x1 -> x2, matrix products: 1.89 us -> 5.53 us  [shards(): lax.dot_general(dispatch, normed, (((0,), (0,)), ((), ())), preferred_ele...]
  transfers between devices with their start and end apart: 4 -> 7, of which waited for: 3 -> 6; matrix products, arithmetic and copies ran while one was open for 7% -> 17% of each run, Pallas kernels for 0% -> 0%
where the time goes in v3:
time: 224 us; the launch traced here: 222 us
  waiting for transfers between devices  138 us (62%)
  matrix products  38.8 us (17%)
  starting transfers between devices  30.3 us (14%)
  other arithmetic  11.4 us (5%)
  local copies, waits for them, and re-layouts  2.45 us (1%)
    all_to_all x2, waiting for transfers between devices, shards(): lax.all_to_all(outgoing, 'tok', split_axis=0, concat_axis=0, tiled=True)  65.6 us
    all_to_all x2, waiting for transfers between devices, shards(): lax.all_to_all(computed, 'tok', split_axis=0, concat_axis=0, tiled=True)  59.6 us
    all_to_all x2, starting transfers between devices, shards(): lax.all_to_all(outgoing, 'tok', split_axis=0, concat_axis=0, tiled=True)  13.4 us
    dot_general x2, matrix products, shards(): hidden = jnp.dot(arrived, w_in[local], preferred_element_type=jnp.float32)  12.8 us
    ppermute x3, waiting for transfers between devices, shards(): attn_out = attn_out + lax.ppermute(sent, 'tp', pairs).astype(jnp.float32)  12.7 us
    all_to_all x2, starting transfers between devices, shards(): lax.all_to_all(computed, 'tok', split_axis=0, concat_axis=0, tiled=True)  11.6 us
    dot_general x2, matrix products, shards(): jnp.dot(activated, w_out[local], preferred_element_type=jnp.float32)  7 us
    dot_general x2, matrix products, shards(): jnp.dot(combine_lo, returned, preferred_element_type=jnp.float32)  6.09 us
  transfers between devices with their start and end apart: 7, of which 6 were waited for; matrix products, arithmetic and copies ran while one was open for 17% of the time, Pallas kernels for 0%

profile of v3, /device:TPU:8, one launch (start us, length us, event | category | flops | bytes accessed | tf_op | source)
XLA Modules:
  0.0 221.8 jit_solution(17040687809408270093)
XLA Ops:
  0.7 1.2 copy-done
  1.9 2.0 convolution_convert_fusion.4
  3.9 1.0 dynamic-slice_bitcast_fusion.2
  4.9 4.0 %collective-permute-start.2 = (bf16[128,1536]{1,0:T(8,128)(2,1)}, bf16[128,1536]{1,0:T(8,128)(2,1)}, u32[]{:S(2)}, u32[]{:S(2)}) collective-permute-start(bf16[128,1536]{1,0:T(8,128)(2,1)} %get-tuple-element.11), channel_id=1, source_target_pairs={{0,3},{1,0},{2,1},{3,2},{4,7},{5,4},{6,5},{7,6},{8,11},{9,8},{10,9... | collective-permute-start | bytes 1179656 | tf_op jit(solution)/shard_map/ppermute | solution.py:58
  8.9 1.3 collective-permute-start
  10.7 0.7 fusion.55
  11.6 0.6 add_compare_fusion.1
  12.6 3.9 %compare_reduce_fusion.1 = (pred[128,1024]{1,0:T(8,128)(4,1)S(1)}, pred[128,1024]{1,0:T(8,128)(4,1)S(1)}) fusion(s32[1024]{0:T(1024)S(1)} %get-tuple-element.16, s32[128,8]{1,0:T(8,128)S(1)} %copy.16, s32[1024]{0:T(1024)S(1)} %get-tuple-element.15), kind=kLoop, calls=%fused_computation.2 | loop fusion | flops 3932160 | bytes 274432 | tf_op jit(solution)/shard_map/reduce_or | solution.py:83
  16.5 9.5 %collective-permute-done.2 = bf16[128,1536]{1,0:T(8,128)(2,1)} collective-permute-done((bf16[128,1536]{1,0:T(8,128)(2,1)}, bf16[128,1536]{1,0:T(8,128)(2,1)}, u32[]{:S(2)}, u32[]{:S(2)}) %collective-permute-start.2) | collective-permute-done | bytes 393248 | tf_op jit(solution)/shard_map/ppermute | solution.py:58
  26.1 3.2 %collective-permute-done = bf16[128,1536]{1,0:T(8,128)(2,1)} collective-permute-done((bf16[128,1536]{1,0:T(8,128)(2,1)S(1)}, bf16[128,1536]{1,0:T(8,128)(2,1)}, u32[]{:S(2)}, u32[]{:S(2)}) %collective-permute-start) | collective-permute-done | bytes 393248 | tf_op jit(solution)/shard_map/ppermute | solution.py:58
  29.3 1.7 fusion.24
  31.0 2.8 %convolution_convert_fusion.1 = bf16[1024,1536]{1,0:T(8,128)(2,1)} fusion(pred[128,1024]{1,0:T(8,128)(4,1)S(1)} %get-tuple-element.5, bf16[128,1536]{1,0:T(8,128)(2,1)S(1)} %get-tuple-element.9, f32[1536]{0:T(1024)S(1)} %copy-done.4, f32[128]{0:T(128)S(1)} %add_rsqrt_fusion.1), kind=kOutput, calls=%fused_computation.7 | convolution fusion | flops 405012480 | bytes 3676672 | tf_op jit(solution)/shard_map/dot_general | solution.py:84
  33.8 7.6 %all-to-all-start.2 = ((bf16[32,32,1536]{2,1,0:T(8,128)(2,1)}), bf16[32,32,1536]{2,1,0:T(8,128)(2,1)}, u32[]{:S(2)}, u32[]{:S(2)}) async-start(bf16[32,32,1536]{2,1,0:T(8,128)(2,1)} %bitcast.43), calls=%async_computation.2 | async-start | bytes 6291456 | tf_op jit(solution)/shard_map/all_to_all | solution.py:88
  41.4 2.7 %convolution_convert_fusion.3 = bf16[1024,1536]{1,0:T(8,128)(2,1)} fusion(pred[128,1024]{1,0:T(8,128)(4,1)S(1)} %get-tuple-element.4, bf16[128,1536]{1,0:T(8,128)(2,1)S(1)} %get-tuple-element.9, f32[1536]{0:T(1024)S(1)} %copy-done.4, f32[128]{0:T(128)S(1)} %add_rsqrt_fusion.1), kind=kOutput, calls=%fused_computation.9 | convolution fusion | flops 405012480 | bytes 3676672 | tf_op jit(solution)/shard_map/dot_general | solution.py:84
  44.1 36.3 %all-to-all-done.2 = bf16[32,32,1536]{2,1,0:T(8,128)(2,1)} async-done(((bf16[32,32,1536]{2,1,0:T(8,128)(2,1)}), bf16[32,32,1536]{2,1,0:T(8,128)(2,1)}, u32[]{:S(2)}, u32[]{:S(2)}) %all-to-all-start.2) | async-done | bytes 3145760 | tf_op jit(solution)/shard_map/all_to_all | solution.py:88
  80.4 5.8 %all-to-all-start = ((bf16[32,32,1536]{2,1,0:T(8,128)(2,1)}), bf16[32,32,1536]{2,1,0:T(8,128)(2,1)}, u32[]{:S(2)}, u32[]{:S(2)}) async-start(bf16[32,32,1536]{2,1,0:T(8,128)(2,1)} %bitcast.42), calls=%async_computation | async-start | bytes 6291456 | tf_op jit(solution)/shard_map/all_to_all | solution.py:88
  86.3 6.4 %fusion.2 = f32[1024,1024]{1,0:T(8,128)S(1)} fusion(bf16[1024,1536]{1,0:T(8,128)(2,1)} %bitcast.12, bf16[2,1536,1024]{2,1,0:T(8,128)(2,1)} %param.19), kind=kOutput, calls=%fused_computation.10 | convolution fusion | flops 3221225472 | bytes 10485760 | tf_op jit(solution)/shard_map/dot_general | solution.py:90
  92.7 3.5 %convolution_convert_fusion = bf16[1024,1536]{1,0:T(8,128)(2,1)} fusion(bf16[2,512,1536]{2,1,0:T(8,128)(2,1)S(1)} %copy-done.7, f32[1024,1024]{1,0:T(8,128)S(1)} %fusion.2), kind=kOutput, calls=%fused_computation.6 | convolution fusion | flops 1615331328 | bytes 8912896 | tf_op jit(solution)/shard_map/dot_general | solution.py:94
  96.2 29.3 %all-to-all-done = bf16[32,32,1536]{2,1,0:T(8,128)(2,1)} async-done(((bf16[32,32,1536]{2,1,0:T(8,128)(2,1)}), bf16[32,32,1536]{2,1,0:T(8,128)(2,1)}, u32[]{:S(2)}, u32[]{:S(2)}) %all-to-all-start) | async-done | bytes 3145760 | tf_op jit(solution)/shard_map/all_to_all | solution.py:88
  125.5 5.8 %all-to-all-start.3 = ((bf16[32,32,1536]{2,1,0:T(8,128)(2,1)}), bf16[32,32,1536]{2,1,0:T(8,128)(2,1)}, u32[]{:S(2)}, u32[]{:S(2)}) async-start(bf16[32,32,1536]{2,1,0:T(8,128)(2,1)} %bitcast.47), calls=%async_computation.3 | async-start | bytes 6291456 | tf_op jit(solution)/shard_map/all_to_all | solution.py:98
  131.3 6.4 %fusion.4 = f32[1024,1024]{1,0:T(8,128)S(1)} fusion(bf16[1024,1536]{1,0:T(8,128)(2,1)} %bitcast.6, bf16[2,1536,1024]{2,1,0:T(8,128)(2,1)} %param.19), kind=kOutput, calls=%fused_computation.12 | convolution fusion | flops 3221225472 | bytes 10485760 | tf_op jit(solution)/shard_map/dot_general | solution.py:90
  137.7 3.5 %convolution_convert_fusion.2 = bf16[1024,1536]{1,0:T(8,128)(2,1)} fusion(bf16[2,512,1536]{2,1,0:T(8,128)(2,1)S(1)} %copy-done.8, f32[1024,1024]{1,0:T(8,128)S(1)} %fusion.4), kind=kOutput, calls=%fused_computation.8 | convolution fusion | flops 1615331328 | bytes 8912896 | tf_op jit(solution)/shard_map/dot_general | solution.py:94
  141.1 29.4 %all-to-all-done.3 = bf16[32,32,1536]{2,1,0:T(8,128)(2,1)} async-done(((bf16[32,32,1536]{2,1,0:T(8,128)(2,1)}), bf16[32,32,1536]{2,1,0:T(8,128)(2,1)}, u32[]{:S(2)}, u32[]{:S(2)}) %all-to-all-start.3) | async-done | bytes 3145760 | tf_op jit(solution)/shard_map/all_to_all | solution.py:98
  170.6 5.8 %all-to-all-start.1 = ((bf16[32,32,1536]{2,1,0:T(8,128)(2,1)}), bf16[32,32,1536]{2,1,0:T(8,128)(2,1)}, u32[]{:S(2)}, u32[]{:S(2)}) async-start(bf16[32,32,1536]{2,1,0:T(8,128)(2,1)} %bitcast.46), calls=%async_computation.1 | async-start | bytes 6291456 | tf_op jit(solution)/shard_map/all_to_all | solution.py:98
  176.4 0.3 fusion.60
  176.9 2.7 %fusion = (f32[128,1024]{1,0:T(8,128)S(1)}, f32[128,1024]{1,0:T(8,128)S(1)}) fusion(f32[128,8]{1,0:T(8,128)S(1)} %copy.17, s32[1024]{0:T(1024)S(1)} %get-tuple-element.16, s32[128,8]{1,0:T(8,128)S(1)} %copy.16, s32[1024]{0:T(1024)S(1)} %get-tuple-element.15), kind=kLoop, calls=%fused_computation.4 | loop fusion | flops 6029312 | bytes 1064960 | tf_op jit(solution)/shard_map/reduce_sum | solution.py:100
  179.6 2.5 %fusion.33 = f32[128,1536]{1,0:T(8,128)S(1)} fusion(bf16[1024,1536]{1,0:T(8,128)(2,1)} %bitcast.16, f32[128,1024]{1,0:T(8,128)S(1)} %get-tuple-element.3), kind=kOutput, calls=%fused_computation.59 | convolution fusion | flops 402784256 | bytes 4456448 | tf_op jit(solution)/shard_map/dot_general | solution.py:104
  182.1 3.4 %convolution_add_fusion = f32[128,1536]{1,0:T(8,128)} fusion(f32[128,1536]{1,0:T(8,128)S(1)} %fusion.33, bf16[1024,1536]{1,0:T(8,128)(2,1)} %bitcast.16, f32[128,1024]{1,0:T(8,128)S(1)} %get-tuple-element.3), kind=kOutput, calls=%fused_computation.17 | convolution fusion | flops 403374080 | bytes 5242880 | tf_op jit(solution)/shard_map/dot_general | solution.py:105
  185.5 30.2 %all-to-all-done.1 = bf16[32,32,1536]{2,1,0:T(8,128)(2,1)} async-done(((bf16[32,32,1536]{2,1,0:T(8,128)(2,1)}), bf16[32,32,1536]{2,1,0:T(8,128)(2,1)}, u32[]{:S(2)}, u32[]{:S(2)}) %all-to-all-start.1) | async-done | bytes 3145760 | tf_op jit(solution)/shard_map/all_to_all | solution.py:98
  215.7 2.5 %fusion.36 = f32[128,1536]{1,0:T(8,128)S(1)} fusion(bf16[1024,1536]{1,0:T(8,128)(2,1)} %bitcast.10, f32[128,1024]{1,0:T(8,128)S(1)} %get-tuple-element.2), kind=kOutput, calls=%fused_computation.62 | convolution fusion | flops 402784256 | bytes 4456448 | tf_op jit(solution)/shard_map/dot_general | solution.py:104
  218.2 2.7 %fusion.21 = (f32[128]{0:T(128)S(1)}, bf16[128,1536]{1,0:T(8,128)(2,1)S(1)}) fusion(f32[128,1536]{1,0:T(8,128)S(1)} %copy-done.1, f32[128,1536]{1,0:T(8,128)S(1)} %fusion.36, bf16[1024,1536]{1,0:T(8,128)(2,1)} %bitcast.10, f32[128,1024]{1,0:T(8,128)S(1)} %get-tuple-element.2, bf16[128,1536]{1,0:T(8,128)(2,1)S(1)} %get-tuple-element.9), kind=kOutput, calls=%fused_computation.37 | convolution fusion | flops 404750208 | bytes 6029824 | tf_op jit(solution)/shard_map/dot_general | solution.py:105
  220.9 0.9 fusion.23
  (41 shorter events, 1.3 us)
Async XLA Ops:
  0.6 1.3 copy-start
  0.6 9.6 %copy-start.6 = (s32[64]{0:T(128)S(1)}, s32[64]{0:T(128)}, u32[]{:S(2)}) copy-start(s32[64]{0:T(128)} %param.18) | copy-start | bytes 772
  0.7 9.9 %copy-start.3 = (s32[128,8]{0,1:T(8,128)S(1)}, s32[128,8]{0,1:T(8,128)}, u32[]{:S(2)}) copy-start(s32[128,8]{0,1:T(8,128)} %param.16) | copy-start | bytes 12292
  0.7 10.1 %copy-start.10 = (s32[32]{0:T(128)S(1)}, s32[32]{0:T(128)}, u32[]{:S(2)}) copy-start(s32[32]{0:T(128)} %param.17) | copy-start | bytes 388
  3.9 27.1 %copy-start.4 = (f32[1536]{0:T(1024)S(1)}, f32[1536]{0:T(1024)}, u32[]{:S(2)}) copy-start(f32[1536]{0:T(1024)} %param.14) | copy-start | bytes 18436
  4.9 21.2 %collective-permute-start.2 = (bf16[128,1536]{1,0:T(8,128)(2,1)}, bf16[128,1536]{1,0:T(8,128)(2,1)}, u32[]{:S(2)}, u32[]{:S(2)}) collective-permute-start(bf16[128,1536]{1,0:T(8,128)(2,1)} %get-tuple-element.11), channel_id=1, source_target_pairs={{0,3},{1,0},{2,1},{3,2},{4,7},{5,4},{6,5},{7,6},{8,11},{9,8},{10,9... | collective-permute-start | bytes 1179656 | tf_op jit(solution)/shard_map/ppermute | solution.py:58
  8.9 17.1 %collective-permute-start.1 = (bf16[128,1536]{1,0:T(8,128)(2,1)}, bf16[128,1536]{1,0:T(8,128)(2,1)}, u32[]{:S(2)}, u32[]{:S(2)}) collective-permute-start(bf16[128,1536]{1,0:T(8,128)(2,1)} %get-tuple-element.12), channel_id=1, source_target_pairs={{0,2},{1,3},{2,0},{3,1},{4,6},{5,7},{6,4},{7,5},{8,10},{9,11},{10,... | collective-permute-start | bytes 1179656 | tf_op jit(solution)/shard_map/ppermute | solution.py:58
  8.9 20.3 %collective-permute-start = (bf16[128,1536]{1,0:T(8,128)(2,1)S(1)}, bf16[128,1536]{1,0:T(8,128)(2,1)}, u32[]{:S(2)}, u32[]{:S(2)}) collective-permute-start(bf16[128,1536]{1,0:T(8,128)(2,1)S(1)} %get-tuple-element.10), channel_id=1, source_target_pairs={{0,1},{1,2},{2,3},{3,0},{4,5},{5,6},{6,7},{7,4},{8,9},{9,10},{10,1... | collective-permute-start | bytes 1179656 | tf_op jit(solution)/shard_map/ppermute | solution.py:58
  33.8 46.6 %all-to-all-start.2 = ((bf16[32,32,1536]{2,1,0:T(8,128)(2,1)}), bf16[32,32,1536]{2,1,0:T(8,128)(2,1)}, u32[]{:S(2)}, u32[]{:S(2)}) async-start(bf16[32,32,1536]{2,1,0:T(8,128)(2,1)} %bitcast.43), calls=%async_computation.2 | async-start | bytes 6291456 | tf_op jit(solution)/shard_map/all_to_all | solution.py:88
  80.4 45.0 %all-to-all-start = ((bf16[32,32,1536]{2,1,0:T(8,128)(2,1)}), bf16[32,32,1536]{2,1,0:T(8,128)(2,1)}, u32[]{:S(2)}, u32[]{:S(2)}) async-start(bf16[32,32,1536]{2,1,0:T(8,128)(2,1)} %bitcast.42), calls=%async_computation | async-start | bytes 6291456 | tf_op jit(solution)/shard_map/all_to_all | solution.py:88
  86.3 6.4 %copy-start.7 = (bf16[2,512,1536]{2,1,0:T(8,128)(2,1)S(1)}, bf16[2,512,1536]{2,1,0:T(8,128)(2,1)}, u32[]{:S(2)}) copy-start(bf16[2,512,1536]{2,1,0:T(8,128)(2,1)} %param.20) | copy-start | bytes 9437188
  125.5 45.1 %all-to-all-start.3 = ((bf16[32,32,1536]{2,1,0:T(8,128)(2,1)}), bf16[32,32,1536]{2,1,0:T(8,128)(2,1)}, u32[]{:S(2)}, u32[]{:S(2)}) async-start(bf16[32,32,1536]{2,1,0:T(8,128)(2,1)} %bitcast.47), calls=%async_computation.3 | async-start | bytes 6291456 | tf_op jit(solution)/shard_map/all_to_all | solution.py:98
  131.3 6.4 %copy-start.8 = (bf16[2,512,1536]{2,1,0:T(8,128)(2,1)S(1)}, bf16[2,512,1536]{2,1,0:T(8,128)(2,1)}, u32[]{:S(2)}) copy-start(bf16[2,512,1536]{2,1,0:T(8,128)(2,1)} %param.20) | copy-start | bytes 9437188
  170.6 5.8 %copy-start.9 = (bf16[1536,40]{0,1:T(8,128)(2,1)S(1)}, bf16[1536,40]{0,1:T(8,128)(2,1)}, u32[]{:S(2)}) copy-start(bf16[1536,40]{0,1:T(8,128)(2,1)} %param.15) | copy-start | bytes 368644
  170.6 45.1 %all-to-all-start.1 = ((bf16[32,32,1536]{2,1,0:T(8,128)(2,1)}), bf16[32,32,1536]{2,1,0:T(8,128)(2,1)}, u32[]{:S(2)}, u32[]{:S(2)}) async-start(bf16[32,32,1536]{2,1,0:T(8,128)(2,1)} %bitcast.46), calls=%async_computation.1 | async-start | bytes 6291456 | tf_op jit(solution)/shard_map/all_to_all | solution.py:98
  185.5 32.7 %copy-start.1 = (f32[128,1536]{1,0:T(8,128)S(1)}, f32[128,1536]{1,0:T(8,128)}, u32[]{:S(2)}) copy-start(f32[128,1536]{1,0:T(8,128)} %convolution_add_fusion) | copy-start | bytes 2359300
  218.2 2.7 %copy-start.5 = (f32[1536]{0:T(1024)S(1)}, f32[1536]{0:T(1024)}, u32[]{:S(2)}) copy-start(f32[1536]{0:T(1024)} %param.21) | copy-start | bytes 18436
  220.9 0.9 copy-start.2

commit v4 on v3

--- a/solution.py
+++ b/solution.py
@@ -49,13 +49,25 @@
     slot_total = slot_expert.shape[0]
     capacity = slot_total * DEPTH
     tp_total = lax.axis_size("tp")
-    partial = jnp.dot(context, attn_weight, preferred_element_type=jnp.float32).astype(jnp.bfloat16)
-    blocks = partial.reshape(tp_total, row_count, width)
-    attn_out = blocks[tp_rank].astype(jnp.float32)
-    for shift in range(1, tp_total):
-        sent = blocks[(tp_rank + shift) % tp_total]
-        pairs = [(j, (j + shift) % tp_total) for j in range(tp_total)]
-        attn_out = attn_out + lax.ppermute(sent, "tp", pairs).astype(jnp.float32)
+    half = row_count // 2
+
+    def block_for(shift):
+        rows = lax.dynamic_slice_in_dim(context, ((tp_rank + shift) % tp_total) * row_count, row_count)
+        return jnp.dot(rows, attn_weight, preferred_element_type=jnp.float32).astype(jnp.bfloat16)
+
+    up = [(j, (j + 1) % tp_total) for j in range(tp_total)]
+    down = [(j, (j - 1) % tp_total) for j in range(tp_total)]
+    far = block_for(2)
+    from_below = lax.ppermute(jnp.concatenate([block_for(1), far[:half]]), "tp", up)
+    from_above = lax.ppermute(jnp.concatenate([block_for(3), far[half:]]), "tp", down)
+    relayed_up = lax.ppermute(from_below[row_count:], "tp", up)
+    relayed_down = lax.ppermute(from_above[row_count:], "tp", down)
+    attn_out = (
+        block_for(0).astype(jnp.float32)
+        + from_below[:row_count].astype(jnp.float32)
+        + from_above[:row_count].astype(jnp.float32)
+        + jnp.concatenate([relayed_up, relayed_down]).astype(jnp.float32)
+    )
     stream = (residual.astype(jnp.float32) + attn_out).astype(jnp.bfloat16)
     normed = rms_norm(stream, gain_first)
     logits = jnp.dot(normed, router, preferred_element_type=jnp.float32)

time: 224 us -> 229 us (1.022)
  starting transfers between devices: 30.3 us -> 33.1 us
    ppermute x3 -> x4, starting transfers between devices: 5.3 us -> 8.12 us  [the longest x1 4.1 us: shards(): lax.ppermute(jnp.concatenate([block_for(3), far[half:]]), 'tp', down)]
    dot_general x1 -> x4, matrix products: 1.97 us -> 4.68 us  [block_for(): jnp.dot(rows, attn_weight, preferred_element_type=jnp.float32)]
    ppermute x3 -> x4, waiting for transfers between devices: 12.7 us -> 12.6 us  [the longest x1 9.65 us: shards(): lax.ppermute(jnp.concatenate([block_for(3), far[half:]]), 'tp', down)]
  transfers between devices with their start and end apart: 7 -> 8, of which waited for: 6 -> 6; matrix products, arithmetic and copies ran while one was open for 17% -> 17% of each run, Pallas kernels for 0% -> 0%
where the time goes in v4:
time: 229 us; the launch traced here: 227 us
  waiting for transfers between devices  139 us (61%)
  matrix products  40.6 us (18%)
  starting transfers between devices  33.1 us (14%)
  other arithmetic  9.75 us (4%)
  local copies, waits for them, and re-layouts  3.4 us (1%)
    all_to_all x2, waiting for transfers between devices, shards(): lax.all_to_all(outgoing, 'tok', split_axis=0, concat_axis=0, tiled=True)  65.6 us
    all_to_all x2, waiting for transfers between devices, shards(): lax.all_to_all(computed, 'tok', split_axis=0, concat_axis=0, tiled=True)  60.5 us
    all_to_all x2, starting transfers between devices, shards(): lax.all_to_all(outgoing, 'tok', split_axis=0, concat_axis=0, tiled=True)  13.4 us
    dot_general x2, matrix products, shards(): hidden = jnp.dot(arrived, w_in[local], preferred_element_type=jnp.float32)  12.8 us
    all_to_all x2, starting transfers between devices, shards(): lax.all_to_all(computed, 'tok', split_axis=0, concat_axis=0, tiled=True)  11.6 us
    ppermute x1, waiting for transfers between devices, shards(): lax.ppermute(jnp.concatenate([block_for(3), far[half:]]), 'tp', down)  9.65 us
    dot_general x2, matrix products, shards(): jnp.dot(activated, w_out[local], preferred_element_type=jnp.float32)  7.04 us
    dot_general x2, matrix products, shards(): lax.dot_general(dispatch, normed, (((0,), (0,)), ((), ())), preferred_ele...  5.52 us
  transfers between devices with their start and end apart: 8, of which 6 were waited for; matrix products, arithmetic and copies ran while one was open for 17% of the time, Pallas kernels for 0%

profile of v4, /device:TPU:8, one launch (start us, length us, event | category | flops | bytes accessed | tf_op | source)
XLA Modules:
  0.0 226.6 jit_solution(2721040395968220449)
XLA Ops:
  0.7 1.2 copy-done
  1.9 1.3 convolution_convert_fusion.5
  3.3 1.3 convolution_convert_fusion.4
  4.6 4.1 %collective-permute-start.1 = (bf16[192,1536]{1,0:T(8,128)(2,1)S(1)}, bf16[192,1536]{1,0:T(8,128)(2,1)}, u32[]{:S(2)}, u32[]{:S(2)}) collective-permute-start(bf16[192,1536]{1,0:T(8,128)(2,1)S(1)} %pad_maximum_fusion.1), channel_id=1, source_target_pairs={{0,3},{1,0},{2,1},{3,2},{4,7},{5,4},{6,5},{7,6},{8,11},{9,8},{10,9... | collective-permute-start | bytes 1769480 | tf_op jit(solution)/shard_map/ppermute | solution.py:62
  10.0 0.7 add_compare_fusion.1
  11.6 9.7 %collective-permute-done.1 = bf16[192,1536]{1,0:T(8,128)(2,1)} collective-permute-done((bf16[192,1536]{1,0:T(8,128)(2,1)S(1)}, bf16[192,1536]{1,0:T(8,128)(2,1)}, u32[]{:S(2)}, u32[]{:S(2)}) %collective-permute-start.1) | collective-permute-done | bytes 589856 | tf_op jit(solution)/shard_map/ppermute | solution.py:62
  21.3 0.9 slice.61
  22.2 3.9 %collective-permute-start.3 = (bf16[64,1536]{1,0:T(8,128)(2,1)S(1)}, bf16[64,1536]{1,0:T(8,128)(2,1)S(1)}, u32[]{:S(2)}, u32[]{:S(2)}) collective-permute-start(bf16[64,1536]{1,0:T(8,128)(2,1)S(1)} %slice.61), channel_id=1, source_target_pairs={{0,3},{1,0},{2,1},{3,2},{4,7},{5,4},{6,5},{7,6},{8,11},{9,8},{10,9... | collective-permute-start | bytes 589832 | tf_op jit(solution)/shard_map/ppermute | solution.py:64
  26.1 0.9 slice.60
  27.1 3.9 %compare_reduce_fusion.1 = (pred[128,1024]{1,0:T(8,128)(4,1)S(1)}, pred[128,1024]{1,0:T(8,128)(4,1)S(1)}) fusion(s32[1024]{0:T(1024)S(1)} %get-tuple-element.15, s32[128,8]{1,0:T(8,128)S(1)} %copy.16, s32[1024]{0:T(1024)S(1)} %get-tuple-element.14), kind=kLoop, calls=%fused_computation.2 | loop fusion | flops 3932160 | bytes 274432 | tf_op jit(solution)/shard_map/reduce_or | solution.py:95
  31.0 3.0 %collective-permute-done.2 = bf16[64,1536]{1,0:T(8,128)(2,1)S(1)} collective-permute-done((bf16[64,1536]{1,0:T(8,128)(2,1)S(1)}, bf16[64,1536]{1,0:T(8,128)(2,1)S(1)}, u32[]{:S(2)}, u32[]{:S(2)}) %collective-permute-start.2) | collective-permute-done | bytes 196640 | tf_op jit(solution)/shard_map/ppermute | solution.py:63
  34.0 1.8 fusion.25
  35.8 2.7 %convolution_convert_fusion.1 = bf16[1024,1536]{1,0:T(8,128)(2,1)} fusion(pred[128,1024]{1,0:T(8,128)(4,1)S(1)} %get-tuple-element.5, bf16[128,1536]{1,0:T(8,128)(2,1)S(1)} %get-tuple-element.11, f32[1536]{0:T(1024)S(1)} %copy-done.4, f32[128]{0:T(128)S(1)} %add_rsqrt_fusion.1), kind=kOutput, calls=%fused_computation.7 | convolution fusion | flops 405012480 | bytes 3676672 | tf_op jit(solution)/shard_map/dot_general | solution.py:96
  38.5 7.6 %all-to-all-start.2 = ((bf16[32,32,1536]{2,1,0:T(8,128)(2,1)}), bf16[32,32,1536]{2,1,0:T(8,128)(2,1)}, u32[]{:S(2)}, u32[]{:S(2)}) async-start(bf16[32,32,1536]{2,1,0:T(8,128)(2,1)} %bitcast.34), calls=%async_computation.2 | async-start | bytes 6291456 | tf_op jit(solution)/shard_map/all_to_all | solution.py:100
  46.1 2.8 %convolution_convert_fusion.3 = bf16[1024,1536]{1,0:T(8,128)(2,1)} fusion(pred[128,1024]{1,0:T(8,128)(4,1)S(1)} %get-tuple-element.4, bf16[128,1536]{1,0:T(8,128)(2,1)S(1)} %get-tuple-element.11, f32[1536]{0:T(1024)S(1)} %copy-done.4, f32[128]{0:T(128)S(1)} %add_rsqrt_fusion.1), kind=kOutput, calls=%fused_computation.9 | convolution fusion | flops 405012480 | bytes 3676672 | tf_op jit(solution)/shard_map/dot_general | solution.py:96
  48.9 36.3 %all-to-all-done.2 = bf16[32,32,1536]{2,1,0:T(8,128)(2,1)} async-done(((bf16[32,32,1536]{2,1,0:T(8,128)(2,1)}), bf16[32,32,1536]{2,1,0:T(8,128)(2,1)}, u32[]{:S(2)}, u32[]{:S(2)}) %all-to-all-start.2) | async-done | bytes 3145760 | tf_op jit(solution)/shard_map/all_to_all | solution.py:100
  85.2 5.8 %all-to-all-start = ((bf16[32,32,1536]{2,1,0:T(8,128)(2,1)}), bf16[32,32,1536]{2,1,0:T(8,128)(2,1)}, u32[]{:S(2)}, u32[]{:S(2)}) async-start(bf16[32,32,1536]{2,1,0:T(8,128)(2,1)} %bitcast.33), calls=%async_computation | async-start | bytes 6291456 | tf_op jit(solution)/shard_map/all_to_all | solution.py:100
  91.0 6.4 %fusion.2 = f32[1024,1024]{1,0:T(8,128)S(1)} fusion(bf16[1024,1536]{1,0:T(8,128)(2,1)} %bitcast.7, bf16[2,1536,1024]{2,1,0:T(8,128)(2,1)} %param.19), kind=kOutput, calls=%fused_computation.10 | convolution fusion | flops 3221225472 | bytes 10485760 | tf_op jit(solution)/shard_map/dot_general | solution.py:102
  97.4 3.5 %convolution_convert_fusion = bf16[1024,1536]{1,0:T(8,128)(2,1)} fusion(bf16[2,512,1536]{2,1,0:T(8,128)(2,1)S(1)} %copy-done.7, f32[1024,1024]{1,0:T(8,128)S(1)} %fusion.2), kind=kOutput, calls=%fused_computation.6 | convolution fusion | flops 1615331328 | bytes 8912896 | tf_op jit(solution)/shard_map/dot_general | solution.py:106
  100.9 29.3 %all-to-all-done = bf16[32,32,1536]{2,1,0:T(8,128)(2,1)} async-done(((bf16[32,32,1536]{2,1,0:T(8,128)(2,1)}), bf16[32,32,1536]{2,1,0:T(8,128)(2,1)}, u32[]{:S(2)}, u32[]{:S(2)}) %all-to-all-start) | async-done | bytes 3145760 | tf_op jit(solution)/shard_map/all_to_all | solution.py:100
  130.2 5.8 %all-to-all-start.3 = ((bf16[32,32,1536]{2,1,0:T(8,128)(2,1)}), bf16[32,32,1536]{2,1,0:T(8,128)(2,1)}, u32[]{:S(2)}, u32[]{:S(2)}) async-start(bf16[32,32,1536]{2,1,0:T(8,128)(2,1)} %bitcast.36), calls=%async_computation.3 | async-start | bytes 6291456 | tf_op jit(solution)/shard_map/all_to_all | solution.py:110
  136.0 6.4 %fusion.4 = f32[1024,1024]{1,0:T(8,128)S(1)} fusion(bf16[1024,1536]{1,0:T(8,128)(2,1)} %bitcast.1, bf16[2,1536,1024]{2,1,0:T(8,128)(2,1)} %param.19), kind=kOutput, calls=%fused_computation.12 | convolution fusion | flops 3221225472 | bytes 10485760 | tf_op jit(solution)/shard_map/dot_general | solution.py:102
  142.4 3.5 %convolution_convert_fusion.2 = bf16[1024,1536]{1,0:T(8,128)(2,1)} fusion(bf16[2,512,1536]{2,1,0:T(8,128)(2,1)S(1)} %copy-done.8, f32[1024,1024]{1,0:T(8,128)S(1)} %fusion.4), kind=kOutput, calls=%fused_computation.8 | convolution fusion | flops 1615331328 | bytes 8912896 | tf_op jit(solution)/shard_map/dot_general | solution.py:106
  145.9 29.4 %all-to-all-done.3 = bf16[32,32,1536]{2,1,0:T(8,128)(2,1)} async-done(((bf16[32,32,1536]{2,1,0:T(8,128)(2,1)}), bf16[32,32,1536]{2,1,0:T(8,128)(2,1)}, u32[]{:S(2)}, u32[]{:S(2)}) %all-to-all-start.3) | async-done | bytes 3145760 | tf_op jit(solution)/shard_map/all_to_all | solution.py:110
  175.3 5.8 %all-to-all-start.1 = ((bf16[32,32,1536]{2,1,0:T(8,128)(2,1)}), bf16[32,32,1536]{2,1,0:T(8,128)(2,1)}, u32[]{:S(2)}, u32[]{:S(2)}) async-start(bf16[32,32,1536]{2,1,0:T(8,128)(2,1)} %bitcast.35), calls=%async_computation.1 | async-start | bytes 6291456 | tf_op jit(solution)/shard_map/all_to_all | solution.py:110
  181.6 2.7 %fusion = (f32[128,1024]{1,0:T(8,128)S(1)}, f32[128,1024]{1,0:T(8,128)S(1)}) fusion(f32[128,8]{1,0:T(8,128)S(1)} %copy.17, s32[1024]{0:T(1024)S(1)} %get-tuple-element.15, s32[128,8]{1,0:T(8,128)S(1)} %copy.16, s32[1024]{0:T(1024)S(1)} %get-tuple-element.14), kind=kLoop, calls=%fused_computation.4 | loop fusion | flops 6029312 | bytes 1064960 | tf_op jit(solution)/shard_map/reduce_sum | solution.py:112
  184.3 2.5 %fusion.30 = f32[128,1536]{1,0:T(8,128)S(1)} fusion(bf16[1024,1536]{1,0:T(8,128)(2,1)} %bitcast.11, f32[128,1024]{1,0:T(8,128)S(1)} %get-tuple-element.3), kind=kOutput, calls=%fused_computation.58 | convolution fusion | flops 402784256 | bytes 4456448 | tf_op jit(solution)/shard_map/dot_general | solution.py:116
  186.8 2.5 %convolution_add_fusion = f32[128,1536]{1,0:T(8,128)S(1)} fusion(f32[128,1536]{1,0:T(8,128)S(1)} %fusion.30, bf16[1024,1536]{1,0:T(8,128)(2,1)} %bitcast.11, f32[128,1024]{1,0:T(8,128)S(1)} %get-tuple-element.3), kind=kOutput, calls=%fused_computation.16 | convolution fusion | flops 403374080 | bytes 5242880 | tf_op jit(solution)/shard_map/dot_general | solution.py:117
  189.3 31.1 %all-to-all-done.1 = bf16[32,32,1536]{2,1,0:T(8,128)(2,1)} async-done(((bf16[32,32,1536]{2,1,0:T(8,128)(2,1)}), bf16[32,32,1536]{2,1,0:T(8,128)(2,1)}, u32[]{:S(2)}, u32[]{:S(2)}) %all-to-all-start.1) | async-done | bytes 3145760 | tf_op jit(solution)/shard_map/all_to_all | solution.py:110
  220.4 2.5 %fusion.33 = f32[128,1536]{1,0:T(8,128)S(1)} fusion(bf16[1024,1536]{1,0:T(8,128)(2,1)} %bitcast.5, f32[128,1024]{1,0:T(8,128)S(1)} %get-tuple-element.2), kind=kOutput, calls=%fused_computation.61 | convolution fusion | flops 402784256 | bytes 4456448 | tf_op jit(solution)/shard_map/dot_general | solution.py:116
  222.9 2.7 %fusion.22 = (f32[128]{0:T(128)S(1)}, bf16[128,1536]{1,0:T(8,128)(2,1)S(1)}) fusion(f32[128,1536]{1,0:T(8,128)S(1)} %convolution_add_fusion, f32[128,1536]{1,0:T(8,128)S(1)} %fusion.33, bf16[1024,1536]{1,0:T(8,128)(2,1)} %bitcast.5, f32[128,1024]{1,0:T(8,128)S(1)} %get-tuple-element.2, bf16[128,1536]{1,0:T(8,128)(2,1)S(1)} %get-tuple-element.11), kind=kOutput, calls=%fused_computation.41 | convolution fusion | flops 404750208 | bytes 6029824 | tf_op jit(solution)/shard_map/dot_general | solution.py:117
  225.7 0.9 fusion.24
  (49 shorter events, 2.9 us)
Async XLA Ops:
  0.6 1.3 copy-start
  0.6 8.0 %copy-start.2 = (bf16[512,384]{1,0:T(8,128)(2,1)S(1)}, bf16[512,384]{1,0:T(8,128)(2,1)}, u32[]{:S(2)}) copy-start(bf16[512,384]{1,0:T(8,128)(2,1)} %param.11) | copy-start | bytes 1179652
  3.2 6.0 %copy-start.6 = (s32[64]{0:T(128)S(1)}, s32[64]{0:T(128)}, u32[]{:S(2)}) copy-start(s32[64]{0:T(128)} %param.18) | copy-start | bytes 772
  3.2 6.1 %copy-start.3 = (s32[128,8]{0,1:T(8,128)S(1)}, s32[128,8]{0,1:T(8,128)}, u32[]{:S(2)}) copy-start(s32[128,8]{0,1:T(8,128)} %param.16) | copy-start | bytes 12292
  3.2 6.2 %copy-start.10 = (s32[32]{0:T(128)S(1)}, s32[32]{0:T(128)}, u32[]{:S(2)}) copy-start(s32[32]{0:T(128)} %param.17) | copy-start | bytes 388
  4.6 16.7 %collective-permute-start.1 = (bf16[192,1536]{1,0:T(8,128)(2,1)S(1)}, bf16[192,1536]{1,0:T(8,128)(2,1)}, u32[]{:S(2)}, u32[]{:S(2)}) collective-permute-start(bf16[192,1536]{1,0:T(8,128)(2,1)S(1)} %pad_maximum_fusion.1), channel_id=1, source_target_pairs={{0,3},{1,0},{2,1},{3,2},{4,7},{5,4},{6,5},{7,6},{8,11},{9,8},{10,9... | collective-permute-start | bytes 1769480 | tf_op jit(solution)/shard_map/ppermute | solution.py:62
  9.1 26.7 %copy-start.4 = (f32[1536]{0:T(1024)S(1)}, f32[1536]{0:T(1024)}, u32[]{:S(2)}) copy-start(f32[1536]{0:T(1024)} %param.14) | copy-start | bytes 18436
  9.1 17.0 %collective-permute-start = (bf16[192,1536]{1,0:T(8,128)(2,1)S(1)}, bf16[192,1536]{1,0:T(8,128)(2,1)}, u32[]{:S(2)}, u32[]{:S(2)}) collective-permute-start(bf16[192,1536]{1,0:T(8,128)(2,1)S(1)} %pad_maximum_fusion), channel_id=1, source_target_pairs={{0,1},{1,2},{2,3},{3,0},{4,5},{5,6},{6,7},{7,4},{8,9},{9,10},{10,1... | collective-permute-start | bytes 1769480 | tf_op jit(solution)/shard_map/ppermute | solution.py:61
  22.2 8.8 %collective-permute-start.3 = (bf16[64,1536]{1,0:T(8,128)(2,1)S(1)}, bf16[64,1536]{1,0:T(8,128)(2,1)S(1)}, u32[]{:S(2)}, u32[]{:S(2)}) collective-permute-start(bf16[64,1536]{1,0:T(8,128)(2,1)S(1)} %slice.61), channel_id=1, source_target_pairs={{0,3},{1,0},{2,1},{3,2},{4,7},{5,4},{6,5},{7,6},{8,11},{9,8},{10,9... | collective-permute-start | bytes 589832 | tf_op jit(solution)/shard_map/ppermute | solution.py:64
  27.0 7.0 %collective-permute-start.2 = (bf16[64,1536]{1,0:T(8,128)(2,1)S(1)}, bf16[64,1536]{1,0:T(8,128)(2,1)S(1)}, u32[]{:S(2)}, u32[]{:S(2)}) collective-permute-start(bf16[64,1536]{1,0:T(8,128)(2,1)S(1)} %slice.60), channel_id=1, source_target_pairs={{0,1},{1,2},{2,3},{3,0},{4,5},{5,6},{6,7},{7,4},{8,9},{9,10},{10,1... | collective-permute-start | bytes 589832 | tf_op jit(solution)/shard_map/ppermute | solution.py:63
  38.5 46.6 %all-to-all-start.2 = ((bf16[32,32,1536]{2,1,0:T(8,128)(2,1)}), bf16[32,32,1536]{2,1,0:T(8,128)(2,1)}, u32[]{:S(2)}, u32[]{:S(2)}) async-start(bf16[32,32,1536]{2,1,0:T(8,128)(2,1)} %bitcast.34), calls=%async_computation.2 | async-start | bytes 6291456 | tf_op jit(solution)/shard_map/all_to_all | solution.py:100
  85.2 45.0 %all-to-all-start = ((bf16[32,32,1536]{2,1,0:T(8,128)(2,1)}), bf16[32,32,1536]{2,1,0:T(8,128)(2,1)}, u32[]{:S(2)}, u32[]{:S(2)}) async-start(bf16[32,32,1536]{2,1,0:T(8,128)(2,1)} %bitcast.33), calls=%async_computation | async-start | bytes 6291456 | tf_op jit(solution)/shard_map/all_to_all | solution.py:100
  91.0 6.4 %copy-start.7 = (bf16[2,512,1536]{2,1,0:T(8,128)(2,1)S(1)}, bf16[2,512,1536]{2,1,0:T(8,128)(2,1)}, u32[]{:S(2)}) copy-start(bf16[2,512,1536]{2,1,0:T(8,128)(2,1)} %param.20) | copy-start | bytes 9437188
  130.2 45.1 %all-to-all-start.3 = ((bf16[32,32,1536]{2,1,0:T(8,128)(2,1)}), bf16[32,32,1536]{2,1,0:T(8,128)(2,1)}, u32[]{:S(2)}, u32[]{:S(2)}) async-start(bf16[32,32,1536]{2,1,0:T(8,128)(2,1)} %bitcast.36), calls=%async_computation.3 | async-start | bytes 6291456 | tf_op jit(solution)/shard_map/all_to_all | solution.py:110
  136.0 6.4 %copy-start.8 = (bf16[2,512,1536]{2,1,0:T(8,128)(2,1)S(1)}, bf16[2,512,1536]{2,1,0:T(8,128)(2,1)}, u32[]{:S(2)}) copy-start(bf16[2,512,1536]{2,1,0:T(8,128)(2,1)} %param.20) | copy-start | bytes 9437188
  175.3 5.8 %copy-start.9 = (bf16[1536,40]{0,1:T(8,128)(2,1)S(1)}, bf16[1536,40]{0,1:T(8,128)(2,1)}, u32[]{:S(2)}) copy-start(bf16[1536,40]{0,1:T(8,128)(2,1)} %param.15) | copy-start | bytes 368644
  175.3 45.1 %all-to-all-start.1 = ((bf16[32,32,1536]{2,1,0:T(8,128)(2,1)}), bf16[32,32,1536]{2,1,0:T(8,128)(2,1)}, u32[]{:S(2)}, u32[]{:S(2)}) async-start(bf16[32,32,1536]{2,1,0:T(8,128)(2,1)} %bitcast.35), calls=%async_computation.1 | async-start | bytes 6291456 | tf_op jit(solution)/shard_map/all_to_all | solution.py:110
  222.9 2.7 %copy-start.5 = (f32[1536]{0:T(1024)S(1)}, f32[1536]{0:T(1024)}, u32[]{:S(2)}) copy-start(f32[1536]{0:T(1024)} %param.21) | copy-start | bytes 18436
  225.6 0.9 copy-start.1

commit v5 on v3

--- a/solution.py
+++ b/solution.py
@@ -75,19 +75,20 @@
     position = jnp.sum(jnp.where(chooser, earlier[:, None, :], 0), axis=-1)
     target = jnp.where(live_rows[:, None], slot_of * DEPTH + position, capacity)
     gate_live = jnp.where(live_rows[:, None], gate_probs, jnp.float32(0.0))
-    column = jnp.arange(tok_total * DEPTH, dtype=jnp.int32)
+    picks = target[:, :, None] == jnp.arange(capacity, dtype=jnp.int32)[None, None, :]
+    dispatch = jnp.any(picks, axis=1).astype(jnp.bfloat16)
+    outgoing = lax.dot_general(
+        dispatch, normed, (((0,), (0,)), ((), ())), preferred_element_type=jnp.float32
+    ).astype(jnp.bfloat16)
+    outgoing = outgoing.reshape(tok_total, local_slots * DEPTH, width)
+    arrived = lax.all_to_all(outgoing, "tok", split_axis=0, concat_axis=0, tiled=True)
+    arrived = arrived.reshape(tok_total, local_slots, DEPTH, width)
+    combine_all = jnp.sum(jnp.where(picks, gate_live[:, :, None], jnp.float32(0.0)), axis=1)
+    combine_all = combine_all.reshape(row_count, tok_total, local_slots, DEPTH)
     expert_sum = jnp.zeros((row_count, width), jnp.float32)
     for local in range(local_slots):
-        slot_cols = (column // DEPTH) * (local_slots * DEPTH) + local * DEPTH + column % DEPTH
-        picks = target[:, :, None] == slot_cols[None, None, :]
-        dispatch = jnp.any(picks, axis=1).astype(jnp.bfloat16)
-        outgoing = lax.dot_general(
-            dispatch, normed, (((0,), (0,)), ((), ())), preferred_element_type=jnp.float32
-        ).astype(jnp.bfloat16)
-        outgoing = outgoing.reshape(tok_total, DEPTH, width)
-        arrived = lax.all_to_all(outgoing, "tok", split_axis=0, concat_axis=0, tiled=True)
-        arrived = arrived.reshape(tok_total * DEPTH, width)
-        hidden = jnp.dot(arrived, w_in[local], preferred_element_type=jnp.float32)
+        rows_in = arrived[:, local].reshape(tok_total * DEPTH, width)
+        hidden = jnp.dot(rows_in, w_in[local], preferred_element_type=jnp.float32)
         activated = (
             jax.nn.silu(hidden[:, :hidden_units]) * hidden[:, hidden_units:]
         ).astype(jnp.bfloat16)
@@ -97,7 +98,7 @@
         computed = computed.reshape(tok_total, DEPTH, width)
         returned = lax.all_to_all(computed, "tok", split_axis=0, concat_axis=0, tiled=True)
         returned = returned.reshape(tok_total * DEPTH, width)
-        combine = jnp.sum(jnp.where(picks, gate_live[:, :, None], jnp.float32(0.0)), axis=1)
+        combine = combine_all[:, :, local].reshape(row_count, tok_total * DEPTH)
         combine_hi = combine.astype(jnp.bfloat16)
         combine_lo = (combine - combine_hi.astype(jnp.float32)).astype(jnp.bfloat16)
         expert_sum = expert_sum + (

time: 224 us -> 221 us (0.987)
  blocking collectives: 0 us -> 79.3 us
  waiting for transfers between devices: 138 us -> 72.5 us
  starting transfers between devices: 30.3 us -> 18.2 us
  matrix products: 38.8 us -> 31.4 us
  local copies, waits for them, and re-layouts: 2.45 us -> 5.07 us
    all_to_all x0 -> x1, blocking collectives: none -> 79.3 us  [shards(): lax.all_to_all(outgoing, 'tok', split_axis=0, concat_axis=0, tiled=True)]
    all_to_all x2 -> x0, waiting for transfers between devices: 65.6 us -> none  [shards(): lax.all_to_all(outgoing, 'tok', split_axis=0, concat_axis=0, tiled=True)]
    all_to_all x2 -> x0, starting transfers between devices: 13.4 us -> none  [shards(): lax.all_to_all(outgoing, 'tok', split_axis=0, concat_axis=0, tiled=True)]
    dot_general x2 -> x1, matrix products: 5.53 us -> 1.89 us  [shards(): lax.dot_general(dispatch, normed, (((0,), (0,)), ((), ())), preferred_ele...]
    dot_general x2, matrix products: 12.8 us -> 9.8 us  [shards(): hidden = jnp.dot(rows_in, w_in[local], preferred_element_type=jnp.float32)]
    all_to_all x2, waiting for transfers between devices: 59.6 us -> 62.3 us  [shards(): lax.all_to_all(computed, 'tok', split_axis=0, concat_axis=0, tiled=True)]
    ppermute x3, waiting for transfers between devices: 12.7 us -> 10.2 us  [shards(): attn_out = attn_out + lax.ppermute(sent, 'tp', pairs).astype(jnp.float32)]
    slice x0 -> x1, local copies, waits for them, and re-layouts: none -> 2.29 us  [shards(): rows_in = arrived[:, local].reshape(tok_total * DEPTH, width)]
  transfers between devices with their start and end apart: 7 -> 5, of which waited for: 6 -> 4; matrix products, arithmetic and copies ran while one was open for 17% -> 10% of each run, Pallas kernels for 0% -> 0%
where the time goes in v5:
time: 221 us; the launch traced here: 219 us
  blocking collectives  79.3 us (36%)
  waiting for transfers between devices  72.5 us (33%)
  matrix products  31.4 us (14%)
  starting transfers between devices  18.2 us (8%)
  other arithmetic  11.7 us (5%)
  local copies, waits for them, and re-layouts  5.07 us (2%)
    all_to_all x1, blocking collectives, shards(): lax.all_to_all(outgoing, 'tok', split_axis=0, concat_axis=0, tiled=True)  79.3 us
    all_to_all x2, waiting for transfers between devices, shards(): lax.all_to_all(computed, 'tok', split_axis=0, concat_axis=0, tiled=True)  62.3 us
    all_to_all x2, starting transfers between devices, shards(): lax.all_to_all(computed, 'tok', split_axis=0, concat_axis=0, tiled=True)  11.7 us
    ppermute x3, waiting for transfers between devices, shards(): attn_out = attn_out + lax.ppermute(sent, 'tp', pairs).astype(jnp.float32)  10.2 us
    dot_general x2, matrix products, shards(): hidden = jnp.dot(rows_in, w_in[local], preferred_element_type=jnp.float32)  9.8 us
    dot_general x2, matrix products, shards(): jnp.dot(activated, w_out[local], preferred_element_type=jnp.float32)  7.08 us
    ppermute x3, starting transfers between devices, shards(): attn_out = attn_out + lax.ppermute(sent, 'tp', pairs).astype(jnp.float32)  6.51 us
    dot_general x2, matrix products, shards(): jnp.dot(combine_lo, returned, preferred_element_type=jnp.float32)  5.21 us
  transfers between devices with their start and end apart: 5, of which 4 were waited for; matrix products, arithmetic and copies ran while one was open for 10% of the time, Pallas kernels for 0%

profile of v5, /device:TPU:8, one launch (start us, length us, event | category | flops | bytes accessed | tf_op | source)
XLA Modules:
  0.0 219.2 jit_solution(5843534118457837369)
XLA Ops:
  0.7 1.2 copy-done
  1.9 2.0 convolution_convert_fusion.3
  3.9 1.0 dynamic-slice_bitcast_fusion.2
  4.9 1.9 collective-permute-start
  6.8 3.6 %collective-permute-start.1 = (bf16[128,1536]{1,0:T(8,128)(2,1)}, bf16[128,1536]{1,0:T(8,128)(2,1)}, u32[]{:S(2)}, u32[]{:S(2)}) collective-permute-start(bf16[128,1536]{1,0:T(8,128)(2,1)} %get-tuple-element.14), channel_id=1, source_target_pairs={{0,2},{1,3},{2,0},{3,1},{4,6},{5,7},{6,4},{7,5},{8,10},{9,11},{10,... | collective-permute-start | bytes 1179656 | tf_op jit(solution)/shard_map/ppermute | solution.py:58
  10.4 1.0 collective-permute-start.2
  11.6 0.7 fusion.40
  12.4 0.2 reduce_window_sum.11
  12.6 0.6 add_compare_fusion.1
  13.8 4.0 %fusion = pred[128,2048]{1,0:T(8,128)(4,1)S(1)} fusion(s32[128,8]{1,0:T(8,128)S(1)} %copy.19), kind=kLoop, calls=%fused_computation.2 | loop fusion | flops 3932160 | bytes 266240 | tf_op jit(solution)/shard_map/reduce_or | solution.py:79
  17.8 0.6 collective-permute-done
  18.3 9.6 %collective-permute-done.1 = bf16[128,1536]{1,0:T(8,128)(2,1)} collective-permute-done((bf16[128,1536]{1,0:T(8,128)(2,1)}, bf16[128,1536]{1,0:T(8,128)(2,1)}, u32[]{:S(2)}, u32[]{:S(2)}) %collective-permute-start.1) | collective-permute-done | bytes 393248 | tf_op jit(solution)/shard_map/ppermute | solution.py:58
  28.0 1.7 fusion.23
  29.7 1.9 convolution_convert_fusion
  31.6 79.3 %all_to_all.15 = bf16[32,64,1536]{2,1,0:T(8,128)(2,1)S(1)} all-to-all(bf16[32,64,1536]{2,1,0:T(8,128)(2,1)S(1)} %bitcast.50), channel_id=1, replica_groups=mesh['tok'=32,'tp'=4] {'tok'}, dimensions={0} | all-to-all | bytes 12582912 | tf_op jit(solution)/shard_map/all_to_all | solution.py:84
  110.9 2.3 %fusion.44 = (bf16[32,1,32,1536]{3,2,1,0:T(8,128)(2,1)S(1)}, bf16[32,1,32,1536]{3,2,1,0:T(8,128)(2,1)}) fusion(bf16[32,2,32,1536]{3,2,1,0:T(8,128)(2,1)S(1)} %bitcast.51), kind=kLoop, calls=%fused_computation.80 | loop fusion | bytes 12582912 | tf_op jit(solution)/shard_map/slice | solution.py:90
  113.2 3.4 %fusion.3 = f32[1024,1024]{1,0:T(8,128)S(1)} fusion(bf16[1024,1536]{1,0:T(8,128)(2,1)S(1)} %bitcast.58, bf16[2,1536,1024]{2,1,0:T(8,128)(2,1)S(1)} %bitcast.64), kind=kOutput, calls=%fused_computation.8 | convolution fusion | flops 3221225472 | bytes 10485760 | tf_op jit(solution)/shard_map/dot_general | solution.py:91
  116.7 3.5 %convolution_convert_fusion.2 = bf16[1024,1536]{1,0:T(8,128)(2,1)} fusion(bf16[2,512,1536]{2,1,0:T(8,128)(2,1)S(1)} %copy-done.8, f32[1024,1024]{1,0:T(8,128)S(1)} %fusion.3), kind=kOutput, calls=%fused_computation.5 | convolution fusion | flops 1615331328 | bytes 8912896 | tf_op jit(solution)/shard_map/dot_general | solution.py:95
  120.2 5.9 %all-to-all-start.1 = ((bf16[32,32,1536]{2,1,0:T(8,128)(2,1)}), bf16[32,32,1536]{2,1,0:T(8,128)(2,1)}, u32[]{:S(2)}, u32[]{:S(2)}) async-start(bf16[32,32,1536]{2,1,0:T(8,128)(2,1)} %bitcast.56), calls=%async_computation.1 | async-start | bytes 6291456 | tf_op jit(solution)/shard_map/all_to_all | solution.py:99
  126.1 6.4 %fusion.1 = f32[1024,1024]{1,0:T(8,128)S(1)} fusion(bf16[1024,1536]{1,0:T(8,128)(2,1)} %bitcast.57, bf16[2,1536,1024]{2,1,0:T(8,128)(2,1)} %param.19), kind=kOutput, calls=%fused_computation.6 | convolution fusion | flops 3221225472 | bytes 10485760 | tf_op jit(solution)/shard_map/dot_general | solution.py:91
  132.5 3.5 %convolution_convert_fusion.1 = bf16[1024,1536]{1,0:T(8,128)(2,1)} fusion(bf16[2,512,1536]{2,1,0:T(8,128)(2,1)S(1)} %copy-done.9, f32[1024,1024]{1,0:T(8,128)S(1)} %fusion.1), kind=kOutput, calls=%fused_computation.4 | convolution fusion | flops 1615331328 | bytes 8912896 | tf_op jit(solution)/shard_map/dot_general | solution.py:95
  136.1 29.4 %all-to-all-done.1 = bf16[32,32,1536]{2,1,0:T(8,128)(2,1)} async-done(((bf16[32,32,1536]{2,1,0:T(8,128)(2,1)}), bf16[32,32,1536]{2,1,0:T(8,128)(2,1)}, u32[]{:S(2)}, u32[]{:S(2)}) %all-to-all-start.1) | async-done | bytes 3145760 | tf_op jit(solution)/shard_map/all_to_all | solution.py:99
  165.4 5.8 %all-to-all-start.2 = ((bf16[32,32,1536]{2,1,0:T(8,128)(2,1)}), bf16[32,32,1536]{2,1,0:T(8,128)(2,1)}, u32[]{:S(2)}, u32[]{:S(2)}) async-start(bf16[32,32,1536]{2,1,0:T(8,128)(2,1)} %bitcast.55), calls=%async_computation.2 | async-start | bytes 6291456 | tf_op jit(solution)/shard_map/all_to_all | solution.py:99
  171.3 0.3 fusion.32
  171.8 2.8 %select_reduce_fusion = f32[128,2048]{1,0:T(8,128)S(1)} fusion(f32[128,8]{1,0:T(8,128)S(1)} %copy.20, s32[128,8]{1,0:T(8,128)S(1)} %copy.19), kind=kLoop, calls=%fused_computation | loop fusion | flops 6029312 | bytes 1056768 | tf_op jit(solution)/shard_map/reduce_sum | solution.py:86
  174.6 0.3 copy.21
  175.0 2.5 %fusion.45 = f32[128,1536]{1,0:T(8,128)S(1)} fusion(bf16[128,1024]{0,1:T(8,128)(2,1)S(1)} %bitcast.62, bf16[1024,1536]{1,0:T(8,128)(2,1)} %bitcast.13), kind=kOutput, calls=%fused_computation.81 | convolution fusion | flops 402653184 | bytes 4194304 | tf_op jit(solution)/shard_map/dot_general | solution.py:105
  177.6 32.9 %all-to-all-done.2 = bf16[32,32,1536]{2,1,0:T(8,128)(2,1)} async-done(((bf16[32,32,1536]{2,1,0:T(8,128)(2,1)}), bf16[32,32,1536]{2,1,0:T(8,128)(2,1)}, u32[]{:S(2)}, u32[]{:S(2)}) %all-to-all-start.2) | async-done | bytes 3145760 | tf_op jit(solution)/shard_map/all_to_all | solution.py:99
  210.5 2.5 %fusion.46 = f32[128,1536]{1,0:T(8,128)S(1)} fusion(bf16[128,1024]{0,1:T(8,128)(2,1)S(1)} %bitcast.61, bf16[1024,1536]{1,0:T(8,128)(2,1)} %bitcast.20), kind=kOutput, calls=%fused_computation.82 | convolution fusion | flops 402653184 | bytes 4194304 | tf_op jit(solution)/shard_map/dot_general | solution.py:105
  213.0 2.5 %convolution_add_fusion = f32[128,1536]{1,0:T(8,128)S(1)} fusion(f32[128,1536]{1,0:T(8,128)S(1)} %fusion.46, bf16[128,1024]{0,1:T(8,128)(2,1)S(1)} %bitcast.60, bf16[1024,1536]{1,0:T(8,128)(2,1)} %bitcast.20), kind=kOutput, calls=%fused_computation.13 | convolution fusion | flops 402849792 | bytes 4980736 | tf_op jit(solution)/shard_map/dot_general | solution.py:106
  215.6 2.7 %fusion.20 = (f32[128]{0:T(128)S(1)}, bf16[128,1536]{1,0:T(8,128)(2,1)S(1)}) fusion(f32[128,1536]{1,0:T(8,128)S(1)} %convolution_add_fusion, f32[128,1536]{1,0:T(8,128)S(1)} %fusion.45, bf16[128,1024]{0,1:T(8,128)(2,1)S(1)} %bitcast.59, bf16[1024,1536]{1,0:T(8,128)(2,1)} %bitcast.13, bf16[128,1536]{1,0:T(8,128)(2,1)S(1)} %copy-done.2), kind=kOutput, calls=%fused_computation.33 | convolution fusion | flops 404225920 | bytes 5767680 | tf_op jit(solution)/shard_map/dot_general | solution.py:106
  218.3 0.9 fusion.22
  (46 shorter events, 1.2 us)
Async XLA Ops:
  0.6 1.3 copy-start
  0.6 10.8 %copy-start.7 = (s32[64]{0:T(128)S(1)}, s32[64]{0:T(128)}, u32[]{:S(2)}) copy-start(s32[64]{0:T(128)} %param.18) | copy-start | bytes 772
  0.7 10.9 %copy-start.4 = (s32[128,8]{0,1:T(8,128)S(1)}, s32[128,8]{0,1:T(8,128)}, u32[]{:S(2)}) copy-start(s32[128,8]{0,1:T(8,128)} %param.16) | copy-start | bytes 12292
  0.7 10.9 %copy-start.11 = (s32[32]{0:T(128)S(1)}, s32[32]{0:T(128)}, u32[]{:S(2)}) copy-start(s32[32]{0:T(128)} %param.17) | copy-start | bytes 388
  3.9 25.8 %copy-start.5 = (f32[1536]{0:T(1024)S(1)}, f32[1536]{0:T(1024)}, u32[]{:S(2)}) copy-start(f32[1536]{0:T(1024)} %param.14) | copy-start | bytes 18436
  4.9 13.5 %collective-permute-start = (bf16[128,1536]{1,0:T(8,128)(2,1)}, bf16[128,1536]{1,0:T(8,128)(2,1)}, u32[]{:S(2)}, u32[]{:S(2)}) collective-permute-start(bf16[128,1536]{1,0:T(8,128)(2,1)} %get-tuple-element.12), channel_id=1, source_target_pairs={{0,1},{1,2},{2,3},{3,0},{4,5},{5,6},{6,7},{7,4},{8,9},{9,10},{10,1... | collective-permute-start | bytes 1179656 | tf_op jit(solution)/shard_map/ppermute | solution.py:58
  6.8 21.2 %collective-permute-start.1 = (bf16[128,1536]{1,0:T(8,128)(2,1)}, bf16[128,1536]{1,0:T(8,128)(2,1)}, u32[]{:S(2)}, u32[]{:S(2)}) collective-permute-start(bf16[128,1536]{1,0:T(8,128)(2,1)} %get-tuple-element.14), channel_id=1, source_target_pairs={{0,2},{1,3},{2,0},{3,1},{4,6},{5,7},{6,4},{7,5},{8,10},{9,11},{10,... | collective-permute-start | bytes 1179656 | tf_op jit(solution)/shard_map/ppermute | solution.py:58
  10.4 17.6 %collective-permute-start.2 = (bf16[128,1536]{1,0:T(8,128)(2,1)S(1)}, bf16[128,1536]{1,0:T(8,128)(2,1)}, u32[]{:S(2)}, u32[]{:S(2)}) collective-permute-start(bf16[128,1536]{1,0:T(8,128)(2,1)S(1)} %get-tuple-element.13), channel_id=1, source_target_pairs={{0,3},{1,0},{2,1},{3,2},{4,7},{5,4},{6,5},{7,6},{8,11},{9,8},{10,9... | collective-permute-start | bytes 1179656 | tf_op jit(solution)/shard_map/ppermute | solution.py:58
  29.7 141.6 %copy-start.1 = (bf16[128,1536]{1,0:T(8,128)(2,1)}, bf16[128,1536]{1,0:T(8,128)(2,1)S(1)}, u32[]{:S(2)}) copy-start(bf16[128,1536]{1,0:T(8,128)(2,1)S(1)} %get-tuple-element.9) | copy-start | bytes 1179652
  31.6 81.6 %slice-start = ((s8[6291456]{0:T(1024)(128)(4,1)}), s8[4194304]{0:T(1024)(128)(4,1)S(1)}, s32[]{:S(2)}) async-start(s8[6291456]{0:T(1024)(128)(4,1)} %bitcast.63), calls=%async_computation.3 | async-start | bytes 8388608
  110.9 2.3 %slice-start.1 = ((s8[6291456]{0:T(1024)(128)(4,1)}), s8[2097152]{0:T(1024)(128)(4,1)S(1)}, s32[]{:S(2)}) async-start(s8[6291456]{0:T(1024)(128)(4,1)} %bitcast.63), calls=%async_computation.4 | async-start | bytes 4194304
  113.2 3.4 %copy-start.8 = (bf16[2,512,1536]{2,1,0:T(8,128)(2,1)S(1)}, bf16[2,512,1536]{2,1,0:T(8,128)(2,1)}, u32[]{:S(2)}) copy-start(bf16[2,512,1536]{2,1,0:T(8,128)(2,1)} %param.20) | copy-start | bytes 9437188
  120.2 45.2 %all-to-all-start.1 = ((bf16[32,32,1536]{2,1,0:T(8,128)(2,1)}), bf16[32,32,1536]{2,1,0:T(8,128)(2,1)}, u32[]{:S(2)}, u32[]{:S(2)}) async-start(bf16[32,32,1536]{2,1,0:T(8,128)(2,1)} %bitcast.56), calls=%async_computation.1 | async-start | bytes 6291456 | tf_op jit(solution)/shard_map/all_to_all | solution.py:99
  126.1 6.4 %copy-start.9 = (bf16[2,512,1536]{2,1,0:T(8,128)(2,1)S(1)}, bf16[2,512,1536]{2,1,0:T(8,128)(2,1)}, u32[]{:S(2)}) copy-start(bf16[2,512,1536]{2,1,0:T(8,128)(2,1)} %param.20) | copy-start | bytes 9437188
  165.4 5.9 %copy-start.10 = (bf16[1536,40]{0,1:T(8,128)(2,1)S(1)}, bf16[1536,40]{0,1:T(8,128)(2,1)}, u32[]{:S(2)}) copy-start(bf16[1536,40]{0,1:T(8,128)(2,1)} %param.15) | copy-start | bytes 368644
  165.4 45.1 %all-to-all-start.2 = ((bf16[32,32,1536]{2,1,0:T(8,128)(2,1)}), bf16[32,32,1536]{2,1,0:T(8,128)(2,1)}, u32[]{:S(2)}, u32[]{:S(2)}) async-start(bf16[32,32,1536]{2,1,0:T(8,128)(2,1)} %bitcast.55), calls=%async_computation.2 | async-start | bytes 6291456 | tf_op jit(solution)/shard_map/all_to_all | solution.py:99
  213.0 2.6 %copy-start.2 = (bf16[128,1536]{1,0:T(8,128)(2,1)S(1)}, bf16[128,1536]{1,0:T(8,128)(2,1)}, u32[]{:S(2)}) copy-start(bf16[128,1536]{1,0:T(8,128)(2,1)} %copy-done.1) | copy-start | bytes 1179652
  215.5 2.7 %copy-start.6 = (f32[1536]{0:T(1024)S(1)}, f32[1536]{0:T(1024)}, u32[]{:S(2)}) copy-start(f32[1536]{0:T(1024)} %param.21) | copy-start | bytes 18436
  218.2 0.9 copy-start.3

commit v6 on v5

--- a/solution.py
+++ b/solution.py
@@ -101,10 +101,10 @@
         combine = combine_all[:, :, local].reshape(row_count, tok_total * DEPTH)
         combine_hi = combine.astype(jnp.bfloat16)
         combine_lo = (combine - combine_hi.astype(jnp.float32)).astype(jnp.bfloat16)
-        expert_sum = expert_sum + (
-            jnp.dot(combine_hi, returned, preferred_element_type=jnp.float32)
-            + jnp.dot(combine_lo, returned, preferred_element_type=jnp.float32)
+        both = jnp.dot(
+            jnp.concatenate([combine_hi, combine_lo]), returned, preferred_element_type=jnp.float32
         )
+        expert_sum = expert_sum + (both[:row_count] + both[row_count:])
     stream_out = (stream.astype(jnp.float32) + expert_sum).astype(jnp.bfloat16)
     next_normed = rms_norm(stream_out, gain_next)
     return (stream_out, next_normed)

time: 221 us -> 219 us (level)
  matrix products: 31.4 us -> 27 us
    dot_general x4 -> x2, matrix products: 10.2 us -> 5.87 us  [shards(): jnp.dot(jnp.concatenate([combine_hi, combine_lo]), returned, preferred_el...]
    ppermute x3, waiting for transfers between devices: 10.2 us -> 12.7 us  [shards(): attn_out = attn_out + lax.ppermute(sent, 'tp', pairs).astype(jnp.float32)]
  transfers between devices with their start and end apart: 5 -> 5, of which waited for: 4 -> 4; matrix products, arithmetic and copies ran while one was open for 10% -> 11% of each run, Pallas kernels for 0% -> 0%
where the time goes in v6:
time: 219 us; the launch traced here: 216 us
  blocking collectives  79.3 us (36%)
  waiting for transfers between devices  73.8 us (34%)
  matrix products  27 us (12%)
  starting transfers between devices  17 us (8%)
  other arithmetic  12.9 us (6%)
  local copies, waits for them, and re-layouts  5.36 us (2%)
    all_to_all x1, blocking collectives, shards(): lax.all_to_all(outgoing, 'tok', split_axis=0, concat_axis=0, tiled=True)  79.3 us
    all_to_all x2, waiting for transfers between devices, shards(): lax.all_to_all(computed, 'tok', split_axis=0, concat_axis=0, tiled=True)  61.1 us
    ppermute x3, waiting for transfers between devices, shards(): attn_out = attn_out + lax.ppermute(sent, 'tp', pairs).astype(jnp.float32)  12.7 us
    all_to_all x2, starting transfers between devices, shards(): lax.all_to_all(computed, 'tok', split_axis=0, concat_axis=0, tiled=True)  11.7 us
    dot_general x2, matrix products, shards(): hidden = jnp.dot(rows_in, w_in[local], preferred_element_type=jnp.float32)  9.8 us
    dot_general x2, matrix products, shards(): jnp.dot(activated, w_out[local], preferred_element_type=jnp.float32)  7.07 us
    dot_general x2, matrix products, shards(): jnp.dot(jnp.concatenate([combine_hi, combine_lo]), returned, preferred_el...  5.87 us
    ppermute x3, starting transfers between devices, shards(): attn_out = attn_out + lax.ppermute(sent, 'tp', pairs).astype(jnp.float32)  5.3 us
  transfers between devices with their start and end apart: 5, of which 4 were waited for; matrix products, arithmetic and copies ran while one was open for 11% of the time, Pallas kernels for 0%

profile of v6, /device:TPU:8, one launch (start us, length us, event | category | flops | bytes accessed | tf_op | source)
XLA Modules:
  0.0 216.4 jit_solution(10738605196780098112)
XLA Ops:
  0.7 1.2 copy-done
  1.9 2.0 convolution_convert_fusion.3
  3.9 1.0 dynamic-slice_bitcast_fusion.2
  4.9 4.0 %collective-permute-start.2 = (bf16[128,1536]{1,0:T(8,128)(2,1)}, bf16[128,1536]{1,0:T(8,128)(2,1)}, u32[]{:S(2)}, u32[]{:S(2)}) collective-permute-start(bf16[128,1536]{1,0:T(8,128)(2,1)} %get-tuple-element.15), channel_id=1, source_target_pairs={{0,3},{1,0},{2,1},{3,2},{4,7},{5,4},{6,5},{7,6},{8,11},{9,8},{10,9... | collective-permute-start | bytes 1179656 | tf_op jit(solution)/shard_map/ppermute | solution.py:58
  8.9 1.3 collective-permute-start
  10.3 0.2 reduce_window_sum.11
  10.7 0.7 fusion.49
  11.6 0.6 add_compare_fusion.1
  12.6 4.0 %fusion = pred[128,2048]{1,0:T(8,128)(4,1)S(1)} fusion(s32[128,8]{1,0:T(8,128)S(1)} %copy.19), kind=kLoop, calls=%fused_computation.2 | loop fusion | flops 3932160 | bytes 266240 | tf_op jit(solution)/shard_map/reduce_or | solution.py:79
  16.6 9.5 %collective-permute-done.2 = bf16[128,1536]{1,0:T(8,128)(2,1)} collective-permute-done((bf16[128,1536]{1,0:T(8,128)(2,1)}, bf16[128,1536]{1,0:T(8,128)(2,1)}, u32[]{:S(2)}, u32[]{:S(2)}) %collective-permute-start.2) | collective-permute-done | bytes 393248 | tf_op jit(solution)/shard_map/ppermute | solution.py:58
  26.1 3.2 %collective-permute-done = bf16[128,1536]{1,0:T(8,128)(2,1)} collective-permute-done((bf16[128,1536]{1,0:T(8,128)(2,1)S(1)}, bf16[128,1536]{1,0:T(8,128)(2,1)}, u32[]{:S(2)}, u32[]{:S(2)}) %collective-permute-start) | collective-permute-done | bytes 393248 | tf_op jit(solution)/shard_map/ppermute | solution.py:58
  29.3 1.7 fusion.20
  31.0 1.9 convolution_convert_fusion
  32.9 79.3 %all_to_all.15 = bf16[32,64,1536]{2,1,0:T(8,128)(2,1)S(1)} all-to-all(bf16[32,64,1536]{2,1,0:T(8,128)(2,1)S(1)} %bitcast.52), channel_id=1, replica_groups=mesh['tok'=32,'tp'=4] {'tok'}, dimensions={0} | all-to-all | bytes 12582912 | tf_op jit(solution)/shard_map/all_to_all | solution.py:84
  112.2 2.3 %fusion.56 = (bf16[32,1,32,1536]{3,2,1,0:T(8,128)(2,1)}, bf16[32,1,32,1536]{3,2,1,0:T(8,128)(2,1)S(1)}) fusion(bf16[32,2,32,1536]{3,2,1,0:T(8,128)(2,1)S(1)} %bitcast.53), kind=kLoop, calls=%fused_computation.92 | loop fusion | bytes 12582912 | tf_op jit(solution)/shard_map/slice | solution.py:90
  114.5 3.4 %fusion.1 = f32[1024,1024]{1,0:T(8,128)S(1)} fusion(bf16[1024,1536]{1,0:T(8,128)(2,1)S(1)} %bitcast.60, bf16[2,1536,1024]{2,1,0:T(8,128)(2,1)S(1)} %bitcast.62), kind=kOutput, calls=%fused_computation.6 | convolution fusion | flops 3221225472 | bytes 10485760 | tf_op jit(solution)/shard_map/dot_general | solution.py:91
  117.9 3.5 %convolution_convert_fusion.1 = bf16[1024,1536]{1,0:T(8,128)(2,1)} fusion(bf16[2,512,1536]{2,1,0:T(8,128)(2,1)S(1)} %copy-done.8, f32[1024,1024]{1,0:T(8,128)S(1)} %fusion.1), kind=kOutput, calls=%fused_computation.4 | convolution fusion | flops 1615331328 | bytes 8912896 | tf_op jit(solution)/shard_map/dot_general | solution.py:95
  121.5 5.9 %all-to-all-start.2 = ((bf16[32,32,1536]{2,1,0:T(8,128)(2,1)}), bf16[32,32,1536]{2,1,0:T(8,128)(2,1)}, u32[]{:S(2)}, u32[]{:S(2)}) async-start(bf16[32,32,1536]{2,1,0:T(8,128)(2,1)} %bitcast.58), calls=%async_computation.2 | async-start | bytes 6291456 | tf_op jit(solution)/shard_map/all_to_all | solution.py:99
  127.4 6.4 %fusion.3 = f32[1024,1024]{1,0:T(8,128)S(1)} fusion(bf16[1024,1536]{1,0:T(8,128)(2,1)} %bitcast.59, bf16[2,1536,1024]{2,1,0:T(8,128)(2,1)} %param.19), kind=kOutput, calls=%fused_computation.8 | convolution fusion | flops 3221225472 | bytes 10485760 | tf_op jit(solution)/shard_map/dot_general | solution.py:91
  133.8 3.5 %convolution_convert_fusion.2 = bf16[1024,1536]{1,0:T(8,128)(2,1)} fusion(bf16[2,512,1536]{2,1,0:T(8,128)(2,1)S(1)} %copy-done.9, f32[1024,1024]{1,0:T(8,128)S(1)} %fusion.3), kind=kOutput, calls=%fused_computation.5 | convolution fusion | flops 1615331328 | bytes 8912896 | tf_op jit(solution)/shard_map/dot_general | solution.py:95
  137.3 29.4 %all-to-all-done.2 = bf16[32,32,1536]{2,1,0:T(8,128)(2,1)} async-done(((bf16[32,32,1536]{2,1,0:T(8,128)(2,1)}), bf16[32,32,1536]{2,1,0:T(8,128)(2,1)}, u32[]{:S(2)}, u32[]{:S(2)}) %all-to-all-start.2) | async-done | bytes 3145760 | tf_op jit(solution)/shard_map/all_to_all | solution.py:99
  166.7 5.8 %all-to-all-start.1 = ((bf16[32,32,1536]{2,1,0:T(8,128)(2,1)}), bf16[32,32,1536]{2,1,0:T(8,128)(2,1)}, u32[]{:S(2)}, u32[]{:S(2)}) async-start(bf16[32,32,1536]{2,1,0:T(8,128)(2,1)} %bitcast.57), calls=%async_computation.1 | async-start | bytes 6291456 | tf_op jit(solution)/shard_map/all_to_all | solution.py:99
  172.6 0.3 fusion.41
  173.1 2.8 %select_reduce_fusion = f32[128,2048]{1,0:T(8,128)S(1)} fusion(f32[128,8]{1,0:T(8,128)S(1)} %copy.20, s32[128,8]{1,0:T(8,128)S(1)} %copy.19), kind=kLoop, calls=%fused_computation | loop fusion | flops 6029312 | bytes 1056768 | tf_op jit(solution)/shard_map/reduce_sum | solution.py:86
  175.8 0.3 copy.21
  176.3 0.8 fusion.38
  177.1 2.9 %fusion.33 = f32[256,1536]{1,0:T(8,128)S(1)} fusion(bf16[1024,1536]{1,0:T(8,128)(2,1)} %bitcast.19, bf16[128,1024]{0,1:T(8,128)(2,1)S(1)} %get-tuple-element.8, bf16[128,1024]{0,1:T(8,128)(2,1)S(1)} %get-tuple-element.9), kind=kOutput, calls=%fused_computation.48 | convolution fusion | flops 806354944 | bytes 5242880 | tf_op jit(solution)/shard_map/dot_general | solution.py:104
  180.0 31.7 %all-to-all-done.1 = bf16[32,32,1536]{2,1,0:T(8,128)(2,1)} async-done(((bf16[32,32,1536]{2,1,0:T(8,128)(2,1)}), bf16[32,32,1536]{2,1,0:T(8,128)(2,1)}, u32[]{:S(2)}, u32[]{:S(2)}) %all-to-all-start.1) | async-done | bytes 3145760 | tf_op jit(solution)/shard_map/all_to_all | solution.py:99
  211.8 3.0 %fusion.29 = f32[256,1536]{1,0:T(8,128)S(1)} fusion(bf16[1024,1536]{1,0:T(8,128)(2,1)} %bitcast.13, bf16[128,1024]{0,1:T(8,128)(2,1)S(1)} %get-tuple-element.6, bf16[128,1024]{0,1:T(8,128)(2,1)} %get-tuple-element.7), kind=kOutput, calls=%fused_computation.44 | convolution fusion | flops 806354944 | bytes 5242880 | tf_op jit(solution)/shard_map/dot_general | solution.py:104
  214.8 0.5 fusion.17
  215.3 0.2 copy-done.6
  215.5 0.9 fusion.19
  (47 shorter events, 1.2 us)
Async XLA Ops:
  0.6 1.3 copy-start
  0.6 9.6 %copy-start.7 = (s32[64]{0:T(128)S(1)}, s32[64]{0:T(128)}, u32[]{:S(2)}) copy-start(s32[64]{0:T(128)} %param.18) | copy-start | bytes 772
  0.7 9.9 %copy-start.4 = (s32[128,8]{0,1:T(8,128)S(1)}, s32[128,8]{0,1:T(8,128)}, u32[]{:S(2)}) copy-start(s32[128,8]{0,1:T(8,128)} %param.16) | copy-start | bytes 12292
  0.7 10.1 %copy-start.11 = (s32[32]{0:T(128)S(1)}, s32[32]{0:T(128)}, u32[]{:S(2)}) copy-start(s32[32]{0:T(128)} %param.17) | copy-start | bytes 388
  3.9 27.1 %copy-start.5 = (f32[1536]{0:T(1024)S(1)}, f32[1536]{0:T(1024)}, u32[]{:S(2)}) copy-start(f32[1536]{0:T(1024)} %param.14) | copy-start | bytes 18436
  4.9 21.2 %collective-permute-start.2 = (bf16[128,1536]{1,0:T(8,128)(2,1)}, bf16[128,1536]{1,0:T(8,128)(2,1)}, u32[]{:S(2)}, u32[]{:S(2)}) collective-permute-start(bf16[128,1536]{1,0:T(8,128)(2,1)} %get-tuple-element.15), channel_id=1, source_target_pairs={{0,3},{1,0},{2,1},{3,2},{4,7},{5,4},{6,5},{7,6},{8,11},{9,8},{10,9... | collective-permute-start | bytes 1179656 | tf_op jit(solution)/shard_map/ppermute | solution.py:58
  8.9 17.1 %collective-permute-start.1 = (bf16[128,1536]{1,0:T(8,128)(2,1)}, bf16[128,1536]{1,0:T(8,128)(2,1)}, u32[]{:S(2)}, u32[]{:S(2)}) collective-permute-start(bf16[128,1536]{1,0:T(8,128)(2,1)} %get-tuple-element.16), channel_id=1, source_target_pairs={{0,2},{1,3},{2,0},{3,1},{4,6},{5,7},{6,4},{7,5},{8,10},{9,11},{10,... | collective-permute-start | bytes 1179656 | tf_op jit(solution)/shard_map/ppermute | solution.py:58
  8.9 20.3 %collective-permute-start = (bf16[128,1536]{1,0:T(8,128)(2,1)S(1)}, bf16[128,1536]{1,0:T(8,128)(2,1)}, u32[]{:S(2)}, u32[]{:S(2)}) collective-permute-start(bf16[128,1536]{1,0:T(8,128)(2,1)S(1)} %get-tuple-element.14), channel_id=1, source_target_pairs={{0,1},{1,2},{2,3},{3,0},{4,5},{5,6},{6,7},{7,4},{8,9},{9,10},{10,1... | collective-permute-start | bytes 1179656 | tf_op jit(solution)/shard_map/ppermute | solution.py:58
  31.0 141.6 %copy-start.1 = (bf16[128,1536]{1,0:T(8,128)(2,1)}, bf16[128,1536]{1,0:T(8,128)(2,1)S(1)}, u32[]{:S(2)}) copy-start(bf16[128,1536]{1,0:T(8,128)(2,1)S(1)} %get-tuple-element.11) | copy-start | bytes 1179652
  32.9 81.6 %slice-start = ((s8[6291456]{0:T(1024)(128)(4,1)}), s8[4194304]{0:T(1024)(128)(4,1)S(1)}, s32[]{:S(2)}) async-start(s8[6291456]{0:T(1024)(128)(4,1)} %bitcast.61), calls=%async_computation.3 | async-start | bytes 8388608
  112.2 2.3 %slice-start.1 = ((s8[6291456]{0:T(1024)(128)(4,1)}), s8[2097152]{0:T(1024)(128)(4,1)S(1)}, s32[]{:S(2)}) async-start(s8[6291456]{0:T(1024)(128)(4,1)} %bitcast.61), calls=%async_computation.4 | async-start | bytes 4194304
  114.5 3.4 %copy-start.8 = (bf16[2,512,1536]{2,1,0:T(8,128)(2,1)S(1)}, bf16[2,512,1536]{2,1,0:T(8,128)(2,1)}, u32[]{:S(2)}) copy-start(bf16[2,512,1536]{2,1,0:T(8,128)(2,1)} %param.20) | copy-start | bytes 9437188
  121.5 45.2 %all-to-all-start.2 = ((bf16[32,32,1536]{2,1,0:T(8,128)(2,1)}), bf16[32,32,1536]{2,1,0:T(8,128)(2,1)}, u32[]{:S(2)}, u32[]{:S(2)}) async-start(bf16[32,32,1536]{2,1,0:T(8,128)(2,1)} %bitcast.58), calls=%async_computation.2 | async-start | bytes 6291456 | tf_op jit(solution)/shard_map/all_to_all | solution.py:99
  127.4 6.4 %copy-start.9 = (bf16[2,512,1536]{2,1,0:T(8,128)(2,1)S(1)}, bf16[2,512,1536]{2,1,0:T(8,128)(2,1)}, u32[]{:S(2)}) copy-start(bf16[2,512,1536]{2,1,0:T(8,128)(2,1)} %param.20) | copy-start | bytes 9437188
  166.7 5.9 %copy-start.10 = (bf16[1536,40]{0,1:T(8,128)(2,1)S(1)}, bf16[1536,40]{0,1:T(8,128)(2,1)}, u32[]{:S(2)}) copy-start(bf16[1536,40]{0,1:T(8,128)(2,1)} %param.15) | copy-start | bytes 368644
  166.7 45.1 %all-to-all-start.1 = ((bf16[32,32,1536]{2,1,0:T(8,128)(2,1)}), bf16[32,32,1536]{2,1,0:T(8,128)(2,1)}, u32[]{:S(2)}, u32[]{:S(2)}) async-start(bf16[32,32,1536]{2,1,0:T(8,128)(2,1)} %bitcast.57), calls=%async_computation.1 | async-start | bytes 6291456 | tf_op jit(solution)/shard_map/all_to_all | solution.py:99
  180.0 34.7 %copy-start.2 = (bf16[128,1536]{1,0:T(8,128)(2,1)S(1)}, bf16[128,1536]{1,0:T(8,128)(2,1)}, u32[]{:S(2)}) copy-start(bf16[128,1536]{1,0:T(8,128)(2,1)} %copy-done.1) | copy-start | bytes 1179652
  214.8 0.7 copy-start.6
  215.2 1.1 copy-start.3

commit v7 on v6

--- a/solution.py
+++ b/solution.py
@@ -49,13 +49,19 @@
     slot_total = slot_expert.shape[0]
     capacity = slot_total * DEPTH
     tp_total = lax.axis_size("tp")
-    partial = jnp.dot(context, attn_weight, preferred_element_type=jnp.float32).astype(jnp.bfloat16)
-    blocks = partial.reshape(tp_total, row_count, width)
-    attn_out = blocks[tp_rank].astype(jnp.float32)
+
+    def block_for(shift):
+        start = ((tp_rank + shift) % tp_total) * row_count
+        rows = lax.dynamic_slice_in_dim(context, start, row_count)
+        return jnp.dot(rows, attn_weight, preferred_element_type=jnp.float32).astype(jnp.bfloat16)
+
+    received = {}
+    for shift in [tp_total // 2] + [k for k in range(1, tp_total) if k != tp_total // 2]:
+        pairs = [(j, (j + shift) % tp_total) for j in range(tp_total)]
+        received[shift] = lax.ppermute(block_for(shift), "tp", pairs)
+    attn_out = block_for(0).astype(jnp.float32)
     for shift in range(1, tp_total):
-        sent = blocks[(tp_rank + shift) % tp_total]
-        pairs = [(j, (j + shift) % tp_total) for j in range(tp_total)]
-        attn_out = attn_out + lax.ppermute(sent, "tp", pairs).astype(jnp.float32)
+        attn_out = attn_out + received[shift].astype(jnp.float32)
     stream = (residual.astype(jnp.float32) + attn_out).astype(jnp.bfloat16)
     normed = rms_norm(stream, gain_first)
     logits = jnp.dot(normed, router, preferred_element_type=jnp.float32)

time: 219 us -> 219 us (level)
  matrix products: 27 us -> 31 us
    dot_general x1 -> x4, matrix products: 1.97 us -> 5.94 us  [block_for(): jnp.dot(rows, attn_weight, preferred_element_type=jnp.float32)]
  transfers between devices with their start and end apart: 5 -> 5, of which waited for: 4 -> 4; matrix products, arithmetic and copies ran while one was open for 11% -> 12% of each run, Pallas kernels for 0% -> 0%
where the time goes in v7:
time: 219 us; the launch traced here: 217 us
  blocking collectives  79.3 us (36%)
  waiting for transfers between devices  73.2 us (33%)
  matrix products  31 us (14%)
  starting transfers between devices  17.1 us (8%)
  other arithmetic  11.1 us (5%)
  local copies, waits for them, and re-layouts  4.37 us (2%)
    all_to_all x1, blocking collectives, shards(): lax.all_to_all(outgoing, 'tok', split_axis=0, concat_axis=0, tiled=True)  79.3 us
    all_to_all x2, waiting for transfers between devices, shards(): lax.all_to_all(computed, 'tok', split_axis=0, concat_axis=0, tiled=True)  61.1 us
    ppermute x3, waiting for transfers between devices, shards(): received[shift] = lax.ppermute(block_for(shift), 'tp', pairs)  12.1 us
    all_to_all x2, starting transfers between devices, shards(): lax.all_to_all(computed, 'tok', split_axis=0, concat_axis=0, tiled=True)  11.7 us
    dot_general x2, matrix products, shards(): hidden = jnp.dot(rows_in, w_in[local], preferred_element_type=jnp.float32)  9.8 us
    dot_general x2, matrix products, shards(): jnp.dot(activated, w_out[local], preferred_element_type=jnp.float32)  7.07 us
    dot_general x4, matrix products, block_for(): jnp.dot(rows, attn_weight, preferred_element_type=jnp.float32)  5.94 us
    dot_general x2, matrix products, shards(): jnp.dot(jnp.concatenate([combine_hi, combine_lo]), returned, preferred_el...  5.87 us
  transfers between devices with their start and end apart: 5, of which 4 were waited for; matrix products, arithmetic and copies ran while one was open for 12% of the time, Pallas kernels for 0%

profile of v7, /device:TPU:8, one launch (start us, length us, event | category | flops | bytes accessed | tf_op | source)
XLA Modules:
  0.0 217.0 jit_solution(16737274530574148013)
XLA Ops:
  0.7 1.2 copy-done
  1.9 1.3 convolution_convert_fusion.3
  3.2 4.1 %collective-permute-start.2 = (bf16[128,1536]{1,0:T(8,128)(2,1)S(1)}, bf16[128,1536]{1,0:T(8,128)(2,1)S(1)}, u32[]{:S(2)}, u32[]{:S(2)}) collective-permute-start(bf16[128,1536]{1,0:T(8,128)(2,1)S(1)} %convolution_convert_fusion.3), channel_id=1, source_target_pairs={{0,3},{1,0},{2,1},{3,2},{4,7},{5,4},{6,5},{7,6},{8,11},{9,8},{10,9... | collective-permute-start | bytes 1179656 | tf_op jit(solution)/shard_map/ppermute | solution.py:61
  7.3 2.0 convolution_convert_fusion.4
  9.3 1.1 convolution_convert_fusion.5
  10.4 1.2 collective-permute-start
  11.8 0.2 reduce_window_sum.11
  12.2 0.7 fusion.56
  13.1 0.6 add_compare_fusion.1
  14.1 4.0 %fusion = pred[128,2048]{1,0:T(8,128)(4,1)S(1)} fusion(s32[128,8]{1,0:T(8,128)S(1)} %copy.19), kind=kLoop, calls=%fused_computation.2 | loop fusion | flops 3932160 | bytes 266240 | tf_op jit(solution)/shard_map/reduce_or | solution.py:85
  18.1 6.0 %collective-permute-done.2 = bf16[128,1536]{1,0:T(8,128)(2,1)S(1)} collective-permute-done((bf16[128,1536]{1,0:T(8,128)(2,1)S(1)}, bf16[128,1536]{1,0:T(8,128)(2,1)S(1)}, u32[]{:S(2)}, u32[]{:S(2)}) %collective-permute-start.2) | collective-permute-done | bytes 393248 | tf_op jit(solution)/shard_map/ppermute | solution.py:61
  24.1 6.0 %collective-permute-done = bf16[128,1536]{1,0:T(8,128)(2,1)} collective-permute-done((bf16[128,1536]{1,0:T(8,128)(2,1)}, bf16[128,1536]{1,0:T(8,128)(2,1)}, u32[]{:S(2)}, u32[]{:S(2)}) %collective-permute-start) | collective-permute-done | bytes 393248 | tf_op jit(solution)/shard_map/ppermute | solution.py:61
  30.1 1.5 fusion.21
  31.7 1.9 convolution_convert_fusion
  33.6 79.3 %all_to_all.15 = bf16[32,64,1536]{2,1,0:T(8,128)(2,1)S(1)} all-to-all(bf16[32,64,1536]{2,1,0:T(8,128)(2,1)S(1)} %bitcast.43), channel_id=1, replica_groups=mesh['tok'=32,'tp'=4] {'tok'}, dimensions={0} | all-to-all | bytes 12582912 | tf_op jit(solution)/shard_map/all_to_all | solution.py:90
  112.9 2.3 %fusion.62 = (bf16[32,1,32,1536]{3,2,1,0:T(8,128)(2,1)}, bf16[32,1,32,1536]{3,2,1,0:T(8,128)(2,1)S(1)}) fusion(bf16[32,2,32,1536]{3,2,1,0:T(8,128)(2,1)S(1)} %bitcast.44), kind=kLoop, calls=%fused_computation.97 | loop fusion | bytes 12582912 | tf_op jit(solution)/shard_map/slice | solution.py:96
  115.2 3.4 %fusion.1 = f32[1024,1024]{1,0:T(8,128)S(1)} fusion(bf16[1024,1536]{1,0:T(8,128)(2,1)S(1)} %bitcast.49, bf16[2,1536,1024]{2,1,0:T(8,128)(2,1)S(1)} %bitcast.51), kind=kOutput, calls=%fused_computation.6 | convolution fusion | flops 3221225472 | bytes 10485760 | tf_op jit(solution)/shard_map/dot_general | solution.py:97
  118.6 3.5 %convolution_convert_fusion.1 = bf16[1024,1536]{1,0:T(8,128)(2,1)} fusion(bf16[2,512,1536]{2,1,0:T(8,128)(2,1)S(1)} %copy-done.10, f32[1024,1024]{1,0:T(8,128)S(1)} %fusion.1), kind=kOutput, calls=%fused_computation.4 | convolution fusion | flops 1615331328 | bytes 8912896 | tf_op jit(solution)/shard_map/dot_general | solution.py:101
  122.2 5.9 %all-to-all-start.2 = ((bf16[32,32,1536]{2,1,0:T(8,128)(2,1)}), bf16[32,32,1536]{2,1,0:T(8,128)(2,1)}, u32[]{:S(2)}, u32[]{:S(2)}) async-start(bf16[32,32,1536]{2,1,0:T(8,128)(2,1)} %bitcast.47), calls=%async_computation.2 | async-start | bytes 6291456 | tf_op jit(solution)/shard_map/all_to_all | solution.py:105
  128.1 6.4 %fusion.3 = f32[1024,1024]{1,0:T(8,128)S(1)} fusion(bf16[1024,1536]{1,0:T(8,128)(2,1)} %bitcast.48, bf16[2,1536,1024]{2,1,0:T(8,128)(2,1)} %param.19), kind=kOutput, calls=%fused_computation.8 | convolution fusion | flops 3221225472 | bytes 10485760 | tf_op jit(solution)/shard_map/dot_general | solution.py:97
  134.5 3.5 %convolution_convert_fusion.2 = bf16[1024,1536]{1,0:T(8,128)(2,1)} fusion(bf16[2,512,1536]{2,1,0:T(8,128)(2,1)S(1)} %copy-done.11, f32[1024,1024]{1,0:T(8,128)S(1)} %fusion.3), kind=kOutput, calls=%fused_computation.5 | convolution fusion | flops 1615331328 | bytes 8912896 | tf_op jit(solution)/shard_map/dot_general | solution.py:101
  138.0 29.4 %all-to-all-done.2 = bf16[32,32,1536]{2,1,0:T(8,128)(2,1)} async-done(((bf16[32,32,1536]{2,1,0:T(8,128)(2,1)}), bf16[32,32,1536]{2,1,0:T(8,128)(2,1)}, u32[]{:S(2)}, u32[]{:S(2)}) %all-to-all-start.2) | async-done | bytes 3145760 | tf_op jit(solution)/shard_map/all_to_all | solution.py:105
  167.4 5.8 %all-to-all-start.1 = ((bf16[32,32,1536]{2,1,0:T(8,128)(2,1)}), bf16[32,32,1536]{2,1,0:T(8,128)(2,1)}, u32[]{:S(2)}, u32[]{:S(2)}) async-start(bf16[32,32,1536]{2,1,0:T(8,128)(2,1)} %bitcast.46), calls=%async_computation.1 | async-start | bytes 6291456 | tf_op jit(solution)/shard_map/all_to_all | solution.py:105
  173.2 0.3 fusion.38
  173.8 2.8 %select_reduce_fusion = f32[128,2048]{1,0:T(8,128)S(1)} fusion(f32[128,8]{1,0:T(8,128)S(1)} %copy.20, s32[128,8]{1,0:T(8,128)S(1)} %copy.19), kind=kLoop, calls=%fused_computation | loop fusion | flops 6029312 | bytes 1056768 | tf_op jit(solution)/shard_map/reduce_sum | solution.py:92
  176.5 0.3 copy.21
  177.0 0.8 fusion.35
  177.8 2.9 %fusion.30 = f32[256,1536]{1,0:T(8,128)S(1)} fusion(bf16[1024,1536]{1,0:T(8,128)(2,1)} %bitcast.14, bf16[128,1024]{0,1:T(8,128)(2,1)S(1)} %get-tuple-element.8, bf16[128,1024]{0,1:T(8,128)(2,1)S(1)} %get-tuple-element.9), kind=kOutput, calls=%fused_computation.48 | convolution fusion | flops 806354944 | bytes 5242880 | tf_op jit(solution)/shard_map/dot_general | solution.py:110
  180.7 31.7 %all-to-all-done.1 = bf16[32,32,1536]{2,1,0:T(8,128)(2,1)} async-done(((bf16[32,32,1536]{2,1,0:T(8,128)(2,1)}), bf16[32,32,1536]{2,1,0:T(8,128)(2,1)}, u32[]{:S(2)}, u32[]{:S(2)}) %all-to-all-start.1) | async-done | bytes 3145760 | tf_op jit(solution)/shard_map/all_to_all | solution.py:105
  212.4 3.0 %fusion.26 = f32[256,1536]{1,0:T(8,128)S(1)} fusion(bf16[1024,1536]{1,0:T(8,128)(2,1)} %bitcast.8, bf16[128,1024]{0,1:T(8,128)(2,1)S(1)} %get-tuple-element.6, bf16[128,1024]{0,1:T(8,128)(2,1)} %get-tuple-element.7), kind=kOutput, calls=%fused_computation.44 | convolution fusion | flops 806354944 | bytes 5242880 | tf_op jit(solution)/shard_map/dot_general | solution.py:110
  215.4 0.5 fusion.18
  216.1 0.9 fusion.20
  (52 shorter events, 1.5 us)
Async XLA Ops:
  0.6 1.3 copy-start
  0.6 8.7 %copy-start.4 = (bf16[512,384]{1,0:T(8,128)(2,1)S(1)}, bf16[512,384]{1,0:T(8,128)(2,1)}, u32[]{:S(2)}) copy-start(bf16[512,384]{1,0:T(8,128)(2,1)} %param.11) | copy-start | bytes 1179652
  0.7 11.0 %copy-start.9 = (s32[64]{0:T(128)S(1)}, s32[64]{0:T(128)}, u32[]{:S(2)}) copy-start(s32[64]{0:T(128)} %param.18) | copy-start | bytes 772
  0.7 11.4 %copy-start.6 = (s32[128,8]{0,1:T(8,128)S(1)}, s32[128,8]{0,1:T(8,128)}, u32[]{:S(2)}) copy-start(s32[128,8]{0,1:T(8,128)} %param.16) | copy-start | bytes 12292
  0.7 11.5 %copy-start.13 = (s32[32]{0:T(128)S(1)}, s32[32]{0:T(128)}, u32[]{:S(2)}) copy-start(s32[32]{0:T(128)} %param.17) | copy-start | bytes 388
  0.7 29.4 %copy-start.5 = (bf16[128,1536]{1,0:T(8,128)(2,1)S(1)}, bf16[128,1536]{1,0:T(8,128)(2,1)}, u32[]{:S(2)}) copy-start(bf16[128,1536]{1,0:T(8,128)(2,1)} %param.13) | copy-start | bytes 1179652
  3.2 20.9 %collective-permute-start.2 = (bf16[128,1536]{1,0:T(8,128)(2,1)S(1)}, bf16[128,1536]{1,0:T(8,128)(2,1)S(1)}, u32[]{:S(2)}, u32[]{:S(2)}) collective-permute-start(bf16[128,1536]{1,0:T(8,128)(2,1)S(1)} %convolution_convert_fusion.3), channel_id=1, source_target_pairs={{0,3},{1,0},{2,1},{3,2},{4,7},{5,4},{6,5},{7,6},{8,11},{9,8},{10,9... | collective-permute-start | bytes 1179656 | tf_op jit(solution)/shard_map/ppermute | solution.py:61
  9.3 22.4 %copy-start.7 = (f32[1536]{0:T(1024)S(1)}, f32[1536]{0:T(1024)}, u32[]{:S(2)}) copy-start(f32[1536]{0:T(1024)} %param.14) | copy-start | bytes 18436
  9.3 14.8 %collective-permute-start.1 = (bf16[128,1536]{1,0:T(8,128)(2,1)}, bf16[128,1536]{1,0:T(8,128)(2,1)S(1)}, u32[]{:S(2)}, u32[]{:S(2)}) collective-permute-start(bf16[128,1536]{1,0:T(8,128)(2,1)} %convolution_convert_fusion.4), channel_id=1, source_target_pairs={{0,2},{1,3},{2,0},{3,1},{4,6},{5,7},{6,4},{7,5},{8,10},{9,11},{10,... | collective-permute-start | bytes 1179656 | tf_op jit(solution)/shard_map/ppermute | solution.py:61
  10.4 19.7 %collective-permute-start = (bf16[128,1536]{1,0:T(8,128)(2,1)}, bf16[128,1536]{1,0:T(8,128)(2,1)}, u32[]{:S(2)}, u32[]{:S(2)}) collective-permute-start(bf16[128,1536]{1,0:T(8,128)(2,1)} %convolution_convert_fusion.5), channel_id=1, source_target_pairs={{0,1},{1,2},{2,3},{3,0},{4,5},{5,6},{6,7},{7,4},{8,9},{9,10},{10,1... | collective-permute-start | bytes 1179656 | tf_op jit(solution)/shard_map/ppermute | solution.py:61
  31.7 141.5 %copy-start.1 = (bf16[128,1536]{1,0:T(8,128)(2,1)}, bf16[128,1536]{1,0:T(8,128)(2,1)S(1)}, u32[]{:S(2)}) copy-start(bf16[128,1536]{1,0:T(8,128)(2,1)S(1)} %get-tuple-element.15) | copy-start | bytes 1179652
  33.6 81.6 %slice-start = ((s8[6291456]{0:T(1024)(128)(4,1)}), s8[4194304]{0:T(1024)(128)(4,1)S(1)}, s32[]{:S(2)}) async-start(s8[6291456]{0:T(1024)(128)(4,1)} %bitcast.50), calls=%async_computation.3 | async-start | bytes 8388608
  112.9 2.3 %slice-start.1 = ((s8[6291456]{0:T(1024)(128)(4,1)}), s8[2097152]{0:T(1024)(128)(4,1)S(1)}, s32[]{:S(2)}) async-start(s8[6291456]{0:T(1024)(128)(4,1)} %bitcast.50), calls=%async_computation.4 | async-start | bytes 4194304
  115.2 3.4 %copy-start.10 = (bf16[2,512,1536]{2,1,0:T(8,128)(2,1)S(1)}, bf16[2,512,1536]{2,1,0:T(8,128)(2,1)}, u32[]{:S(2)}) copy-start(bf16[2,512,1536]{2,1,0:T(8,128)(2,1)} %param.20) | copy-start | bytes 9437188
  122.2 45.2 %all-to-all-start.2 = ((bf16[32,32,1536]{2,1,0:T(8,128)(2,1)}), bf16[32,32,1536]{2,1,0:T(8,128)(2,1)}, u32[]{:S(2)}, u32[]{:S(2)}) async-start(bf16[32,32,1536]{2,1,0:T(8,128)(2,1)} %bitcast.47), calls=%async_computation.2 | async-start | bytes 6291456 | tf_op jit(solution)/shard_map/all_to_all | solution.py:105
  128.1 6.4 %copy-start.11 = (bf16[2,512,1536]{2,1,0:T(8,128)(2,1)S(1)}, bf16[2,512,1536]{2,1,0:T(8,128)(2,1)}, u32[]{:S(2)}) copy-start(bf16[2,512,1536]{2,1,0:T(8,128)(2,1)} %param.20) | copy-start | bytes 9437188
  167.4 5.9 %copy-start.12 = (bf16[1536,40]{0,1:T(8,128)(2,1)S(1)}, bf16[1536,40]{0,1:T(8,128)(2,1)}, u32[]{:S(2)}) copy-start(bf16[1536,40]{0,1:T(8,128)(2,1)} %param.15) | copy-start | bytes 368644
  167.4 45.1 %all-to-all-start.1 = ((bf16[32,32,1536]{2,1,0:T(8,128)(2,1)}), bf16[32,32,1536]{2,1,0:T(8,128)(2,1)}, u32[]{:S(2)}, u32[]{:S(2)}) async-start(bf16[32,32,1536]{2,1,0:T(8,128)(2,1)} %bitcast.46), calls=%async_computation.1 | async-start | bytes 6291456 | tf_op jit(solution)/shard_map/all_to_all | solution.py:105
  180.7 34.7 %copy-start.2 = (bf16[128,1536]{1,0:T(8,128)(2,1)S(1)}, bf16[128,1536]{1,0:T(8,128)(2,1)}, u32[]{:S(2)}) copy-start(bf16[128,1536]{1,0:T(8,128)(2,1)} %copy-done.1) | copy-start | bytes 1179652
  215.4 0.7 copy-start.8
  215.9 1.1 copy-start.3

commit v8 on v7

--- a/solution.py
+++ b/solution.py
@@ -84,7 +84,7 @@
     picks = target[:, :, None] == jnp.arange(capacity, dtype=jnp.int32)[None, None, :]
     dispatch = jnp.any(picks, axis=1).astype(jnp.bfloat16)
     outgoing = lax.dot_general(
-        dispatch, normed, (((0,), (0,)), ((), ())), preferred_element_type=jnp.float32
+        dispatch, stream, (((0,), (0,)), ((), ())), preferred_element_type=jnp.float32
     ).astype(jnp.bfloat16)
     outgoing = outgoing.reshape(tok_total, local_slots * DEPTH, width)
     arrived = lax.all_to_all(outgoing, "tok", split_axis=0, concat_axis=0, tiled=True)
@@ -93,7 +93,7 @@
     combine_all = combine_all.reshape(row_count, tok_total, local_slots, DEPTH)
     expert_sum = jnp.zeros((row_count, width), jnp.float32)
     for local in range(local_slots):
-        rows_in = arrived[:, local].reshape(tok_total * DEPTH, width)
+        rows_in = rms_norm(arrived[:, local].reshape(tok_total * DEPTH, width), gain_first)
         hidden = jnp.dot(rows_in, w_in[local], preferred_element_type=jnp.float32)
         activated = (
             jax.nn.silu(hidden[:, :hidden_units]) * hidden[:, hidden_units:]

time: 219 us -> 221 us (level)
  other arithmetic: 11.1 us -> 15.3 us
  local copies, waits for them, and re-layouts: 4.37 us -> 2.09 us
    convert_element_type x1 -> x2, other arithmetic: 0.9 us -> 3.64 us  [rms_norm(): return (values * inverse_rms * gain_vec).astype(jnp.bfloat16)]
    slice x1 -> x0, local copies, waits for them, and re-layouts: 2.28 us -> none  [shards(): rows_in = arrived[:, local].reshape(tok_total * DEPTH, width)]
where the time goes in v8:
time: 221 us; the launch traced here: 219 us
  blocking collectives  79 us (36%)
  waiting for transfers between devices  73.1 us (33%)
  matrix products  31 us (14%)
  starting transfers between devices  17.1 us (8%)
  other arithmetic  15.3 us (7%)
    all_to_all x1, blocking collectives, shards(): lax.all_to_all(outgoing, 'tok', split_axis=0, concat_axis=0, tiled=True)  79 us
    all_to_all x2, waiting for transfers between devices, shards(): lax.all_to_all(computed, 'tok', split_axis=0, concat_axis=0, tiled=True)  61.1 us
    ppermute x3, waiting for transfers between devices, shards(): received[shift] = lax.ppermute(block_for(shift), 'tp', pairs)  12.1 us
    all_to_all x2, starting transfers between devices, shards(): lax.all_to_all(computed, 'tok', split_axis=0, concat_axis=0, tiled=True)  11.7 us
    dot_general x2, matrix products, shards(): hidden = jnp.dot(rows_in, w_in[local], preferred_element_type=jnp.float32)  9.8 us
    dot_general x2, matrix products, shards(): jnp.dot(activated, w_out[local], preferred_element_type=jnp.float32)  7.09 us
    dot_general x4, matrix products, block_for(): jnp.dot(rows, attn_weight, preferred_element_type=jnp.float32)  5.94 us
    dot_general x2, matrix products, shards(): jnp.dot(jnp.concatenate([combine_hi, combine_lo]), returned, preferred_el...  5.87 us
  transfers between devices with their start and end apart: 5, of which 4 were waited for; matrix products, arithmetic and copies ran while one was open for 12% of the time, Pallas kernels for 0%

profile of v8, /device:TPU:8, one launch (start us, length us, event | category | flops | bytes accessed | tf_op | source)
XLA Modules:
  0.0 218.5 jit_solution(10471836717717023271)
XLA Ops:
  0.7 1.2 copy-done
  1.9 1.3 convolution_convert_fusion.3
  3.2 4.1 %collective-permute-start.2 = (bf16[128,1536]{1,0:T(8,128)(2,1)S(1)}, bf16[128,1536]{1,0:T(8,128)(2,1)S(1)}, u32[]{:S(2)}, u32[]{:S(2)}) collective-permute-start(bf16[128,1536]{1,0:T(8,128)(2,1)S(1)} %convolution_convert_fusion.3), channel_id=1, source_target_pairs={{0,3},{1,0},{2,1},{3,2},{4,7},{5,4},{6,5},{7,6},{8,11},{9,8},{10,9... | collective-permute-start | bytes 1179656 | tf_op jit(solution)/shard_map/ppermute | solution.py:61
  7.3 2.0 convolution_convert_fusion.4
  9.3 1.1 convolution_convert_fusion.5
  10.4 1.3 collective-permute-start
  12.2 0.7 fusion.63
  13.1 0.6 add_compare_fusion.1
  14.1 4.0 %fusion = pred[128,2048]{1,0:T(8,128)(4,1)S(1)} fusion(s32[128,8]{1,0:T(8,128)S(1)} %copy.19), kind=kLoop, calls=%fused_computation.2 | loop fusion | flops 3932160 | bytes 266240 | tf_op jit(solution)/shard_map/reduce_or | solution.py:85
  18.1 6.0 %collective-permute-done.2 = bf16[128,1536]{1,0:T(8,128)(2,1)S(1)} collective-permute-done((bf16[128,1536]{1,0:T(8,128)(2,1)S(1)}, bf16[128,1536]{1,0:T(8,128)(2,1)S(1)}, u32[]{:S(2)}, u32[]{:S(2)}) %collective-permute-start.2) | collective-permute-done | bytes 393248 | tf_op jit(solution)/shard_map/ppermute | solution.py:61
  24.1 6.0 %collective-permute-done = bf16[128,1536]{1,0:T(8,128)(2,1)} collective-permute-done((bf16[128,1536]{1,0:T(8,128)(2,1)}, bf16[128,1536]{1,0:T(8,128)(2,1)}, u32[]{:S(2)}, u32[]{:S(2)}) %collective-permute-start) | collective-permute-done | bytes 393248 | tf_op jit(solution)/shard_map/ppermute | solution.py:61
  30.1 1.5 fusion.27
  31.7 1.8 convolution_convert_fusion
  33.5 79.0 %all_to_all.15 = bf16[32,64,1536]{2,1,0:T(8,128)(2,1)S(1)} all-to-all(bf16[32,64,1536]{2,1,0:T(8,128)(2,1)S(1)} %bitcast.46), channel_id=1, replica_groups=mesh['tok'=32,'tp'=4] {'tok'}, dimensions={0} | all-to-all | bytes 12582912 | tf_op jit(solution)/shard_map/all_to_all | solution.py:90
  112.6 1.3 fusion.1
  114.0 2.7 %fusion.3 = (bf16[32,1,32,1536]{3,2,1,0:T(8,128)(2,1)}, bf16[32,1,32,1536]{3,2,1,0:T(8,128)(2,1)S(1)}) fusion(f32[1536]{0:T(1024)S(1)} %copy-done.8, f32[32,32]{1,0:T(8,128)S(1)} %get-tuple-element.19, bf16[32,2,32,1536]{3,2,1,0:T(8,128)(2,1)S(1)} %bitcast.45, f32[32,32]{1,0:T(8,128)S(1)} %get-tuple-element.18), kind=kLoop, calls=%fused_computation.10 | loop fusion | flops 12582912 | bytes 12597248 | tf_op jit(solution)/shard_map/convert_element_type | solution.py:15
  116.7 3.4 %fusion.7 = f32[1024,1024]{1,0:T(8,128)S(1)} fusion(bf16[1024,1536]{1,0:T(8,128)(2,1)S(1)} %bitcast.51, bf16[2,1536,1024]{2,1,0:T(8,128)(2,1)S(1)} %bitcast.53), kind=kOutput, calls=%fused_computation.16 | convolution fusion | flops 3221225472 | bytes 10485760 | tf_op jit(solution)/shard_map/dot_general | solution.py:97
  120.1 3.5 %convolution_convert_fusion.1 = bf16[1024,1536]{1,0:T(8,128)(2,1)} fusion(bf16[2,512,1536]{2,1,0:T(8,128)(2,1)S(1)} %copy-done.10, f32[1024,1024]{1,0:T(8,128)S(1)} %fusion.7), kind=kOutput, calls=%fused_computation.14 | convolution fusion | flops 1615331328 | bytes 8912896 | tf_op jit(solution)/shard_map/dot_general | solution.py:101
  123.7 5.9 %all-to-all-start.2 = ((bf16[32,32,1536]{2,1,0:T(8,128)(2,1)}), bf16[32,32,1536]{2,1,0:T(8,128)(2,1)}, u32[]{:S(2)}, u32[]{:S(2)}) async-start(bf16[32,32,1536]{2,1,0:T(8,128)(2,1)} %bitcast.49), calls=%async_computation.2 | async-start | bytes 6291456 | tf_op jit(solution)/shard_map/all_to_all | solution.py:105
  129.6 6.4 %fusion.9 = f32[1024,1024]{1,0:T(8,128)S(1)} fusion(bf16[1024,1536]{1,0:T(8,128)(2,1)} %bitcast.50, bf16[2,1536,1024]{2,1,0:T(8,128)(2,1)} %param.19), kind=kOutput, calls=%fused_computation.18 | convolution fusion | flops 3221225472 | bytes 10485760 | tf_op jit(solution)/shard_map/dot_general | solution.py:97
  136.0 3.5 %convolution_convert_fusion.2 = bf16[1024,1536]{1,0:T(8,128)(2,1)} fusion(bf16[2,512,1536]{2,1,0:T(8,128)(2,1)S(1)} %copy-done.11, f32[1024,1024]{1,0:T(8,128)S(1)} %fusion.9), kind=kOutput, calls=%fused_computation.15 | convolution fusion | flops 1615331328 | bytes 8912896 | tf_op jit(solution)/shard_map/dot_general | solution.py:101
  139.5 29.4 %all-to-all-done.2 = bf16[32,32,1536]{2,1,0:T(8,128)(2,1)} async-done(((bf16[32,32,1536]{2,1,0:T(8,128)(2,1)}), bf16[32,32,1536]{2,1,0:T(8,128)(2,1)}, u32[]{:S(2)}, u32[]{:S(2)}) %all-to-all-start.2) | async-done | bytes 3145760 | tf_op jit(solution)/shard_map/all_to_all | solution.py:105
  168.9 5.8 %all-to-all-start.1 = ((bf16[32,32,1536]{2,1,0:T(8,128)(2,1)}), bf16[32,32,1536]{2,1,0:T(8,128)(2,1)}, u32[]{:S(2)}, u32[]{:S(2)}) async-start(bf16[32,32,1536]{2,1,0:T(8,128)(2,1)} %bitcast.48), calls=%async_computation.1 | async-start | bytes 6291456 | tf_op jit(solution)/shard_map/all_to_all | solution.py:105
  174.8 0.3 fusion.42
  175.3 2.8 %select_reduce_fusion = f32[128,2048]{1,0:T(8,128)S(1)} fusion(f32[128,8]{1,0:T(8,128)S(1)} %copy.20, s32[128,8]{1,0:T(8,128)S(1)} %copy.19), kind=kLoop, calls=%fused_computation | loop fusion | flops 6029312 | bytes 1056768 | tf_op jit(solution)/shard_map/reduce_sum | solution.py:92
  178.0 0.3 copy.21
  178.5 0.8 fusion.41
  179.3 2.9 %fusion.36 = f32[256,1536]{1,0:T(8,128)S(1)} fusion(bf16[1024,1536]{1,0:T(8,128)(2,1)} %bitcast.14, bf16[128,1024]{0,1:T(8,128)(2,1)S(1)} %get-tuple-element.10, bf16[128,1024]{0,1:T(8,128)(2,1)S(1)} %get-tuple-element.11), kind=kOutput, calls=%fused_computation.58 | convolution fusion | flops 806354944 | bytes 5242880 | tf_op jit(solution)/shard_map/dot_general | solution.py:110
  182.2 31.7 %all-to-all-done.1 = bf16[32,32,1536]{2,1,0:T(8,128)(2,1)} async-done(((bf16[32,32,1536]{2,1,0:T(8,128)(2,1)}), bf16[32,32,1536]{2,1,0:T(8,128)(2,1)}, u32[]{:S(2)}, u32[]{:S(2)}) %all-to-all-start.1) | async-done | bytes 3145760 | tf_op jit(solution)/shard_map/all_to_all | solution.py:105
  213.9 3.0 %fusion.32 = f32[256,1536]{1,0:T(8,128)S(1)} fusion(bf16[1024,1536]{1,0:T(8,128)(2,1)} %bitcast.8, bf16[128,1024]{0,1:T(8,128)(2,1)S(1)} %get-tuple-element.8, bf16[128,1024]{0,1:T(8,128)(2,1)} %get-tuple-element.9), kind=kOutput, calls=%fused_computation.54 | convolution fusion | flops 806354944 | bytes 5242880 | tf_op jit(solution)/shard_map/dot_general | solution.py:110
  217.0 0.5 fusion.24
  217.6 0.9 fusion.26
  (54 shorter events, 1.7 us)
Async XLA Ops:
  0.6 1.3 copy-start
  0.6 8.7 %copy-start.4 = (bf16[512,384]{1,0:T(8,128)(2,1)S(1)}, bf16[512,384]{1,0:T(8,128)(2,1)}, u32[]{:S(2)}) copy-start(bf16[512,384]{1,0:T(8,128)(2,1)} %param.11) | copy-start | bytes 1179652
  0.7 11.0 %copy-start.9 = (s32[64]{0:T(128)S(1)}, s32[64]{0:T(128)}, u32[]{:S(2)}) copy-start(s32[64]{0:T(128)} %param.18) | copy-start | bytes 772
  0.7 11.4 %copy-start.6 = (s32[128,8]{0,1:T(8,128)S(1)}, s32[128,8]{0,1:T(8,128)}, u32[]{:S(2)}) copy-start(s32[128,8]{0,1:T(8,128)} %param.16) | copy-start | bytes 12292
  0.7 11.5 %copy-start.13 = (s32[32]{0:T(128)S(1)}, s32[32]{0:T(128)}, u32[]{:S(2)}) copy-start(s32[32]{0:T(128)} %param.17) | copy-start | bytes 388
  0.7 29.4 %copy-start.5 = (bf16[128,1536]{1,0:T(8,128)(2,1)S(1)}, bf16[128,1536]{1,0:T(8,128)(2,1)}, u32[]{:S(2)}) copy-start(bf16[128,1536]{1,0:T(8,128)(2,1)} %param.13) | copy-start | bytes 1179652
  3.2 20.9 %collective-permute-start.2 = (bf16[128,1536]{1,0:T(8,128)(2,1)S(1)}, bf16[128,1536]{1,0:T(8,128)(2,1)S(1)}, u32[]{:S(2)}, u32[]{:S(2)}) collective-permute-start(bf16[128,1536]{1,0:T(8,128)(2,1)S(1)} %convolution_convert_fusion.3), channel_id=1, source_target_pairs={{0,3},{1,0},{2,1},{3,2},{4,7},{5,4},{6,5},{7,6},{8,11},{9,8},{10,9... | collective-permute-start | bytes 1179656 | tf_op jit(solution)/shard_map/ppermute | solution.py:61
  9.3 14.8 %collective-permute-start.1 = (bf16[128,1536]{1,0:T(8,128)(2,1)}, bf16[128,1536]{1,0:T(8,128)(2,1)S(1)}, u32[]{:S(2)}, u32[]{:S(2)}) collective-permute-start(bf16[128,1536]{1,0:T(8,128)(2,1)} %convolution_convert_fusion.4), channel_id=1, source_target_pairs={{0,2},{1,3},{2,0},{3,1},{4,6},{5,7},{6,4},{7,5},{8,10},{9,11},{10,... | collective-permute-start | bytes 1179656 | tf_op jit(solution)/shard_map/ppermute | solution.py:61
  10.4 19.7 %collective-permute-start = (bf16[128,1536]{1,0:T(8,128)(2,1)}, bf16[128,1536]{1,0:T(8,128)(2,1)}, u32[]{:S(2)}, u32[]{:S(2)}) collective-permute-start(bf16[128,1536]{1,0:T(8,128)(2,1)} %convolution_convert_fusion.5), channel_id=1, source_target_pairs={{0,1},{1,2},{2,3},{3,0},{4,5},{5,6},{6,7},{7,4},{8,9},{9,10},{10,1... | collective-permute-start | bytes 1179656 | tf_op jit(solution)/shard_map/ppermute | solution.py:61
  31.7 143.1 %copy-start.1 = (bf16[128,1536]{1,0:T(8,128)(2,1)}, bf16[128,1536]{1,0:T(8,128)(2,1)S(1)}, u32[]{:S(2)}) copy-start(bf16[128,1536]{1,0:T(8,128)(2,1)S(1)} %get-tuple-element.17) | copy-start | bytes 1179652
  112.6 1.4 copy-start.8
  112.6 4.1 %slice-start = ((s8[6291456]{0:T(1024)(128)(4,1)}), s8[4194304]{0:T(1024)(128)(4,1)S(1)}, s32[]{:S(2)}) async-start(s8[6291456]{0:T(1024)(128)(4,1)} %bitcast.52), calls=%async_computation.3 | async-start | bytes 8388608
  113.9 2.8 %slice-start.1 = ((s8[6291456]{0:T(1024)(128)(4,1)}), s8[2097152]{0:T(1024)(128)(4,1)S(1)}, s32[]{:S(2)}) async-start(s8[6291456]{0:T(1024)(128)(4,1)} %bitcast.52), calls=%async_computation.4 | async-start | bytes 4194304
  116.7 3.4 %copy-start.10 = (bf16[2,512,1536]{2,1,0:T(8,128)(2,1)S(1)}, bf16[2,512,1536]{2,1,0:T(8,128)(2,1)}, u32[]{:S(2)}) copy-start(bf16[2,512,1536]{2,1,0:T(8,128)(2,1)} %param.20) | copy-start | bytes 9437188
  123.7 45.2 %all-to-all-start.2 = ((bf16[32,32,1536]{2,1,0:T(8,128)(2,1)}), bf16[32,32,1536]{2,1,0:T(8,128)(2,1)}, u32[]{:S(2)}, u32[]{:S(2)}) async-start(bf16[32,32,1536]{2,1,0:T(8,128)(2,1)} %bitcast.49), calls=%async_computation.2 | async-start | bytes 6291456 | tf_op jit(solution)/shard_map/all_to_all | solution.py:105
  129.6 6.4 %copy-start.11 = (bf16[2,512,1536]{2,1,0:T(8,128)(2,1)S(1)}, bf16[2,512,1536]{2,1,0:T(8,128)(2,1)}, u32[]{:S(2)}) copy-start(bf16[2,512,1536]{2,1,0:T(8,128)(2,1)} %param.20) | copy-start | bytes 9437188
  168.9 5.9 %copy-start.12 = (bf16[1536,40]{0,1:T(8,128)(2,1)S(1)}, bf16[1536,40]{0,1:T(8,128)(2,1)}, u32[]{:S(2)}) copy-start(bf16[1536,40]{0,1:T(8,128)(2,1)} %param.15) | copy-start | bytes 368644
  168.9 45.1 %all-to-all-start.1 = ((bf16[32,32,1536]{2,1,0:T(8,128)(2,1)}), bf16[32,32,1536]{2,1,0:T(8,128)(2,1)}, u32[]{:S(2)}, u32[]{:S(2)}) async-start(bf16[32,32,1536]{2,1,0:T(8,128)(2,1)} %bitcast.48), calls=%async_computation.1 | async-start | bytes 6291456 | tf_op jit(solution)/shard_map/all_to_all | solution.py:105
  182.2 34.7 %copy-start.2 = (bf16[128,1536]{1,0:T(8,128)(2,1)S(1)}, bf16[128,1536]{1,0:T(8,128)(2,1)}, u32[]{:S(2)}) copy-start(bf16[128,1536]{1,0:T(8,128)(2,1)} %copy-done.1) | copy-start | bytes 1179652
  216.9 0.7 copy-start.7
  217.4 1.1 copy-start.3

commit v9 on v7

--- a/solution.py
+++ b/solution.py
@@ -102,6 +102,7 @@
             jnp.bfloat16
         )
         computed = computed.reshape(tok_total, DEPTH, width)
+        arrived, computed = lax.optimization_barrier((arrived, computed))
         returned = lax.all_to_all(computed, "tok", split_axis=0, concat_axis=0, tiled=True)
         returned = returned.reshape(tok_total * DEPTH, width)
         combine = combine_all[:, :, local].reshape(row_count, tok_total * DEPTH)

time: 219 us -> 215 us (0.982)
  waiting for transfers between devices: 73.2 us -> 66.6 us
  local copies, waits for them, and re-layouts: 4.37 us -> 6.96 us
    ppermute x3, waiting for transfers between devices: 12.1 us -> 6.75 us  [shards(): received[shift] = lax.ppermute(block_for(shift), 'tp', pairs)]
    unnamed x32 -> x34, local copies, waits for them, and re-layouts: 1.48 us -> 3.82 us
  transfers between devices with their start and end apart: 5 -> 5, of which waited for: 4 -> 3; matrix products, arithmetic and copies ran while one was open for 12% -> 13% of each run, Pallas kernels for 0% -> 0%
where the time goes in v9:
time: 215 us; the launch traced here: 212 us
  blocking collectives  79.2 us (37%)
  waiting for transfers between devices  66.6 us (31%)
  matrix products  30 us (14%)
  starting transfers between devices  17.6 us (8%)
  other arithmetic  11.1 us (5%)
  local copies, waits for them, and re-layouts  6.96 us (3%)
    all_to_all x1, blocking collectives, shards(): lax.all_to_all(outgoing, 'tok', split_axis=0, concat_axis=0, tiled=True)  79.2 us
    all_to_all x2, waiting for transfers between devices, shards(): lax.all_to_all(computed, 'tok', split_axis=0, concat_axis=0, tiled=True)  59.9 us
    all_to_all x2, starting transfers between devices, shards(): lax.all_to_all(computed, 'tok', split_axis=0, concat_axis=0, tiled=True)  11.6 us
    dot_general x2, matrix products, shards(): hidden = jnp.dot(rows_in, w_in[local], preferred_element_type=jnp.float32)  8.85 us
    dot_general x2, matrix products, shards(): jnp.dot(activated, w_out[local], preferred_element_type=jnp.float32)  6.96 us
    ppermute x3, waiting for transfers between devices, shards(): received[shift] = lax.ppermute(block_for(shift), 'tp', pairs)  6.75 us
    ppermute x3, starting transfers between devices, shards(): received[shift] = lax.ppermute(block_for(shift), 'tp', pairs)  5.97 us
    dot_general x4, matrix products, block_for(): jnp.dot(rows, attn_weight, preferred_element_type=jnp.float32)  5.95 us
  transfers between devices with their start and end apart: 5, of which 3 were waited for; matrix products, arithmetic and copies ran while one was open for 13% of the time, Pallas kernels for 0%

profile of v9, /device:TPU:8, one launch (start us, length us, event | category | flops | bytes accessed | tf_op | source)
XLA Modules:
  0.0 212.4 jit_solution(5242146436608089018)
XLA Ops:
  0.7 1.2 copy-done
  1.9 1.3 convolution_convert_fusion.4
  3.2 4.0 %collective-permute-start.1 = (bf16[128,1536]{1,0:T(8,128)(2,1)S(1)}, bf16[128,1536]{1,0:T(8,128)(2,1)S(1)}, u32[]{:S(2)}, u32[]{:S(2)}) collective-permute-start(bf16[128,1536]{1,0:T(8,128)(2,1)S(1)} %convolution_convert_fusion.4), channel_id=1, source_target_pairs={{0,2},{1,3},{2,0},{3,1},{4,6},{5,7},{6,4},{7,5},{8,10},{9,11},{10,... | collective-permute-start | bytes 1179656 | tf_op jit(solution)/shard_map/ppermute | solution.py:61
  7.1 2.0 convolution_convert_fusion.3
  9.2 0.7 collective-permute-start.2
  9.9 1.1 convolution_convert_fusion.5
  11.0 1.3 collective-permute-start
  12.4 0.7 fusion.56
  13.5 0.6 add_compare_fusion.1
  14.7 4.0 %fusion = pred[128,2048]{1,0:T(8,128)(4,1)S(1)} fusion(s32[128,8]{1,0:T(8,128)S(1)} %copy.19), kind=kLoop, calls=%fused_computation.2 | loop fusion | flops 3932160 | bytes 266240 | tf_op jit(solution)/shard_map/reduce_or | solution.py:85
  18.7 6.7 %collective-permute-done.2 = bf16[128,1536]{1,0:T(8,128)(2,1)S(1)} collective-permute-done((bf16[128,1536]{1,0:T(8,128)(2,1)}, bf16[128,1536]{1,0:T(8,128)(2,1)S(1)}, u32[]{:S(2)}, u32[]{:S(2)}) %collective-permute-start.2) | collective-permute-done | bytes 393248 | tf_op jit(solution)/shard_map/ppermute | solution.py:61
  25.5 1.5 fusion.21
  27.0 1.9 convolution_convert_fusion
  29.0 79.2 %all_to_all.15 = bf16[32,64,1536]{2,1,0:T(8,128)(2,1)S(1)} all-to-all(bf16[32,64,1536]{2,1,0:T(8,128)(2,1)S(1)} %bitcast.43), channel_id=1, replica_groups=mesh['tok'=32,'tp'=4] {'tok'}, dimensions={0} | all-to-all | bytes 12582912 | tf_op jit(solution)/shard_map/all_to_all | solution.py:90
  108.1 0.3 slice.65
  108.4 2.3 %copy-done.1 = bf16[32,64,1536]{2,1,0:T(8,128)(2,1)} copy-done((bf16[32,64,1536]{2,1,0:T(8,128)(2,1)}, bf16[32,64,1536]{2,1,0:T(8,128)(2,1)S(1)}, u32[]{:S(2)}) %copy-start.1) | copy-done | bytes 6291480
  110.8 3.4 %fusion.3 = f32[1024,1024]{1,0:T(8,128)S(1)} fusion(bf16[1024,1536]{1,0:T(8,128)(2,1)S(1)} %bitcast.50, bf16[2,1536,1024]{2,1,0:T(8,128)(2,1)S(1)} %bitcast.52), kind=kOutput, calls=%fused_computation.8 | convolution fusion | flops 3221225472 | bytes 10485760 | tf_op jit(solution)/shard_map/dot_general | solution.py:97
  114.2 3.5 %convolution_convert_fusion.2 = bf16[1024,1536]{1,0:T(8,128)(2,1)} fusion(bf16[2,512,1536]{2,1,0:T(8,128)(2,1)S(1)} %copy-done.11, f32[1024,1024]{1,0:T(8,128)S(1)} %fusion.3), kind=kOutput, calls=%fused_computation.5 | convolution fusion | flops 1615331328 | bytes 8912896 | tf_op jit(solution)/shard_map/dot_general | solution.py:101
  117.7 5.9 %all-to-all-start.1 = ((bf16[32,32,1536]{2,1,0:T(8,128)(2,1)}), bf16[32,32,1536]{2,1,0:T(8,128)(2,1)}, u32[]{:S(2)}, u32[]{:S(2)}) async-start(bf16[32,32,1536]{2,1,0:T(8,128)(2,1)} %bitcast.48), calls=%async_computation.1 | async-start | bytes 6291456 | tf_op jit(solution)/shard_map/all_to_all | solution.py:106
  123.6 2.2 %slice.57 = bf16[32,1,32,1536]{3,2,1,0:T(8,128)(2,1)S(1)} slice(bf16[32,2,32,1536]{3,2,1,0:T(8,128)(2,1)} %bitcast.45), slice={[0:32], [1:2], [0:32], [0:1536]} | slice | bytes 6291456 | tf_op jit(solution)/shard_map/slice | solution.py:96
  125.8 5.4 %fusion.1 = f32[1024,1024]{1,0:T(8,128)S(1)} fusion(bf16[1024,1536]{1,0:T(8,128)(2,1)S(1)} %bitcast.49, bf16[2,1536,1024]{2,1,0:T(8,128)(2,1)} %param.19), kind=kOutput, calls=%fused_computation.6 | convolution fusion | flops 3221225472 | bytes 10485760 | tf_op jit(solution)/shard_map/dot_general | solution.py:97
  131.3 3.5 %convolution_convert_fusion.1 = bf16[1024,1536]{1,0:T(8,128)(2,1)} fusion(bf16[2,512,1536]{2,1,0:T(8,128)(2,1)S(1)} %copy-done.12, f32[1024,1024]{1,0:T(8,128)S(1)} %fusion.1), kind=kOutput, calls=%fused_computation.4 | convolution fusion | flops 1615331328 | bytes 8912896 | tf_op jit(solution)/shard_map/dot_general | solution.py:101
  134.8 28.1 %all-to-all-done.1 = bf16[32,32,1536]{2,1,0:T(8,128)(2,1)} async-done(((bf16[32,32,1536]{2,1,0:T(8,128)(2,1)}), bf16[32,32,1536]{2,1,0:T(8,128)(2,1)}, u32[]{:S(2)}, u32[]{:S(2)}) %all-to-all-start.1) | async-done | bytes 3145760 | tf_op jit(solution)/shard_map/all_to_all | solution.py:106
  162.9 5.7 %all-to-all-start.2 = ((bf16[32,32,1536]{2,1,0:T(8,128)(2,1)}), bf16[32,32,1536]{2,1,0:T(8,128)(2,1)}, u32[]{:S(2)}, u32[]{:S(2)}) async-start(bf16[32,32,1536]{2,1,0:T(8,128)(2,1)} %bitcast.47), calls=%async_computation.2 | async-start | bytes 6291456 | tf_op jit(solution)/shard_map/all_to_all | solution.py:106
  169.1 2.8 %select_reduce_fusion = f32[128,2048]{1,0:T(8,128)S(1)} fusion(f32[128,8]{1,0:T(8,128)S(1)} %copy.20, s32[128,8]{1,0:T(8,128)S(1)} %copy.19), kind=kLoop, calls=%fused_computation | loop fusion | flops 6029312 | bytes 1056768 | tf_op jit(solution)/shard_map/reduce_sum | solution.py:92
  171.9 0.3 copy.21
  172.4 0.8 fusion.34
  173.2 2.9 %fusion.26 = f32[256,1536]{1,0:T(8,128)S(1)} fusion(bf16[1024,1536]{1,0:T(8,128)(2,1)} %bitcast.8, bf16[128,1024]{0,1:T(8,128)(2,1)S(1)} %get-tuple-element.12, bf16[128,1024]{0,1:T(8,128)(2,1)S(1)} %get-tuple-element.13), kind=kOutput, calls=%fused_computation.44 | convolution fusion | flops 806354944 | bytes 5242880 | tf_op jit(solution)/shard_map/dot_general | solution.py:111
  176.1 31.7 %all-to-all-done.2 = bf16[32,32,1536]{2,1,0:T(8,128)(2,1)} async-done(((bf16[32,32,1536]{2,1,0:T(8,128)(2,1)}), bf16[32,32,1536]{2,1,0:T(8,128)(2,1)}, u32[]{:S(2)}, u32[]{:S(2)}) %all-to-all-start.2) | async-done | bytes 3145760 | tf_op jit(solution)/shard_map/all_to_all | solution.py:106
  207.8 3.0 %fusion.30 = f32[256,1536]{1,0:T(8,128)S(1)} fusion(bf16[1024,1536]{1,0:T(8,128)(2,1)} %bitcast.14, bf16[128,1024]{0,1:T(8,128)(2,1)S(1)} %get-tuple-element.14, bf16[128,1024]{0,1:T(8,128)(2,1)} %get-tuple-element.15), kind=kOutput, calls=%fused_computation.48 | convolution fusion | flops 806354944 | bytes 5242880 | tf_op jit(solution)/shard_map/dot_general | solution.py:111
  210.8 0.5 fusion.18
  211.5 0.9 fusion.20
  (55 shorter events, 2.0 us)
Async XLA Ops:
  0.6 1.3 copy-start
  0.6 9.2 %copy-start.5 = (bf16[512,384]{1,0:T(8,128)(2,1)S(1)}, bf16[512,384]{1,0:T(8,128)(2,1)}, u32[]{:S(2)}) copy-start(bf16[512,384]{1,0:T(8,128)(2,1)} %param.11) | copy-start | bytes 1179652
  0.7 11.6 %copy-start.10 = (s32[64]{0:T(128)S(1)}, s32[64]{0:T(128)}, u32[]{:S(2)}) copy-start(s32[64]{0:T(128)} %param.18) | copy-start | bytes 772
  0.7 11.8 %copy-start.14 = (s32[32]{0:T(128)S(1)}, s32[32]{0:T(128)}, u32[]{:S(2)}) copy-start(s32[32]{0:T(128)} %param.17) | copy-start | bytes 388
  0.7 12.6 %copy-start.7 = (s32[128,8]{0,1:T(8,128)S(1)}, s32[128,8]{0,1:T(8,128)}, u32[]{:S(2)}) copy-start(s32[128,8]{0,1:T(8,128)} %param.16) | copy-start | bytes 12292
  0.7 24.8 %copy-start.6 = (bf16[128,1536]{1,0:T(8,128)(2,1)S(1)}, bf16[128,1536]{1,0:T(8,128)(2,1)}, u32[]{:S(2)}) copy-start(bf16[128,1536]{1,0:T(8,128)(2,1)} %param.13) | copy-start | bytes 1179652
  3.2 15.5 %collective-permute-start.1 = (bf16[128,1536]{1,0:T(8,128)(2,1)S(1)}, bf16[128,1536]{1,0:T(8,128)(2,1)S(1)}, u32[]{:S(2)}, u32[]{:S(2)}) collective-permute-start(bf16[128,1536]{1,0:T(8,128)(2,1)S(1)} %convolution_convert_fusion.4), channel_id=1, source_target_pairs={{0,2},{1,3},{2,0},{3,1},{4,6},{5,7},{6,4},{7,5},{8,10},{9,11},{10,... | collective-permute-start | bytes 1179656 | tf_op jit(solution)/shard_map/ppermute | solution.py:61
  9.1 17.9 %copy-start.8 = (f32[1536]{0:T(1024)S(1)}, f32[1536]{0:T(1024)}, u32[]{:S(2)}) copy-start(f32[1536]{0:T(1024)} %param.14) | copy-start | bytes 18436
  9.2 16.3 %collective-permute-start.2 = (bf16[128,1536]{1,0:T(8,128)(2,1)}, bf16[128,1536]{1,0:T(8,128)(2,1)S(1)}, u32[]{:S(2)}, u32[]{:S(2)}) collective-permute-start(bf16[128,1536]{1,0:T(8,128)(2,1)} %convolution_convert_fusion.3), channel_id=1, source_target_pairs={{0,3},{1,0},{2,1},{3,2},{4,7},{5,4},{6,5},{7,6},{8,11},{9,8},{10,9... | collective-permute-start | bytes 1179656 | tf_op jit(solution)/shard_map/ppermute | solution.py:61
  11.0 14.5 %collective-permute-start = (bf16[128,1536]{1,0:T(8,128)(2,1)}, bf16[128,1536]{1,0:T(8,128)(2,1)}, u32[]{:S(2)}, u32[]{:S(2)}) collective-permute-start(bf16[128,1536]{1,0:T(8,128)(2,1)} %convolution_convert_fusion.5), channel_id=1, source_target_pairs={{0,1},{1,2},{2,3},{3,0},{4,5},{5,6},{6,7},{7,4},{8,9},{9,10},{10,1... | collective-permute-start | bytes 1179656 | tf_op jit(solution)/shard_map/ppermute | solution.py:61
  27.0 141.6 %copy-start.2 = (bf16[128,1536]{1,0:T(8,128)(2,1)}, bf16[128,1536]{1,0:T(8,128)(2,1)S(1)}, u32[]{:S(2)}) copy-start(bf16[128,1536]{1,0:T(8,128)(2,1)S(1)} %get-tuple-element.19) | copy-start | bytes 1179652
  27.0 83.7 %slice-start = ((s8[6291456]{0:T(1024)(128)(4,1)}), s8[4194304]{0:T(1024)(128)(4,1)S(1)}, s32[]{:S(2)}) async-start(s8[6291456]{0:T(1024)(128)(4,1)} %bitcast.51), calls=%async_computation.3 | async-start | bytes 8388608
  28.9 81.8 %slice-start.1 = ((s8[6291456]{0:T(1024)(128)(4,1)}), s8[2097152]{0:T(1024)(128)(4,1)S(1)}, s32[]{:S(2)}) async-start(s8[6291456]{0:T(1024)(128)(4,1)} %bitcast.51), calls=%async_computation.4 | async-start | bytes 4194304
  108.1 2.7 %copy-start.1 = (bf16[32,64,1536]{2,1,0:T(8,128)(2,1)}, bf16[32,64,1536]{2,1,0:T(8,128)(2,1)S(1)}, u32[]{:S(2)}) copy-start(bf16[32,64,1536]{2,1,0:T(8,128)(2,1)S(1)} %all_to_all.15) | copy-start | bytes 18874372
  110.8 3.4 %copy-start.11 = (bf16[2,512,1536]{2,1,0:T(8,128)(2,1)S(1)}, bf16[2,512,1536]{2,1,0:T(8,128)(2,1)}, u32[]{:S(2)}) copy-start(bf16[2,512,1536]{2,1,0:T(8,128)(2,1)} %param.20) | copy-start | bytes 9437188
  117.7 45.2 %all-to-all-start.1 = ((bf16[32,32,1536]{2,1,0:T(8,128)(2,1)}), bf16[32,32,1536]{2,1,0:T(8,128)(2,1)}, u32[]{:S(2)}, u32[]{:S(2)}) async-start(bf16[32,32,1536]{2,1,0:T(8,128)(2,1)} %bitcast.48), calls=%async_computation.1 | async-start | bytes 6291456 | tf_op jit(solution)/shard_map/all_to_all | solution.py:106
  125.8 5.5 %copy-start.12 = (bf16[2,512,1536]{2,1,0:T(8,128)(2,1)S(1)}, bf16[2,512,1536]{2,1,0:T(8,128)(2,1)}, u32[]{:S(2)}) copy-start(bf16[2,512,1536]{2,1,0:T(8,128)(2,1)} %param.20) | copy-start | bytes 9437188
  134.8 33.8 %copy-start.13 = (bf16[1536,40]{0,1:T(8,128)(2,1)S(1)}, bf16[1536,40]{0,1:T(8,128)(2,1)}, u32[]{:S(2)}) copy-start(bf16[1536,40]{0,1:T(8,128)(2,1)} %param.15) | copy-start | bytes 368644
  162.9 44.9 %all-to-all-start.2 = ((bf16[32,32,1536]{2,1,0:T(8,128)(2,1)}), bf16[32,32,1536]{2,1,0:T(8,128)(2,1)}, u32[]{:S(2)}, u32[]{:S(2)}) async-start(bf16[32,32,1536]{2,1,0:T(8,128)(2,1)} %bitcast.47), calls=%async_computation.2 | async-start | bytes 6291456 | tf_op jit(solution)/shard_map/all_to_all | solution.py:106
  176.1 34.7 %copy-start.3 = (bf16[128,1536]{1,0:T(8,128)(2,1)S(1)}, bf16[128,1536]{1,0:T(8,128)(2,1)}, u32[]{:S(2)}) copy-start(bf16[128,1536]{1,0:T(8,128)(2,1)} %copy-done.2) | copy-start | bytes 1179652
  210.8 0.7 copy-start.9
  211.3 1.1 copy-start.4

commit v10 on v9

--- a/solution.py
+++ b/solution.py
@@ -106,12 +106,9 @@
         returned = lax.all_to_all(computed, "tok", split_axis=0, concat_axis=0, tiled=True)
         returned = returned.reshape(tok_total * DEPTH, width)
         combine = combine_all[:, :, local].reshape(row_count, tok_total * DEPTH)
-        combine_hi = combine.astype(jnp.bfloat16)
-        combine_lo = (combine - combine_hi.astype(jnp.float32)).astype(jnp.bfloat16)
-        both = jnp.dot(
-            jnp.concatenate([combine_hi, combine_lo]), returned, preferred_element_type=jnp.float32
+        expert_sum = expert_sum + jnp.dot(
+            combine.astype(jnp.bfloat16), returned, preferred_element_type=jnp.float32
         )
-        expert_sum = expert_sum + (both[:row_count] + both[row_count:])
     stream_out = (stream.astype(jnp.float32) + expert_sum).astype(jnp.bfloat16)
     next_normed = rms_norm(stream_out, gain_next)
     return (stream_out, next_normed)

time: 215 us -> 214 us (level)
  no operation moved by 1% of the time
where the time goes in v10:
time: 214 us; the launch traced here: 211 us
  blocking collectives  79.2 us (37%)
  waiting for transfers between devices  68 us (32%)
  matrix products  29.2 us (14%)
  starting transfers between devices  17.6 us (8%)
  other arithmetic  9.9 us (5%)
  local copies, waits for them, and re-layouts  6.65 us (3%)
    all_to_all x1, blocking collectives, shards(): lax.all_to_all(outgoing, 'tok', split_axis=0, concat_axis=0, tiled=True)  79.2 us
    all_to_all x2, waiting for transfers between devices, shards(): lax.all_to_all(computed, 'tok', split_axis=0, concat_axis=0, tiled=True)  61.2 us
    all_to_all x2, starting transfers between devices, shards(): lax.all_to_all(computed, 'tok', split_axis=0, concat_axis=0, tiled=True)  11.6 us
    dot_general x2, matrix products, shards(): hidden = jnp.dot(rows_in, w_in[local], preferred_element_type=jnp.float32)  8.86 us
    dot_general x2, matrix products, shards(): jnp.dot(activated, w_out[local], preferred_element_type=jnp.float32)  6.97 us
    ppermute x3, waiting for transfers between devices, shards(): received[shift] = lax.ppermute(block_for(shift), 'tp', pairs)  6.75 us
    ppermute x3, starting transfers between devices, shards(): received[shift] = lax.ppermute(block_for(shift), 'tp', pairs)  5.97 us
    dot_general x4, matrix products, block_for(): jnp.dot(rows, attn_weight, preferred_element_type=jnp.float32)  5.95 us
  transfers between devices with their start and end apart: 5, of which 3 were waited for; matrix products, arithmetic and copies ran while one was open for 13% of the time, Pallas kernels for 0%

profile of v10, /device:TPU:8, one launch (start us, length us, event | category | flops | bytes accessed | tf_op | source)
XLA Modules:
  0.0 211.5 jit_solution(924431593101374960)
XLA Ops:
  0.7 1.2 copy-done
  1.9 1.3 convolution_convert_fusion.4
  3.2 4.0 %collective-permute-start.1 = (bf16[128,1536]{1,0:T(8,128)(2,1)S(1)}, bf16[128,1536]{1,0:T(8,128)(2,1)S(1)}, u32[]{:S(2)}, u32[]{:S(2)}) collective-permute-start(bf16[128,1536]{1,0:T(8,128)(2,1)S(1)} %convolution_convert_fusion.4), channel_id=1, source_target_pairs={{0,2},{1,3},{2,0},{3,1},{4,6},{5,7},{6,4},{7,5},{8,10},{9,11},{10,... | collective-permute-start | bytes 1179656 | tf_op jit(solution)/shard_map/ppermute | solution.py:61
  7.1 2.0 convolution_convert_fusion.3
  9.2 0.7 collective-permute-start.2
  9.9 1.1 convolution_convert_fusion.5
  11.0 1.3 collective-permute-start
  12.4 0.7 fusion.46
  13.3 0.2 reduce_window_sum.11
  13.5 0.6 add_compare_fusion.1
  14.7 4.0 %fusion = pred[128,2048]{1,0:T(8,128)(4,1)S(1)} fusion(s32[128,8]{1,0:T(8,128)S(1)} %copy.19), kind=kLoop, calls=%fused_computation.2 | loop fusion | flops 3932160 | bytes 266240 | tf_op jit(solution)/shard_map/reduce_or | solution.py:85
  18.7 6.7 %collective-permute-done.2 = bf16[128,1536]{1,0:T(8,128)(2,1)S(1)} collective-permute-done((bf16[128,1536]{1,0:T(8,128)(2,1)}, bf16[128,1536]{1,0:T(8,128)(2,1)S(1)}, u32[]{:S(2)}, u32[]{:S(2)}) %collective-permute-start.2) | collective-permute-done | bytes 393248 | tf_op jit(solution)/shard_map/ppermute | solution.py:61
  25.5 1.5 fusion.23
  27.0 1.9 convolution_convert_fusion
  28.9 79.2 %all_to_all.15 = bf16[32,64,1536]{2,1,0:T(8,128)(2,1)S(1)} all-to-all(bf16[32,64,1536]{2,1,0:T(8,128)(2,1)S(1)} %bitcast.35), channel_id=1, replica_groups=mesh['tok'=32,'tp'=4] {'tok'}, dimensions={0} | all-to-all | bytes 12582912 | tf_op jit(solution)/shard_map/all_to_all | solution.py:90
  108.1 0.3 slice.51
  108.4 2.3 %copy-done.1 = bf16[32,64,1536]{2,1,0:T(8,128)(2,1)} copy-done((bf16[32,64,1536]{2,1,0:T(8,128)(2,1)}, bf16[32,64,1536]{2,1,0:T(8,128)(2,1)S(1)}, u32[]{:S(2)}) %copy-start.1) | copy-done | bytes 6291480
  110.8 3.4 %fusion.3 = f32[1024,1024]{1,0:T(8,128)S(1)} fusion(bf16[1024,1536]{1,0:T(8,128)(2,1)S(1)} %bitcast.41, bf16[2,1536,1024]{2,1,0:T(8,128)(2,1)S(1)} %bitcast.46), kind=kOutput, calls=%fused_computation.8 | convolution fusion | flops 3221225472 | bytes 10485760 | tf_op jit(solution)/shard_map/dot_general | solution.py:97
  114.2 3.5 %convolution_convert_fusion.2 = bf16[1024,1536]{1,0:T(8,128)(2,1)} fusion(bf16[2,512,1536]{2,1,0:T(8,128)(2,1)S(1)} %copy-done.9, f32[1024,1024]{1,0:T(8,128)S(1)} %fusion.3), kind=kOutput, calls=%fused_computation.5 | convolution fusion | flops 1615331328 | bytes 8912896 | tf_op jit(solution)/shard_map/dot_general | solution.py:101
  117.7 5.9 %all-to-all-start.1 = ((bf16[32,32,1536]{2,1,0:T(8,128)(2,1)}), bf16[32,32,1536]{2,1,0:T(8,128)(2,1)}, u32[]{:S(2)}, u32[]{:S(2)}) async-start(bf16[32,32,1536]{2,1,0:T(8,128)(2,1)} %bitcast.39), calls=%async_computation.1 | async-start | bytes 6291456 | tf_op jit(solution)/shard_map/all_to_all | solution.py:106
  123.6 2.2 %slice.45 = bf16[32,1,32,1536]{3,2,1,0:T(8,128)(2,1)S(1)} slice(bf16[32,2,32,1536]{3,2,1,0:T(8,128)(2,1)} %bitcast.37), slice={[0:32], [1:2], [0:32], [0:1536]} | slice | bytes 6291456 | tf_op jit(solution)/shard_map/slice | solution.py:96
  125.8 5.4 %fusion.1 = f32[1024,1024]{1,0:T(8,128)S(1)} fusion(bf16[1024,1536]{1,0:T(8,128)(2,1)S(1)} %bitcast.40, bf16[2,1536,1024]{2,1,0:T(8,128)(2,1)} %param.19), kind=kOutput, calls=%fused_computation.6 | convolution fusion | flops 3221225472 | bytes 10485760 | tf_op jit(solution)/shard_map/dot_general | solution.py:97
  131.3 3.5 %convolution_convert_fusion.1 = bf16[1024,1536]{1,0:T(8,128)(2,1)} fusion(bf16[2,512,1536]{2,1,0:T(8,128)(2,1)S(1)} %copy-done.10, f32[1024,1024]{1,0:T(8,128)S(1)} %fusion.1), kind=kOutput, calls=%fused_computation.4 | convolution fusion | flops 1615331328 | bytes 8912896 | tf_op jit(solution)/shard_map/dot_general | solution.py:101
  134.8 28.1 %all-to-all-done.1 = bf16[32,32,1536]{2,1,0:T(8,128)(2,1)} async-done(((bf16[32,32,1536]{2,1,0:T(8,128)(2,1)}), bf16[32,32,1536]{2,1,0:T(8,128)(2,1)}, u32[]{:S(2)}, u32[]{:S(2)}) %all-to-all-start.1) | async-done | bytes 3145760 | tf_op jit(solution)/shard_map/all_to_all | solution.py:106
  162.9 5.7 %all-to-all-start.2 = ((bf16[32,32,1536]{2,1,0:T(8,128)(2,1)}), bf16[32,32,1536]{2,1,0:T(8,128)(2,1)}, u32[]{:S(2)}, u32[]{:S(2)}) async-start(bf16[32,32,1536]{2,1,0:T(8,128)(2,1)} %bitcast.38), calls=%async_computation.2 | async-start | bytes 6291456 | tf_op jit(solution)/shard_map/all_to_all | solution.py:106
  168.6 0.3 fusion.28
  169.1 2.8 %select_reduce_fusion = bf16[128,2048]{1,0:T(8,128)(2,1)S(1)} fusion(f32[128,8]{1,0:T(8,128)S(1)} %copy.20, s32[128,8]{1,0:T(8,128)S(1)} %copy.19), kind=kLoop, calls=%fused_computation | loop fusion | flops 6029312 | bytes 532480 | tf_op jit(solution)/shard_map/reduce_sum | solution.py:92
  171.9 0.3 copy.21
  172.2 2.5 %fusion.50 = f32[128,1536]{1,0:T(8,128)S(1)} fusion(bf16[128,1024]{0,1:T(8,128)(2,1)S(1)} %bitcast.44, bf16[1024,1536]{1,0:T(8,128)(2,1)} %bitcast.8), kind=kOutput, calls=%fused_computation.80 | convolution fusion | flops 402653184 | bytes 4194304 | tf_op jit(solution)/shard_map/dot_general | solution.py:109
  174.8 33.1 %all-to-all-done.2 = bf16[32,32,1536]{2,1,0:T(8,128)(2,1)} async-done(((bf16[32,32,1536]{2,1,0:T(8,128)(2,1)}), bf16[32,32,1536]{2,1,0:T(8,128)(2,1)}, u32[]{:S(2)}, u32[]{:S(2)}) %all-to-all-start.2) | async-done | bytes 3145760 | tf_op jit(solution)/shard_map/all_to_all | solution.py:106
  207.9 2.6 %fusion.20 = (f32[128]{0:T(128)S(1)}, bf16[128,1536]{1,0:T(8,128)(2,1)S(1)}) fusion(f32[128,1536]{1,0:T(8,128)S(1)} %fusion.50, bf16[128,1024]{0,1:T(8,128)(2,1)S(1)} %bitcast.43, bf16[1024,1536]{1,0:T(8,128)(2,1)} %bitcast.14, bf16[128,1536]{1,0:T(8,128)(2,1)S(1)} %get-tuple-element.13), kind=kOutput, calls=%fused_computation.35 | convolution fusion | flops 404029312 | bytes 4981248 | tf_op jit(solution)/shard_map/dot_general | solution.py:109
  210.5 0.9 fusion.22
  (48 shorter events, 1.1 us)
Async XLA Ops:
  0.6 1.3 copy-start
  0.6 9.2 %copy-start.3 = (bf16[512,384]{1,0:T(8,128)(2,1)S(1)}, bf16[512,384]{1,0:T(8,128)(2,1)}, u32[]{:S(2)}) copy-start(bf16[512,384]{1,0:T(8,128)(2,1)} %param.11) | copy-start | bytes 1179652
  0.7 11.6 %copy-start.8 = (s32[64]{0:T(128)S(1)}, s32[64]{0:T(128)}, u32[]{:S(2)}) copy-start(s32[64]{0:T(128)} %param.18) | copy-start | bytes 772
  0.7 11.8 %copy-start.12 = (s32[32]{0:T(128)S(1)}, s32[32]{0:T(128)}, u32[]{:S(2)}) copy-start(s32[32]{0:T(128)} %param.17) | copy-start | bytes 388
  0.7 12.6 %copy-start.5 = (s32[128,8]{0,1:T(8,128)S(1)}, s32[128,8]{0,1:T(8,128)}, u32[]{:S(2)}) copy-start(s32[128,8]{0,1:T(8,128)} %param.16) | copy-start | bytes 12292
  0.7 24.8 %copy-start.4 = (bf16[128,1536]{1,0:T(8,128)(2,1)S(1)}, bf16[128,1536]{1,0:T(8,128)(2,1)}, u32[]{:S(2)}) copy-start(bf16[128,1536]{1,0:T(8,128)(2,1)} %param.13) | copy-start | bytes 1179652
  3.2 15.5 %collective-permute-start.1 = (bf16[128,1536]{1,0:T(8,128)(2,1)S(1)}, bf16[128,1536]{1,0:T(8,128)(2,1)S(1)}, u32[]{:S(2)}, u32[]{:S(2)}) collective-permute-start(bf16[128,1536]{1,0:T(8,128)(2,1)S(1)} %convolution_convert_fusion.4), channel_id=1, source_target_pairs={{0,2},{1,3},{2,0},{3,1},{4,6},{5,7},{6,4},{7,5},{8,10},{9,11},{10,... | collective-permute-start | bytes 1179656 | tf_op jit(solution)/shard_map/ppermute | solution.py:61
  9.1 17.9 %copy-start.6 = (f32[1536]{0:T(1024)S(1)}, f32[1536]{0:T(1024)}, u32[]{:S(2)}) copy-start(f32[1536]{0:T(1024)} %param.14) | copy-start | bytes 18436
  9.2 16.3 %collective-permute-start.2 = (bf16[128,1536]{1,0:T(8,128)(2,1)}, bf16[128,1536]{1,0:T(8,128)(2,1)S(1)}, u32[]{:S(2)}, u32[]{:S(2)}) collective-permute-start(bf16[128,1536]{1,0:T(8,128)(2,1)} %convolution_convert_fusion.3), channel_id=1, source_target_pairs={{0,3},{1,0},{2,1},{3,2},{4,7},{5,4},{6,5},{7,6},{8,11},{9,8},{10,9... | collective-permute-start | bytes 1179656 | tf_op jit(solution)/shard_map/ppermute | solution.py:61
  11.0 14.5 %collective-permute-start = (bf16[128,1536]{1,0:T(8,128)(2,1)}, bf16[128,1536]{1,0:T(8,128)(2,1)}, u32[]{:S(2)}, u32[]{:S(2)}) collective-permute-start(bf16[128,1536]{1,0:T(8,128)(2,1)} %convolution_convert_fusion.5), channel_id=1, source_target_pairs={{0,1},{1,2},{2,3},{3,0},{4,5},{5,6},{6,7},{7,4},{8,9},{9,10},{10,1... | collective-permute-start | bytes 1179656 | tf_op jit(solution)/shard_map/ppermute | solution.py:61
  27.0 83.7 %slice-start = ((s8[6291456]{0:T(1024)(128)(4,1)}), s8[4194304]{0:T(1024)(128)(4,1)S(1)}, s32[]{:S(2)}) async-start(s8[6291456]{0:T(1024)(128)(4,1)} %bitcast.45), calls=%async_computation.3 | async-start | bytes 8388608
  28.9 81.8 %slice-start.1 = ((s8[6291456]{0:T(1024)(128)(4,1)}), s8[2097152]{0:T(1024)(128)(4,1)S(1)}, s32[]{:S(2)}) async-start(s8[6291456]{0:T(1024)(128)(4,1)} %bitcast.45), calls=%async_computation.4 | async-start | bytes 4194304
  108.1 2.7 %copy-start.1 = (bf16[32,64,1536]{2,1,0:T(8,128)(2,1)}, bf16[32,64,1536]{2,1,0:T(8,128)(2,1)S(1)}, u32[]{:S(2)}) copy-start(bf16[32,64,1536]{2,1,0:T(8,128)(2,1)S(1)} %all_to_all.15) | copy-start | bytes 18874372
  110.8 3.4 %copy-start.9 = (bf16[2,512,1536]{2,1,0:T(8,128)(2,1)S(1)}, bf16[2,512,1536]{2,1,0:T(8,128)(2,1)}, u32[]{:S(2)}) copy-start(bf16[2,512,1536]{2,1,0:T(8,128)(2,1)} %param.20) | copy-start | bytes 9437188
  117.7 45.2 %all-to-all-start.1 = ((bf16[32,32,1536]{2,1,0:T(8,128)(2,1)}), bf16[32,32,1536]{2,1,0:T(8,128)(2,1)}, u32[]{:S(2)}, u32[]{:S(2)}) async-start(bf16[32,32,1536]{2,1,0:T(8,128)(2,1)} %bitcast.39), calls=%async_computation.1 | async-start | bytes 6291456 | tf_op jit(solution)/shard_map/all_to_all | solution.py:106
  125.8 5.5 %copy-start.10 = (bf16[2,512,1536]{2,1,0:T(8,128)(2,1)S(1)}, bf16[2,512,1536]{2,1,0:T(8,128)(2,1)}, u32[]{:S(2)}) copy-start(bf16[2,512,1536]{2,1,0:T(8,128)(2,1)} %param.20) | copy-start | bytes 9437188
  134.8 33.8 %copy-start.11 = (bf16[1536,40]{0,1:T(8,128)(2,1)S(1)}, bf16[1536,40]{0,1:T(8,128)(2,1)}, u32[]{:S(2)}) copy-start(bf16[1536,40]{0,1:T(8,128)(2,1)} %param.15) | copy-start | bytes 368644
  162.9 45.0 %all-to-all-start.2 = ((bf16[32,32,1536]{2,1,0:T(8,128)(2,1)}), bf16[32,32,1536]{2,1,0:T(8,128)(2,1)}, u32[]{:S(2)}, u32[]{:S(2)}) async-start(bf16[32,32,1536]{2,1,0:T(8,128)(2,1)} %bitcast.38), calls=%async_computation.2 | async-start | bytes 6291456 | tf_op jit(solution)/shard_map/all_to_all | solution.py:106
  174.7 35.8 %copy-start.7 = (f32[1536]{0:T(1024)S(1)}, f32[1536]{0:T(1024)}, u32[]{:S(2)}) copy-start(f32[1536]{0:T(1024)} %param.21) | copy-start | bytes 18436
  210.5 0.9 copy-start.2
